TPU v7x, 256 devices: a whole 4x4x8 slice. The times are simulated.
256 devices in a mesh: rep: 8 (over y_hi, x), ep: 32 (over z, y_lo, core).
Axes of the slice: x: 4, y: 4 (y_hi: 2, y_lo: 2; y = y_hi * 2 + y_lo), z: 8, core: 2. Of those that a mesh axis runs over, the one named last changes fastest.
Arguments:
- queries: bfloat16 [8, 128, 36864], P('rep', None, 'ep'), may hold values from -64 to 64
- suffix_latent: bfloat16 [8, 73728], P('rep', 'ep'), may hold values from -4 to 4
- cache_pool: bfloat16 [8, 256, 36864], P('rep', 'ep'), may hold values from -4 to 4
- holders: int32 [8, 64], replicated, may hold values from 0 to 7, as said below
- block_slots: int32 [8, 64], replicated, may hold values from 0 to 7, as said below
- prefix_len: int32 [8], P('rep'), may hold values from 1024 to 4096, as said below
- hidden: bfloat16 [8, 128, 7168], P('rep', 'ep'), may hold values from -16 to 16
- w_value: bfloat16 [64, 512, 128], P('ep'), may hold values from -0.25 to 0.25
- w_out: bfloat16 [8192, 7168], P('ep'), may hold values from -0.0625 to 0.0625
- norm_gain: bfloat16 [7168], replicated, may hold values from 0.099609375 to 1.8984375
- experts: int32 [8, 128, 8], P('rep', 'ep'), may hold values from 0 to 31, all different within a row; in each aligned block of 4 rows (0 to 3, 4 to 7, ..., all dimensions but the last counted through in order) at most 2 rows name the same one
- gate_weights: bfloat16 [8, 128, 8], P('rep', 'ep'), may hold values from 0.029907227 to 0.29882812
- w_gate: bfloat16 [32, 7168, 1024], P('ep', None, 'rep'), may hold values from -0.0625 to 0.0625
- w_up: bfloat16 [32, 7168, 1024], P('ep', None, 'rep'), may hold values from -0.0625 to 0.0625
- w_down: bfloat16 [32, 1024, 7168], P('ep', 'rep'), may hold values from -0.1875 to 0.1875
Outputs:
- layer_out: float32 [8, 128, 7168], P('rep', 'ep')
Inputs may be any that keep to these rules, and one draw needn't show every extreme that they name: `holders`: for each group and each index s of ep, the blocks s * 2 to (s + 1) * 2 - 1 of its prefix come from holder groups none of which gives more than 1 of them. `block_slots`: block b of a prefix lies on index b // 2 of ep of its holder group. `prefix_len`: some group's prefix has 4096 tokens. Each row names 8 different experts; among the rows of one device no expert is named more than 2 times.
All inputs are finite; a program needn't handle non-finite values.
Results may differ from a plain program's by a relative error of at most 0.004.
Values may be sent and summed in bfloat16 or wider, within the bound.
No kernel may reach another device: no remote copies, remote signals or barrier semaphores. Data moves between devices by JAX's collectives and lax.ppermute only.
A program may use at most 128 MiB of HBM per device.

v0:
```python
import jax
import jax.numpy as jnp
from jax import lax
from jax.sharding import PartitionSpec as P

KVR = 512
ROPE = 64
SUF = 128


score_scale = 0.07216878364870323
norm_eps = 1e-06


def expert_units(token_rows, gate_rows, up_rows):
    gate_part = jnp.dot(token_rows, gate_rows, preferred_element_type=jnp.float32)
    up_part = jnp.dot(token_rows, up_rows, preferred_element_type=jnp.float32)
    return (jax.nn.silu(gate_part) * up_part).astype(jnp.bfloat16)


def local(
    queries,
    suffix_latent,
    cache_pool,
    holders,
    block_slots,
    prefix_len,
    hidden,
    w_value,
    w_out,
    norm_gain,
    experts,
    gate_weights,
    w_gate,
    w_up,
    w_down,
):
    rep_count = lax.axis_size("rep")
    ep_count = lax.axis_size("ep")
    rep_index = lax.axis_index("rep")
    ep_index = lax.axis_index("ep")
    pool_count = cache_pool.shape[1]
    block_width = cache_pool.shape[2]
    per_device = holders.shape[1] // ep_count
    per_holder = (per_device + rep_count - 1) // rep_count
    latent_width = KVR + ROPE
    mine_holders = lax.dynamic_slice_in_dim(holders, ep_index * per_device, per_device, 1)
    mine_slots = lax.dynamic_slice_in_dim(block_slots, ep_index * per_device, per_device, 1)
    position = jnp.arange(per_device, dtype=jnp.int32)
    same_holder = mine_holders[:, :, None] == mine_holders[:, None, :]
    earlier = position[None, :] < position[:, None]
    occurrence = jnp.sum((same_holder & earlier[None, :, :]).astype(jnp.int32), axis=2)
    wanted = mine_holders == rep_index
    chosen_slot = occurrence[:, :, None] == jnp.arange(per_holder, dtype=jnp.int32)[None, None, :]
    chosen_row = mine_slots[:, :, None] == jnp.arange(pool_count, dtype=jnp.int32)[None, None, :]
    selector = jnp.einsum(
        "son,soh->snh",
        (wanted[:, :, None] & chosen_slot).astype(jnp.float32),
        chosen_row.astype(jnp.float32),
        precision=lax.Precision.HIGHEST,
    )
    outgoing = jnp.dot(
        selector.reshape(rep_count * per_holder, pool_count).astype(jnp.bfloat16),
        cache_pool[0],
        preferred_element_type=jnp.float32,
    )
    outgoing = outgoing.astype(jnp.bfloat16).reshape(rep_count, per_holder, block_width)
    incoming = lax.all_to_all(outgoing, "rep", split_axis=0, concat_axis=0, tiled=True)
    own_holders = lax.dynamic_index_in_dim(mine_holders, rep_index, 0, keepdims=False)
    own_order = lax.dynamic_index_in_dim(occurrence, rep_index, 0, keepdims=False)
    source = own_holders * per_holder + own_order
    picker = (
        source[:, None] == jnp.arange(rep_count * per_holder, dtype=jnp.int32)[None, :]
    ).astype(jnp.bfloat16)
    own_blocks = jnp.dot(
        picker,
        incoming.reshape(rep_count * per_holder, block_width),
        preferred_element_type=jnp.float32,
    ).astype(jnp.bfloat16)
    prefix_all, suffix_all = (
        lax.all_gather(own_blocks, "ep", axis=0, tiled=True),
        lax.all_gather(suffix_latent, "ep", axis=1, tiled=True),
    )
    prefix_keys = prefix_all.reshape(-1, latent_width)
    suffix_keys = suffix_all.reshape(-1, latent_width)
    query_rows = queries[0].reshape(SUF, -1, latent_width)
    pre_scores = (
        jnp.einsum("thc,kc->htk", query_rows, prefix_keys, preferred_element_type=jnp.float32)
        * score_scale
    )
    suf_scores = (
        jnp.einsum("thc,kc->htk", query_rows, suffix_keys, preferred_element_type=jnp.float32)
        * score_scale
    )
    key_index = jnp.arange(prefix_keys.shape[0], dtype=jnp.int32)
    pre_scores = jnp.where(key_index[None, None, :] < prefix_len[0], pre_scores, -1e30)
    causal = jnp.arange(SUF)[None, :] <= jnp.arange(SUF)[:, None]
    suf_scores = jnp.where(causal[None, :, :], suf_scores, -1e30)
    highest = jnp.maximum(jnp.max(pre_scores, axis=2), jnp.max(suf_scores, axis=2))
    pre_exps = jnp.exp(pre_scores - highest[:, :, None])
    suf_exps = jnp.exp(suf_scores - highest[:, :, None])
    denominator = jnp.sum(pre_exps, axis=2) + jnp.sum(suf_exps, axis=2)
    latent = jnp.einsum(
        "htk,kc->thc",
        pre_exps.astype(jnp.bfloat16),
        prefix_keys[:, :KVR],
        preferred_element_type=jnp.float32,
    )
    latent = latent + jnp.einsum(
        "htk,kc->thc",
        suf_exps.astype(jnp.bfloat16),
        suffix_keys[:, :KVR],
        preferred_element_type=jnp.float32,
    )
    latent = (latent / jnp.transpose(denominator)[:, :, None]).astype(jnp.bfloat16)
    head_values = jnp.einsum(
        "thc,hcv->thv", latent, w_value, preferred_element_type=jnp.float32
    ).astype(jnp.bfloat16)
    head_values = head_values.reshape(SUF, -1)
    attention = lax.psum_scatter(
        jnp.dot(head_values, w_out, preferred_element_type=jnp.float32),
        "ep",
        scatter_dimension=0,
        tiled=True,
    )
    residual = hidden[0].astype(jnp.float32) + attention
    scale_rows = lax.rsqrt(jnp.mean(residual * residual, axis=1, keepdims=True) + norm_eps)
    normed = (residual * scale_rows * norm_gain.astype(jnp.float32)).astype(jnp.bfloat16)
    tok_count = hidden.shape[1]
    chosen = experts[0]
    top_count = chosen.shape[1]
    expert_count = ep_count * w_gate.shape[0]
    capacity = min(tok_count, 2 * max(1, tok_count * top_count // expert_count))
    slot_count = expert_count * capacity
    flat_choice = chosen.reshape(-1)
    hits = (flat_choice[:, None] == jnp.arange(expert_count, dtype=jnp.int32)[None, :]).astype(
        jnp.int32
    )
    rank = jnp.sum((jnp.cumsum(hits, axis=0) - hits) * hits, axis=1)
    slot_id = flat_choice * capacity + rank
    slot_hot = (slot_id[:, None] == jnp.arange(slot_count, dtype=jnp.int32)[None, :]).astype(
        jnp.float32
    )
    owner = jnp.arange(flat_choice.shape[0], dtype=jnp.int32) // top_count
    token_hot = (owner[:, None] == jnp.arange(tok_count, dtype=jnp.int32)[None, :]).astype(
        jnp.float32
    )
    placing = jnp.dot(jnp.transpose(slot_hot), token_hot, precision=lax.Precision.HIGHEST)
    weighted_hot = token_hot * gate_weights[0].astype(jnp.float32).reshape(-1)[:, None]
    combine = jnp.dot(jnp.transpose(weighted_hot), slot_hot, precision=lax.Precision.HIGHEST)
    comb_high = combine.astype(jnp.bfloat16)
    tokens_all, placing_all, high_all = (
        lax.all_gather(normed[None], "rep", axis=0, tiled=True),
        lax.all_gather(placing.astype(jnp.bfloat16)[None], "rep", axis=0, tiled=True),
        lax.all_gather(comb_high[None], "rep", axis=0, tiled=True),
    )
    grouped = jnp.einsum(
        "rst,rtd->srd", placing_all, tokens_all, preferred_element_type=jnp.float32
    ).astype(jnp.bfloat16)
    grouped = grouped.reshape(ep_count, capacity * rep_count, -1)
    batch = lax.all_to_all(grouped, "ep", split_axis=0, concat_axis=0, tiled=True)
    item_count = batch.shape[1]
    units = expert_units(batch.reshape(-1, batch.shape[2]), w_gate[0], w_up[0])
    outputs = jnp.dot(units, w_down[0], preferred_element_type=jnp.float32).astype(jnp.bfloat16)
    served = lax.all_to_all(
        outputs.reshape(ep_count, item_count, -1), "ep", split_axis=0, concat_axis=0, tiled=True
    )
    served = served.reshape(ep_count, capacity, rep_count, -1)
    high_rows = high_all.reshape(rep_count, tok_count, ep_count, capacity)
    term = jnp.einsum("rtec,ecrd->rtd", high_rows, served, preferred_element_type=jnp.float32)
    mixture = lax.psum_scatter(term, "rep", scatter_dimension=0, tiled=True)[0]
    return (residual + mixture)[None]


def solution(mesh):
    return jax.shard_map(
        local,
        mesh=mesh,
        in_specs=(
            P("rep", None, "ep"),
            P("rep", "ep"),
            P("rep", "ep", None),
            P(),
            P(),
            P("rep"),
            P("rep", "ep", None),
            P("ep", None, None),
            P("ep", None),
            P(),
            P("rep", "ep", None),
            P("rep", "ep", None),
            P("ep", None, "rep"),
            P("ep", None, "rep"),
            P("ep", "rep", None),
        ),
        out_specs=P("rep", "ep", None),
        check_vma=False,
    )
```

profile of v0, /device:TPU:1, one launch (start us, length us, event | category | flops | bytes accessed | tf_op | source)
XLA Modules:
  0.0 874.1 jit_solution(10403566159922521318)
XLA Ops:
  6.6 0.9 constant_dynamic-slice_fusion
  7.5 0.1 copy.102
  7.6 0.1 fusion.69
  7.7 0.1 copy.89
  7.8 0.2 fusion.59
  8.0 1.4 fusion
  9.3 0.5 broadcast.104
  9.9 1.1 reduce.3
  10.9 1.3 reshape.165
  12.2 7.5 all-to-all-start
  19.7 0.0 all-gather.9.cloned.1.call-start
  19.7 0.8 dynamic_slice.13
  20.5 0.1 copy.103
  20.6 0.2 add_reduce_fusion
  20.8 11.4 %all-to-all-done = bf16[8,2,18432]{2,1,0:T(2,128)(2,1)} async-done(((bf16[8,2,18432]{2,1,0:T(2,128)(2,1)}), bf16[8,2,18432]{2,1,0:T(2,128)(2,1)}, u32[]{:S(2)}, u32[]{:S(2)}) %all-to-all-start) | async-done | bytes 589856 | tf_op jit(solution)/shard_map/all_to_all | solution.py:68
  32.2 2.3 reshape.166
  34.4 1.4 fusion.1
  35.9 0.0 all-gather.9.cloned.1.call-update
  35.9 0.0 all-reduce.5.cloned.1.call-start
  35.9 0.2 copy.77
  36.8 38.3 %all_gather.16 = bf16[1,73728]{1,0:T(2,128)(2,1)S(1)} all-gather(bf16[1,2304]{1,0:T(2,128)(2,1)S(1)} %copy-done.6), channel_id=1, replica_groups=mesh['rep'=8,'ep'=32] {'ep'}, dimensions={1}, use_global_device_ids=true | all-gather | bytes 152064 | tf_op jit(solution)/shard_map/all_gather | solution.py:82
  75.1 0.9 reduce.1
  76.0 0.2 reshape.129
  76.2 0.2 fusion.77
  76.4 27.2 %all-gather.9.cloned.1.call-done = bf16[32,2,36864]{2,1,0:T(2,128)(2,1)} async-done(((bf16[1,2,36864]{2,1,0:T(2,128)(2,1)}), bf16[32,2,36864]{2,1,0:T(2,128)(2,1)}) %all-gather.9.cloned.1.call-update) | async-done | bytes 4718608 | tf_op jit(solution)/shard_map/all_gather | solution.py:81
  103.7 12.3 %reshape.128 = bf16[4096,576]{1,0:T(8,128)(2,1)} reshape(bf16[32,2,36864]{2,1,0:T(2,128)(2,1)} %all-gather.9.cloned.1.call-done) | data formatting | bytes 9437184 | tf_op jit(solution)/shard_map/reshape | solution.py:84
  116.0 5.1 fusion.76
  121.1 0.6 fusion.8
  121.6 0.0 copy-start.9
  121.7 1.3 fusion.17
  123.0 0.5 fusion.34
  123.6 0.0 copy-start.12
  123.6 4.5 fusion.78
  128.2 0.0 all-reduce.5.cloned.1.call-update
  128.2 0.1 reshape_squeeze.7
  128.3 0.1 fusion.57
  128.4 0.1 reduce_window_sum.11
  128.4 0.6 dynamic-slice
  129.7 0.2 select_reduce_fusion
  129.9 0.3 fusion.36
  130.1 18.6 %all-gather.6 = bf16[8,64,4]{1,2,0:T(4,128)(2,1)S(1)} all-gather(bf16[1,64,4]{1,2,0:T(4,128)(2,1)S(1)} %fusion.36), channel_id=4, replica_groups=mesh['rep'=8,'ep'=32] {'rep'}, dimensions={0}, use_global_device_ids=true | all-gather | bytes 4608 | tf_op jit(solution)/shard_map/all_gather | solution.py:154
  148.7 215.1 %all-reduce.5.cloned.1.call-done = f32[128,7168]{1,0:T(8,128)} async-done(((f32[128,7168]{1,0:T(8,128)}), f32[128,7168]{1,0:T(8,128)}) %all-reduce.5.cloned.1.call-update) | async-done | bytes 3670032
  363.9 1.1 multiply_reduce_fusion
  365.0 1.0 fusion.56
  366.0 29.3 %all-gather.5 = bf16[8,4,7168]{2,1,0:T(4,128)(2,1)S(1)} all-gather(bf16[1,4,7168]{2,1,0:T(4,128)(2,1)S(1)} %fusion.56), channel_id=3, replica_groups=mesh['rep'=8,'ep'=32] {'rep'}, dimensions={0}, use_global_device_ids=true | all-gather | bytes 516096 | tf_op jit(solution)/shard_map/all_gather | solution.py:153
  395.4 2.1 fusion.2
  397.5 7.0 copy.86
  404.5 175.2 %all_to_all.15 = bf16[32,16,7168]{2,1,0:T(8,128)(2,1)S(1)} all-to-all(bf16[32,16,7168]{2,1,0:T(8,128)(2,1)} %bitcast.126), channel_id=1, replica_groups=mesh['rep'=8,'ep'=32] {'ep'}, dimensions={0} | all-to-all | bytes 14680064 | tf_op jit(solution)/shard_map/all_to_all | solution.py:161
  579.6 3.0 copy-done.1
  582.6 2.1 fusion.15
  584.7 15.4 %convolution_convert_fusion.2 = bf16[512,7168]{1,0:T(8,128)(2,1)} fusion(bf16[1,128,7168]{2,1,0:T(8,128)(2,1)S(1)} %copy-done, bf16[512,7168]{1,0:T(8,128)(2,1)} %bitcast.125, bf16[1,7168,128]{2,1,0:T(8,128)(2,1)} %param.28, f32[512,128]{1,0:T(8,128)S(1)} %fusion.15), kind=kOutput, calls=%fused_computation.4 | convolution fusion | flops 1883111424 | bytes 18612224 | tf_op jit(solution)/shard_map/dot_general | solution.py:164
  600.0 6.1 all-to-all-start.2
  606.1 0.0 all-reduce.7.cloned.1.call-start
  606.1 0.1 reshape.137
  606.2 0.3 fusion.35
  606.5 19.9 %all-gather.4 = bf16[8,4,64]{2,1,0:T(4,128)(2,1)S(1)} all-gather(bf16[1,4,64]{2,1,0:T(4,128)(2,1)S(1)} %fusion.35), channel_id=2, replica_groups=mesh['rep'=8,'ep'=32] {'rep'}, dimensions={0}, use_global_device_ids=true | all-gather | bytes 4608 | tf_op jit(solution)/shard_map/all_gather | solution.py:155
  626.4 0.1 copy.85
  626.5 0.1 copy.87
  626.6 143.7 %all-to-all-done.2 = bf16[32,16,7168]{2,1,0:T(8,128)(2,1)} async-done(((bf16[32,16,7168]{2,1,0:T(8,128)(2,1)}), bf16[32,16,7168]{2,1,0:T(8,128)(2,1)}, u32[]{:S(2)}, u32[]{:S(2)}) %all-to-all-start.2) | async-done | bytes 7340064 | tf_op jit(solution)/shard_map/all_to_all | solution.py:165
  770.3 11.9 %convolution_bitcast_fusion = f32[8,4,7168]{2,1,0:T(4,128)} fusion(bf16[8,4,32,2]{2,1,3,0:T(4,128)(2,1)S(1)} %copy.87, bf16[32,2,8,7168]{3,2,1,0:T(8,128)(2,1)} %bitcast.31), kind=kOutput, calls=%fused_computation.7 | convolution fusion | flops 29360128 | bytes 8261632 | tf_op jit(solution)/shard_map/rtec,ecrd->rtd/dot_general | solution.py:170
  782.2 0.0 all-reduce.7.cloned.1.call-update
  782.2 0.6 dynamic-slice.2
  782.8 82.5 %all-reduce.7.cloned.1.call-done = f32[8,4,7168]{2,1,0:T(4,128)} async-done(((f32[8,4,7168]{2,1,0:T(4,128)}), f32[8,4,7168]{2,1,0:T(4,128)}) %all-reduce.7.cloned.1.call-update) | async-done | bytes 917520
  865.3 2.3 fusion.51
  (33 shorter events, 0.2 us)
Async XLA Ops:
  6.5 578.1 %copy-start = (bf16[1,128,7168]{2,1,0:T(8,128)(2,1)S(1)}, bf16[1,128,7168]{2,1,0:T(8,128)(2,1)}, u32[]{:S(2)}) copy-start(bf16[1,128,7168]{2,1,0:T(8,128)(2,1)} %param.29) | copy-start | bytes 5505028
  6.5 29.4 %copy-start.4 = (bf16[1,128,1152]{2,1,0:T(8,128)(2,1)S(1)}, bf16[1,128,1152]{2,1,0:T(8,128)(2,1)}, u32[]{:S(2)}) copy-start(bf16[1,128,1152]{2,1,0:T(8,128)(2,1)} %param.15) | copy-start | bytes 884740
  6.5 30.3 %copy-start.6 = (bf16[1,2304]{1,0:T(2,128)(2,1)S(1)}, bf16[1,2304]{1,0:T(2,128)(2,1)}, u32[]{:S(2)}) copy-start(bf16[1,2304]{1,0:T(2,128)(2,1)} %param.16) | copy-start | bytes 13828
  12.2 20.0 %all-to-all-start = ((bf16[8,2,18432]{2,1,0:T(2,128)(2,1)}), bf16[8,2,18432]{2,1,0:T(2,128)(2,1)}, u32[]{:S(2)}, u32[]{:S(2)}) async-start(bf16[8,2,18432]{2,1,0:T(2,128)(2,1)} %reshape.165), calls=%async_computation | async-start | bytes 1179648 | tf_op jit(solution)/shard_map/all_to_all | solution.py:68
  19.7 84.0 %all-gather.9.cloned.1.call-start = ((), (), s32[]{:S(2)}) async-start(), calls=%async_computation.3 | async-start | bytes 4866048 | tf_op jit(solution)/shard_map/all_gather | solution.py:81
  35.9 328.0 %all-reduce.5.cloned.1.call-start = ((), (), s32[]{:S(2)}) async-start(), calls=%async_computation.4 | async-start | bytes 7340032
  116.0 5.7 copy-start.2
  121.6 1.4 copy-start.9
  123.6 4.6 copy-start.5
  123.6 4.6 copy-start.7
  123.6 4.8 copy-start.12
  123.6 240.3 %copy-start.3 = (bf16[1,4,7168]{2,1,0:T(4,128)(2,1)S(1)}, bf16[1,4,7168]{2,1,0:T(4,128)(2,1)}, u32[]{:S(2)}) copy-start(bf16[1,4,7168]{2,1,0:T(4,128)(2,1)} %param.21) | copy-start | bytes 172036
  404.5 178.1 %copy-start.8 = (bf16[1,7168,128]{2,1,0:T(8,128)(2,1)S(1)}, bf16[1,7168,128]{2,1,0:T(8,128)(2,1)}, u32[]{:S(2)}) copy-start(bf16[1,7168,128]{2,1,0:T(8,128)(2,1)} %param.27) | copy-start | bytes 5505028
  579.6 3.0 copy-start.1
  600.0 6.1 copy-start.10
  600.0 170.3 %all-to-all-start.2 = ((bf16[32,16,7168]{2,1,0:T(8,128)(2,1)}), bf16[32,16,7168]{2,1,0:T(8,128)(2,1)}, u32[]{:S(2)}, u32[]{:S(2)}) async-start(bf16[32,16,7168]{2,1,0:T(8,128)(2,1)} %bitcast.123), calls=%async_computation.2 | async-start | bytes 14680064 | tf_op jit(solution)/shard_map/all_to_all | solution.py:165
  606.1 259.2 %all-reduce.7.cloned.1.call-start = ((), (), s32[]{:S(2)}) async-start(), calls=%async_computation.5 | async-start | bytes 1835008
  770.3 11.9 %copy-start.11 = (u32[256]{0:T(256)S(1)}, u32[256]{0:T(256)}, u32[]{:S(2)}) copy-start(u32[256]{0:T(256)} %constant.91) | copy-start | bytes 3076
Sparse Core Ops, SparseCore 0:
  36.0 67.6 all-gather.8
  128.3 235.5 all-reduce.4
  782.3 82.9 all-reduce.6
where the time goes:
time: 879 us; the launch traced here: 874 us
  waiting for transfers between devices  480 us (55%)
  blocking collectives  281 us (32%)
  matrix products  46.5 us (5%)
  local copies, waits for them, and re-layouts  30.3 us (3%)
  between operations  14.7 us (2%)
  starting transfers between devices  13.7 us (2%)
    unnamed x5, waiting for transfers between devices  298 us
    all_to_all x1, blocking collectives, local(): lax.all_to_all(grouped, 'ep', split_axis=0, concat_axis=0, tiled=True)  175 us
    all_to_all x1, waiting for transfers between devices, local(): lax.all_to_all(outputs.reshape(ep_count, item_count, -1), 'ep', split_axi...  144 us
    all_gather x1, blocking collectives, local(): lax.all_gather(suffix_latent, 'ep', axis=1, tiled=True)  38.3 us
    all_gather x1, blocking collectives, local(): lax.all_gather(normed[None], 'rep', axis=0, tiled=True)  29.3 us
    all_gather x1, waiting for transfers between devices, local(): lax.all_gather(own_blocks, 'ep', axis=0, tiled=True)  27.2 us
    all_gather x1, blocking collectives, local(): lax.all_gather(comb_high[None], 'rep', axis=0, tiled=True)  19.9 us
    all_gather x1, blocking collectives, local(): lax.all_gather(placing.astype(jnp.bfloat16)[None], 'rep', axis=0, tiled=T...  18.6 us
  transfers between devices with their start and end apart: 5, of which 5 were waited for; matrix products, arithmetic and copies ran while one was open for 1% of the time, Pallas kernels for 0%

commit v1 on v0

--- a/solution.py
+++ b/solution.py
@@ -77,10 +77,11 @@
         incoming.reshape(rep_count * per_holder, block_width),
         preferred_element_type=jnp.float32,
     ).astype(jnp.bfloat16)
-    prefix_all, suffix_all = (
-        lax.all_gather(own_blocks, "ep", axis=0, tiled=True),
-        lax.all_gather(suffix_latent, "ep", axis=1, tiled=True),
-    )
+    prefix_width = own_blocks.shape[0] * block_width
+    packed = jnp.concatenate([own_blocks.reshape(1, prefix_width), suffix_latent], axis=1)
+    gathered = lax.all_gather(packed, "ep", axis=0, tiled=True)
+    prefix_all = gathered[:, :prefix_width]
+    suffix_all = gathered[:, prefix_width:]
     prefix_keys = prefix_all.reshape(-1, latent_width)
     suffix_keys = suffix_all.reshape(-1, latent_width)
     query_rows = queries[0].reshape(SUF, -1, latent_width)
@@ -117,12 +118,9 @@
         "thc,hcv->thv", latent, w_value, preferred_element_type=jnp.float32
     ).astype(jnp.bfloat16)
     head_values = head_values.reshape(SUF, -1)
-    attention = lax.psum_scatter(
-        jnp.dot(head_values, w_out, preferred_element_type=jnp.float32),
-        "ep",
-        scatter_dimension=0,
-        tiled=True,
-    )
+    partial = jnp.dot(head_values, w_out, preferred_element_type=jnp.float32)
+    partial = partial.reshape(ep_count, SUF // ep_count, -1)
+    attention = jnp.sum(lax.all_to_all(partial, "ep", 0, 0, tiled=True), axis=0)
     residual = hidden[0].astype(jnp.float32) + attention
     scale_rows = lax.rsqrt(jnp.mean(residual * residual, axis=1, keepdims=True) + norm_eps)
     normed = (residual * scale_rows * norm_gain.astype(jnp.float32)).astype(jnp.bfloat16)
@@ -148,27 +146,21 @@
     placing = jnp.dot(jnp.transpose(slot_hot), token_hot, precision=lax.Precision.HIGHEST)
     weighted_hot = token_hot * gate_weights[0].astype(jnp.float32).reshape(-1)[:, None]
     combine = jnp.dot(jnp.transpose(weighted_hot), slot_hot, precision=lax.Precision.HIGHEST)
-    comb_high = combine.astype(jnp.bfloat16)
-    tokens_all, placing_all, high_all = (
-        lax.all_gather(normed[None], "rep", axis=0, tiled=True),
-        lax.all_gather(placing.astype(jnp.bfloat16)[None], "rep", axis=0, tiled=True),
-        lax.all_gather(comb_high[None], "rep", axis=0, tiled=True),
+    grouped = jnp.dot(
+        placing.astype(jnp.bfloat16), normed, preferred_element_type=jnp.float32
+    ).astype(jnp.bfloat16)
+    grouped = grouped.reshape(expert_count, capacity, -1)
+    mine = lax.all_to_all(grouped, "ep", split_axis=0, concat_axis=0, tiled=True)
+    copies = jnp.broadcast_to(mine[None], (rep_count,) + mine.shape)
+    batch = lax.all_to_all(copies, "rep", split_axis=0, concat_axis=0, tiled=True)
+    units = expert_units(batch.reshape(-1, batch.shape[-1]), w_gate[0], w_up[0])
+    outputs = jnp.dot(units, w_down[0], preferred_element_type=jnp.float32).astype(jnp.bfloat16)
+    back = lax.all_to_all(outputs.reshape(batch.shape), "rep", split_axis=0, concat_axis=0, tiled=True)
+    slice_sum = jnp.sum(back.astype(jnp.float32), axis=0)
+    served = lax.all_to_all(slice_sum, "ep", split_axis=0, concat_axis=0, tiled=True)
+    mixture = jnp.dot(
+        combine, served.reshape(slot_count, -1), precision=lax.Precision.HIGHEST
     )
-    grouped = jnp.einsum(
-        "rst,rtd->srd", placing_all, tokens_all, preferred_element_type=jnp.float32
-    ).astype(jnp.bfloat16)
-    grouped = grouped.reshape(ep_count, capacity * rep_count, -1)
-    batch = lax.all_to_all(grouped, "ep", split_axis=0, concat_axis=0, tiled=True)
-    item_count = batch.shape[1]
-    units = expert_units(batch.reshape(-1, batch.shape[2]), w_gate[0], w_up[0])
-    outputs = jnp.dot(units, w_down[0], preferred_element_type=jnp.float32).astype(jnp.bfloat16)
-    served = lax.all_to_all(
-        outputs.reshape(ep_count, item_count, -1), "ep", split_axis=0, concat_axis=0, tiled=True
-    )
-    served = served.reshape(ep_count, capacity, rep_count, -1)
-    high_rows = high_all.reshape(rep_count, tok_count, ep_count, capacity)
-    term = jnp.einsum("rtec,ecrd->rtd", high_rows, served, preferred_element_type=jnp.float32)
-    mixture = lax.psum_scatter(term, "rep", scatter_dimension=0, tiled=True)[0]
     return (residual + mixture)[None]
 
 

time: 879 us -> 578 us (0.66)
  waiting for transfers between devices: 480 us -> 213 us
  blocking collectives: 281 us -> 207 us
  local copies, waits for them, and re-layouts: 30.3 us -> 66.7 us
  matrix products: 46.5 us -> 37.3 us
  starting transfers between devices: 13.7 us -> 22.5 us
    unnamed x5 -> x1, waiting for transfers between devices: 298 us -> 0.02 us
    all_to_all x0 -> x2, blocking collectives: none -> 177 us  [the longest x1 89.6 us: local(): lax.all_to_all(copies, 'rep', split_axis=0, concat_axis=0, tiled=True)]
    all_to_all x1, blocking collectives: 175 us -> 29.4 us  [local(): lax.all_to_all(grouped, 'ep', split_axis=0, concat_axis=0, tiled=True)]
    all_gather x4 -> x0, blocking collectives: 106 us -> none  [the longest x1 38.3 us: local(): lax.all_gather(suffix_latent, 'ep', axis=1, tiled=True)]
    all_gather x1, waiting for transfers between devices: 27.2 us -> 72.2 us  [local(): gathered = lax.all_gather(packed, 'ep', axis=0, tiled=True)]
    reshape x1 -> x4, local copies, waits for them, and re-layouts: 0.1 us -> 35 us  [the longest x1 15.4 us: local(): units = expert_units(batch.reshape(-1, batch.shape[-1]), w_gate[0], w_up[0])]
    all_to_all x1 -> x2, waiting for transfers between devices: 144 us -> 129 us  [the longest x1 84.7 us: local(): attention = jnp.sum(lax.all_to_all(partial, 'ep', 0, 0, tiled=True), axis=0)]
    reduce_sum x0 -> x2, other arithmetic: none -> 12.4 us  [the longest x1 9.79 us: local(): slice_sum = jnp.sum(back.astype(jnp.float32), axis=0)]
  transfers between devices with their start and end apart: 5 -> 4, of which waited for: 5 -> 4; matrix products, arithmetic and copies ran while one was open for 1% -> 0% of each run, Pallas kernels for 0% -> 0%
where the time goes in v1:
time: 578 us; the launch traced here: 576 us
  waiting for transfers between devices  213 us (37%)
  blocking collectives  207 us (36%)
  local copies, waits for them, and re-layouts  66.7 us (12%)
  matrix products  37.3 us (6%)
  starting transfers between devices  22.5 us (4%)
  other arithmetic  16 us (3%)
  between operations  14.4 us (2%)
    all_to_all x1, blocking collectives, local(): lax.all_to_all(copies, 'rep', split_axis=0, concat_axis=0, tiled=True)  89.6 us
    all_to_all x1, blocking collectives, local(): lax.all_to_all(outputs.reshape(batch.shape), 'rep', split_axis=0, concat_...  87.9 us
    all_to_all x1, waiting for transfers between devices, local(): attention = jnp.sum(lax.all_to_all(partial, 'ep', 0, 0, tiled=True), axis=0)  84.7 us
    all_gather x1, waiting for transfers between devices, local(): gathered = lax.all_gather(packed, 'ep', axis=0, tiled=True)  72.2 us
    all_to_all x1, waiting for transfers between devices, local(): lax.all_to_all(slice_sum, 'ep', split_axis=0, concat_axis=0, tiled=True)  44.3 us
    all_to_all x1, blocking collectives, local(): lax.all_to_all(grouped, 'ep', split_axis=0, concat_axis=0, tiled=True)  29.4 us
    reshape x1, local copies, waits for them, and re-layouts, local(): units = expert_units(batch.reshape(-1, batch.shape[-1]), w_gate[0], w_up[0])  15.4 us
    dot_general x1, matrix products, local(): jnp.dot(units, w_down[0], preferred_element_type=jnp.float32)  15.3 us
  transfers between devices with their start and end apart: 4, of which 4 were waited for; matrix products, arithmetic and copies ran while one was open for 0% of the time, Pallas kernels for 0%

profile of v1, /device:TPU:1, one launch (start us, length us, event | category | flops | bytes accessed | tf_op | source)
XLA Modules:
  0.0 576.4 jit_solution(8854533107538966464)
XLA Ops:
  6.5 0.0 copy-start
  6.6 0.9 constant_dynamic-slice_fusion
  7.5 0.1 copy.86
  7.5 0.1 fusion.67
  7.7 0.1 copy.75
  7.8 0.2 fusion.57
  8.0 1.4 fusion
  9.4 0.5 broadcast.104
  9.9 1.1 reduce.2
  11.0 1.3 reshape.149
  12.2 7.5 %all-to-all-start = ((bf16[8,2,18432]{2,1,0:T(2,128)(2,1)}), bf16[8,2,18432]{2,1,0:T(2,128)(2,1)}, u32[]{:S(2)}, u32[]{:S(2)}) async-start(bf16[8,2,18432]{2,1,0:T(2,128)(2,1)} %reshape.149), calls=%async_computation | async-start | bytes 1179648 | tf_op jit(solution)/shard_map/all_to_all | solution.py:68
  19.7 0.0 all-gather.3.cloned.1.call-start
  19.8 0.8 dynamic_slice.13
  20.5 0.1 copy.87
  20.6 0.2 add_reduce_fusion
  20.8 11.4 %all-to-all-done = bf16[8,2,18432]{2,1,0:T(2,128)(2,1)} async-done(((bf16[8,2,18432]{2,1,0:T(2,128)(2,1)}), bf16[8,2,18432]{2,1,0:T(2,128)(2,1)}, u32[]{:S(2)}, u32[]{:S(2)}) %all-to-all-start) | async-done | bytes 589856 | tf_op jit(solution)/shard_map/all_to_all | solution.py:68
  32.2 2.3 reshape.150
  34.5 0.8 fusion.1
  35.2 0.2 copy.90
  35.5 1.0 maximum_bitcast_fusion
  36.5 0.0 all-gather.3.cloned.1.call-update
  36.6 0.2 copy.65
  37.5 72.2 %all-gather.3.cloned.1.call-done = bf16[32,1,76032]{2,1,0:T(2,128)(2,1)} async-done(((bf16[1,1,76032]{2,1,0:T(2,128)(2,1)}), bf16[32,1,76032]{2,1,0:T(2,128)(2,1)}) %all-gather.3.cloned.1.call-update) | async-done | bytes 4866064 | tf_op jit(solution)/shard_map/all_gather | solution.py:82
  109.7 4.3 copy.98
  114.0 2.5 slice.16
  116.5 8.8 %reshape.131 = bf16[4096,576]{1,0:T(8,128)(2,1)} reshape(bf16[32,73728]{1,0:T(8,128)(2,1)} %slice.16) | data formatting | bytes 9437184 | tf_op jit(solution)/shard_map/reshape | solution.py:85
  125.3 0.2 reshape.132
  125.5 0.0 slice-start
  125.5 0.0 slice-start.1
  125.5 5.1 fusion.74
  130.6 0.2 fusion.75
  130.8 0.6 fusion.7
  131.4 0.0 copy-start.6
  131.4 1.3 fusion.6
  132.8 0.6 fusion.33
  133.4 0.1 copy.72
  133.5 2.7 fusion.9
  136.2 4.2 copy.74
  140.4 6.0 %all-to-all-start.1 = ((f32[32,4,7168]{2,1,0:T(4,128)}), f32[32,4,7168]{2,1,0:T(4,128)}, u32[]{:S(2)}, u32[]{:S(2)}) async-start(f32[32,4,7168]{2,1,0:T(4,128)} %copy.74), calls=%async_computation.1 | async-start | bytes 7340032 | tf_op jit(solution)/shard_map/all_to_all | solution.py:123
  146.4 0.1 reshape_squeeze.7
  146.4 0.1 fusion.55
  146.5 0.1 reduce_window_sum.11
  146.6 0.2 select_reduce_fusion
  146.8 0.3 convolution_convert_fusion.4
  147.0 84.7 %all-to-all-done.1 = f32[32,4,7168]{2,1,0:T(4,128)} async-done(((f32[32,4,7168]{2,1,0:T(4,128)}), f32[32,4,7168]{2,1,0:T(4,128)}, u32[]{:S(2)}, u32[]{:S(2)}) %all-to-all-start.1) | async-done | bytes 3670048 | tf_op jit(solution)/shard_map/all_to_all | solution.py:123
  231.7 2.6 reduce_sum.66
  234.4 0.2 multiply_reduce_fusion
  234.5 0.5 convolution_convert_fusion.3
  235.0 1.3 reshape.133
  236.3 29.4 %all_to_all.30 = bf16[32,2,7168]{2,1,0:T(2,128)(2,1)S(1)} all-to-all(bf16[32,2,7168]{2,1,0:T(2,128)(2,1)} %reshape.133), channel_id=1, replica_groups=mesh['rep'=8,'ep'=32] {'ep'}, dimensions={0} | all-to-all | bytes 1835008 | tf_op jit(solution)/shard_map/all_to_all | solution.py:153
  265.7 4.9 broadcast_in_dim.32
  270.7 89.6 %all_to_all.31 = bf16[8,32,2,7168]{3,2,1,0:T(2,128)(2,1)} all-to-all(bf16[8,32,2,7168]{3,2,1,0:T(2,128)(2,1)S(1)} %broadcast_in_dim.32), channel_id=1, replica_groups=mesh['rep'=8,'ep'=32] {'rep'}, dimensions={0} | all-to-all | bytes 14680064 | tf_op jit(solution)/shard_map/all_to_all | solution.py:155
  360.2 15.4 %reshape.134 = bf16[512,7168]{1,0:T(8,128)(2,1)} reshape(bf16[8,32,2,7168]{3,2,1,0:T(2,128)(2,1)} %all_to_all.31) | data formatting | bytes 14680064 | tf_op jit(solution)/shard_map/reshape | solution.py:156
  375.7 5.6 fusion.16
  381.3 15.3 %convolution_convert_fusion.2 = bf16[512,7168]{1,0:T(8,128)(2,1)} fusion(bf16[1,128,7168]{2,1,0:T(8,128)(2,1)S(1)} %copy-done, bf16[512,7168]{1,0:T(8,128)(2,1)} %reshape.134, bf16[1,7168,128]{2,1,0:T(8,128)(2,1)} %param.28, f32[512,128]{1,0:T(8,128)S(1)} %fusion.16), kind=kOutput, calls=%fused_computation.5 | convolution fusion | flops 1883111424 | bytes 18612224 | tf_op jit(solution)/shard_map/dot_general | solution.py:157
  396.7 14.9 %reshape.135 = bf16[8,32,2,7168]{3,2,1,0:T(2,128)(2,1)} reshape(bf16[512,7168]{1,0:T(8,128)(2,1)} %convolution_convert_fusion.2) | data formatting | bytes 14680064 | tf_op jit(solution)/shard_map/reshape | solution.py:158
  411.6 87.9 %all_to_all.32 = bf16[8,32,2,7168]{3,2,1,0:T(2,128)(2,1)} all-to-all(bf16[8,32,2,7168]{3,2,1,0:T(2,128)(2,1)} %reshape.135), channel_id=1, replica_groups=mesh['rep'=8,'ep'=32] {'rep'}, dimensions={0} | all-to-all | bytes 14680064 | tf_op jit(solution)/shard_map/all_to_all | solution.py:158
  499.5 9.8 %convert_reduce_fusion = f32[32,2,7168]{2,1,0:T(2,128)} fusion(bf16[8,32,2,7168]{3,2,1,0:T(2,128)(2,1)} %all_to_all.32), kind=kLoop, calls=%fused_computation.4 | loop fusion | flops 6881280 | bytes 9175040 | tf_op jit(solution)/shard_map/reduce_sum | solution.py:159
  509.3 9.0 %all-to-all-start.5 = ((f32[32,2,7168]{2,1,0:T(2,128)}), f32[32,2,7168]{2,1,0:T(2,128)}, u32[]{:S(2)}, u32[]{:S(2)}) async-start(f32[32,2,7168]{2,1,0:T(2,128)} %convert_reduce_fusion), calls=%async_computation.5 | async-start | bytes 3670016 | tf_op jit(solution)/shard_map/all_to_all | solution.py:160
  518.3 0.1 reshape.138
  518.4 0.3 fusion.54
  518.6 44.3 %all-to-all-done.5 = f32[32,2,7168]{2,1,0:T(2,128)} async-done(((f32[32,2,7168]{2,1,0:T(2,128)}), f32[32,2,7168]{2,1,0:T(2,128)}, u32[]{:S(2)}, u32[]{:S(2)}) %all-to-all-start.5) | async-done | bytes 1835040 | tf_op jit(solution)/shard_map/all_to_all | solution.py:160
  563.0 3.4 reshape.136
  566.4 3.1 fusion.2
  (29 shorter events, 0.2 us)
Async XLA Ops:
  6.5 374.8 %copy-start = (bf16[1,128,7168]{2,1,0:T(8,128)(2,1)S(1)}, bf16[1,128,7168]{2,1,0:T(8,128)(2,1)}, u32[]{:S(2)}) copy-start(bf16[1,128,7168]{2,1,0:T(8,128)(2,1)} %param.29) | copy-start | bytes 5505028
  6.5 28.9 %copy-start.4 = (bf16[1,2304]{1,0:T(2,128)(2,1)S(1)}, bf16[1,2304]{1,0:T(2,128)(2,1)}, u32[]{:S(2)}) copy-start(bf16[1,2304]{1,0:T(2,128)(2,1)} %param.16) | copy-start | bytes 13828
  8.0 28.6 %copy-start.2 = (bf16[1,128,1152]{2,1,0:T(8,128)(2,1)S(1)}, bf16[1,128,1152]{2,1,0:T(8,128)(2,1)}, u32[]{:S(2)}) copy-start(bf16[1,128,1152]{2,1,0:T(8,128)(2,1)} %param.15) | copy-start | bytes 884740
  12.2 20.0 %all-to-all-start = ((bf16[8,2,18432]{2,1,0:T(2,128)(2,1)}), bf16[8,2,18432]{2,1,0:T(2,128)(2,1)}, u32[]{:S(2)}, u32[]{:S(2)}) async-start(bf16[8,2,18432]{2,1,0:T(2,128)(2,1)} %reshape.149), calls=%async_computation | async-start | bytes 1179648 | tf_op jit(solution)/shard_map/all_to_all | solution.py:68
  19.7 90.0 %all-gather.3.cloned.1.call-start = ((), (), s32[]{:S(2)}) async-start(), calls=%async_computation.6 | async-start | bytes 10036224 | tf_op jit(solution)/shard_map/all_gather | solution.py:82
  125.5 5.9 %slice-start = ((s8[5242880]{0:T(1024)(128)(4,1)}), s8[4194304]{0:T(1024)(128)(4,1)S(1)}, s32[]{:S(2)}) async-start(s8[5242880]{0:T(1024)(128)(4,1)} %bitcast.106), calls=%async_computation.7 | async-start | bytes 8388608
  125.5 5.9 %slice-start.1 = ((s8[5242880]{0:T(1024)(128)(4,1)}), s8[1048576]{0:T(1024)(128)(4,1)S(1)}, s32[]{:S(2)}) async-start(s8[5242880]{0:T(1024)(128)(4,1)} %bitcast.106), calls=%async_computation.8 | async-start | bytes 2097152
  131.4 1.4 copy-start.6
  140.4 6.0 %copy-start.5 = (s32[1,4,8]{2,1,0:T(4,128)S(1)}, s32[1,4,8]{2,1,0:T(4,128)}, u32[]{:S(2)}) copy-start(s32[1,4,8]{2,1,0:T(4,128)} %param.25) | copy-start | bytes 388
  140.4 6.2 %copy-start.3 = (bf16[7168]{0:T(1024)(128)(2,1)S(1)}, bf16[7168]{0:T(1024)(128)(2,1)}, u32[]{:S(2)}) copy-start(bf16[7168]{0:T(1024)(128)(2,1)} %param.24) | copy-start | bytes 43012
  140.4 94.0 %copy-start.1 = (bf16[1,4,7168]{2,1,0:T(4,128)(2,1)S(1)}, bf16[1,4,7168]{2,1,0:T(4,128)(2,1)}, u32[]{:S(2)}) copy-start(bf16[1,4,7168]{2,1,0:T(4,128)(2,1)} %param.21) | copy-start | bytes 172036
  140.4 91.4 %all-to-all-start.1 = ((f32[32,4,7168]{2,1,0:T(4,128)}), f32[32,4,7168]{2,1,0:T(4,128)}, u32[]{:S(2)}, u32[]{:S(2)}) async-start(f32[32,4,7168]{2,1,0:T(4,128)} %copy.74), calls=%async_computation.1 | async-start | bytes 7340032 | tf_op jit(solution)/shard_map/all_to_all | solution.py:123
  499.5 18.8 %copy-start.7 = (bf16[1,4,8]{2,1,0:T(4,128)(2,1)S(1)}, bf16[1,4,8]{2,1,0:T(4,128)(2,1)}, u32[]{:S(2)}) copy-start(bf16[1,4,8]{2,1,0:T(4,128)(2,1)} %param.26) | copy-start | bytes 196
  509.3 53.7 %all-to-all-start.5 = ((f32[32,2,7168]{2,1,0:T(2,128)}), f32[32,2,7168]{2,1,0:T(2,128)}, u32[]{:S(2)}, u32[]{:S(2)}) async-start(f32[32,2,7168]{2,1,0:T(2,128)} %convert_reduce_fusion), calls=%async_computation.5 | async-start | bytes 3670016 | tf_op jit(solution)/shard_map/all_to_all | solution.py:160
Sparse Core Ops, SparseCore 0:
  36.7 72.9 all-gather.2

commit v2 on v1

--- a/solution.py
+++ b/solution.py
@@ -1,11 +1,12 @@
 import jax
 import jax.numpy as jnp
 from jax import lax
-from jax.sharding import PartitionSpec as P
+from jax.sharding import Mesh, PartitionSpec as P
 
 KVR = 512
 ROPE = 64
 SUF = 128
+EP = ("epo", "core")
 
 
 score_scale = 0.07216878364870323
@@ -36,9 +37,9 @@
     w_down,
 ):
     rep_count = lax.axis_size("rep")
-    ep_count = lax.axis_size("ep")
+    ep_count = lax.axis_size(EP)
     rep_index = lax.axis_index("rep")
-    ep_index = lax.axis_index("ep")
+    ep_index = lax.axis_index("epo") * lax.axis_size("core") + lax.axis_index("core")
     pool_count = cache_pool.shape[1]
     block_width = cache_pool.shape[2]
     per_device = holders.shape[1] // ep_count
@@ -79,7 +80,7 @@
     ).astype(jnp.bfloat16)
     prefix_width = own_blocks.shape[0] * block_width
     packed = jnp.concatenate([own_blocks.reshape(1, prefix_width), suffix_latent], axis=1)
-    gathered = lax.all_gather(packed, "ep", axis=0, tiled=True)
+    gathered = lax.all_gather(packed, EP, axis=0, tiled=True)
     prefix_all = gathered[:, :prefix_width]
     suffix_all = gathered[:, prefix_width:]
     prefix_keys = prefix_all.reshape(-1, latent_width)
@@ -119,8 +120,11 @@
     ).astype(jnp.bfloat16)
     head_values = head_values.reshape(SUF, -1)
     partial = jnp.dot(head_values, w_out, preferred_element_type=jnp.float32)
-    partial = partial.reshape(ep_count, SUF // ep_count, -1)
-    attention = jnp.sum(lax.all_to_all(partial, "ep", 0, 0, tiled=True), axis=0)
+    core_count = lax.axis_size("core")
+    partial = partial.reshape(ep_count // core_count, core_count, -1)
+    partial = jnp.sum(lax.all_to_all(partial, "core", 1, 1, tiled=True), axis=1)
+    attention = jnp.sum(lax.all_to_all(partial, "epo", 0, 0, tiled=True), axis=0)
+    attention = attention.reshape(SUF // ep_count, -1)
     residual = hidden[0].astype(jnp.float32) + attention
     scale_rows = lax.rsqrt(jnp.mean(residual * residual, axis=1, keepdims=True) + norm_eps)
     normed = (residual * scale_rows * norm_gain.astype(jnp.float32)).astype(jnp.bfloat16)
@@ -149,42 +153,46 @@
     grouped = jnp.dot(
         placing.astype(jnp.bfloat16), normed, preferred_element_type=jnp.float32
     ).astype(jnp.bfloat16)
-    grouped = grouped.reshape(expert_count, capacity, -1)
-    mine = lax.all_to_all(grouped, "ep", split_axis=0, concat_axis=0, tiled=True)
+    width = grouped.shape[1]
+    grouped = grouped.reshape(expert_count, capacity * width)
+    mine = lax.all_to_all(grouped, EP, split_axis=0, concat_axis=0, tiled=True)
+    mine = mine.reshape(slot_count, width)
     copies = jnp.broadcast_to(mine[None], (rep_count,) + mine.shape)
     batch = lax.all_to_all(copies, "rep", split_axis=0, concat_axis=0, tiled=True)
-    units = expert_units(batch.reshape(-1, batch.shape[-1]), w_gate[0], w_up[0])
+    units = expert_units(batch.reshape(-1, width), w_gate[0], w_up[0])
     outputs = jnp.dot(units, w_down[0], preferred_element_type=jnp.float32).astype(jnp.bfloat16)
     back = lax.all_to_all(outputs.reshape(batch.shape), "rep", split_axis=0, concat_axis=0, tiled=True)
-    slice_sum = jnp.sum(back.astype(jnp.float32), axis=0)
-    served = lax.all_to_all(slice_sum, "ep", split_axis=0, concat_axis=0, tiled=True)
+    slice_sum = jnp.sum(back.astype(jnp.float32), axis=0).reshape(expert_count, capacity * width)
+    served = lax.all_to_all(slice_sum, EP, split_axis=0, concat_axis=0, tiled=True)
     mixture = jnp.dot(
-        combine, served.reshape(slot_count, -1), precision=lax.Precision.HIGHEST
+        combine, served.reshape(slot_count, width), precision=lax.Precision.HIGHEST
     )
     return (residual + mixture)[None]
 
 
 def solution(mesh):
+    rep_n, ep_n = mesh.devices.shape
+    fine = Mesh(mesh.devices.reshape(rep_n, ep_n // 2, 2), ("rep", "epo", "core"))
     return jax.shard_map(
         local,
-        mesh=mesh,
+        mesh=fine,
         in_specs=(
-            P("rep", None, "ep"),
-            P("rep", "ep"),
-            P("rep", "ep", None),
+            P("rep", None, EP),
+            P("rep", EP),
+            P("rep", EP, None),
             P(),
             P(),
             P("rep"),
-            P("rep", "ep", None),
-            P("ep", None, None),
-            P("ep", None),
+            P("rep", EP, None),
+            P(EP, None, None),
+            P(EP, None),
             P(),
-            P("rep", "ep", None),
-            P("rep", "ep", None),
-            P("ep", None, "rep"),
-            P("ep", None, "rep"),
-            P("ep", "rep", None),
+            P("rep", EP, None),
+            P("rep", EP, None),
+            P(EP, None, "rep"),
+            P(EP, None, "rep"),
+            P(EP, "rep", None),
         ),
-        out_specs=P("rep", "ep", None),
+        out_specs=P("rep", EP, None),
         check_vma=False,
     )

time: 578 us -> 565 us (0.978); the launches traced: 576 us -> 554 us
  waiting for transfers between devices: 213 us -> 170 us
  other arithmetic: 16 us -> 34.3 us
  blocking collectives: 207 us -> 216 us
    all_to_all x2, waiting for transfers between devices: 129 us -> 86.2 us  [the longest x1 44.1 us: local(): lax.all_to_all(slice_sum, EP, split_axis=0, concat_axis=0, tiled=True)]
    reshape x4, local copies, waits for them, and re-layouts: 35 us -> 13 us  [the longest x2 10.1 us: local(): partial = partial.reshape(ep_count // core_count, core_count, -1)]
    all_to_all x0 -> x3, other arithmetic: none -> 21.8 us  [the longest x2 14.7 us: local(): mine = lax.all_to_all(grouped, EP, split_axis=0, concat_axis=0, tiled=True)]
    unnamed x27 -> x33, local copies, waits for them, and re-layouts: 8.47 us -> 20.4 us
    all_to_all x0 -> x3, local copies, waits for them, and re-layouts: none -> 11.2 us  [the longest x1 4.67 us: local(): lax.all_to_all(partial, 'epo', 0, 0, tiled=True)]
    all_to_all x1 -> x2, blocking collectives: 29.4 us -> 40.1 us  [the longest x1 32.3 us: local(): mine = lax.all_to_all(grouped, EP, split_axis=0, concat_axis=0, tiled=True)]
    reduce_sum x2 -> x3, other arithmetic: 12.4 us -> 8.9 us  [the longest x1 3.72 us: local(): partial = jnp.sum(lax.all_to_all(partial, 'core', 1, 1, tiled=True), axis=1)]
where the time goes in v2:
time: 565 us; the launch traced here: 554 us
  blocking collectives  216 us (38%)
  waiting for transfers between devices  170 us (30%)
  local copies, waits for them, and re-layouts  61.9 us (11%)
  matrix products  35.5 us (6%)
  other arithmetic  34.3 us (6%)
  starting transfers between devices  21.7 us (4%)
  between operations  14.6 us (3%)
    all_to_all x1, blocking collectives, local(): lax.all_to_all(copies, 'rep', split_axis=0, concat_axis=0, tiled=True)  89.7 us
    all_to_all x1, blocking collectives, local(): lax.all_to_all(outputs.reshape(batch.shape), 'rep', split_axis=0, concat_...  86.1 us
    all_gather x1, waiting for transfers between devices, local(): gathered = lax.all_gather(packed, EP, axis=0, tiled=True)  72.2 us
    all_to_all x1, waiting for transfers between devices, local(): lax.all_to_all(slice_sum, EP, split_axis=0, concat_axis=0, tiled=True)  44.1 us
    all_to_all x1, waiting for transfers between devices, local(): lax.all_to_all(partial, 'epo', 0, 0, tiled=True)  42.1 us
    all_to_all x1, blocking collectives, local(): mine = lax.all_to_all(grouped, EP, split_axis=0, concat_axis=0, tiled=True)  32.3 us
    unnamed x33, local copies, waits for them, and re-layouts  20.4 us
    dot_general x1, matrix products, local(): jnp.dot(units, w_down[0], preferred_element_type=jnp.float32)  15.3 us
  transfers between devices with their start and end apart: 4, of which 4 were waited for; matrix products, arithmetic and copies ran while one was open for 0% of the time, Pallas kernels for 0%

profile of v2, /device:TPU:1, one launch (start us, length us, event | category | flops | bytes accessed | tf_op | source)
XLA Modules:
  0.0 553.7 jit_solution(363248622582021206)
XLA Ops:
  6.5 0.9 constant_dynamic-slice_fusion
  7.5 0.1 copy.87
  7.5 0.1 fusion.63
  7.6 0.1 copy.75
  7.7 0.2 fusion.53
  7.9 1.4 fusion
  9.3 0.5 broadcast.105
  9.8 1.1 reduce.5
  11.0 1.3 reshape.166
  12.2 7.5 %all-to-all-start = ((bf16[8,2,18432]{2,1,0:T(2,128)(2,1)}), bf16[8,2,18432]{2,1,0:T(2,128)(2,1)}, u32[]{:S(2)}, u32[]{:S(2)}) async-start(bf16[8,2,18432]{2,1,0:T(2,128)(2,1)} %reshape.166), calls=%async_computation | async-start | bytes 1179648 | tf_op jit(solution)/shard_map/all_to_all | solution.py:69
  19.8 0.8 dynamic_slice.13
  20.5 0.1 copy.88
  20.6 0.2 add_reduce_fusion
  20.8 11.4 %all-to-all-done = bf16[8,2,18432]{2,1,0:T(2,128)(2,1)} async-done(((bf16[8,2,18432]{2,1,0:T(2,128)(2,1)}), bf16[8,2,18432]{2,1,0:T(2,128)(2,1)}, u32[]{:S(2)}, u32[]{:S(2)}) %all-to-all-start) | async-done | bytes 589856 | tf_op jit(solution)/shard_map/all_to_all | solution.py:69
  32.2 2.3 reshape.167
  34.5 0.8 fusion.1
  35.2 0.2 copy.91
  35.5 1.0 maximum_bitcast_fusion
  36.6 0.2 copy.65
  37.5 72.2 %all-gather.3.cloned.1.call-done = bf16[32,1,76032]{2,1,0:T(2,128)(2,1)} async-done(((bf16[1,1,76032]{2,1,0:T(2,128)(2,1)}), bf16[32,1,76032]{2,1,0:T(2,128)(2,1)}) %all-gather.3.cloned.1.call-update) | async-done | bytes 4866064 | tf_op jit(solution)/shard_map/all_gather | solution.py:83
  109.7 4.3 copy.97
  114.0 2.5 slice.16
  116.5 8.8 %reshape.145 = bf16[4096,576]{1,0:T(8,128)(2,1)} reshape(bf16[32,73728]{1,0:T(8,128)(2,1)} %slice.16) | data formatting | bytes 9437184 | tf_op jit(solution)/shard_map/reshape | solution.py:86
  125.3 0.2 reshape.146
  125.5 5.1 fusion.70
  130.6 0.2 fusion.71
  130.8 0.6 fusion.7
  131.4 1.3 fusion.6
  132.8 0.5 fusion.30
  133.3 4.5 fusion.72
  137.8 5.9 %reshape.148 = f32[16,2,28672]{2,1,0:T(2,128)} reshape(f32[128,7168]{1,0:T(8,128)} %fusion.72) | data formatting | bytes 7340032 | tf_op jit(solution)/shard_map/reshape | solution.py:124
  143.8 4.2 copy.73
  147.9 7.8 %all_to_all.48 = f32[16,2,28672]{2,0,1:T(8,128)} all-to-all(f32[16,2,28672]{2,0,1:T(8,128)S(1)} %copy.73), channel_id=1, replica_groups=mesh['rep'=8,'epo'=16,'core'=2] {'core'}, dimensions={1} | all-to-all | bytes 7340032 | tf_op jit(solution)/shard_map/all_to_all | solution.py:125
  155.7 3.7 reduce_sum.75
  159.4 4.7 all_to_all.32
  164.1 5.4 all-to-all-start.2
  169.7 0.2 select_reduce_fusion
  169.9 0.3 convolution_convert_fusion.4
  170.2 42.1 %all-to-all-done.2 = f32[16,1,28672]{2,1,0:T(1,128)} async-done(((f32[16,1,28672]{2,1,0:T(1,128)}), f32[16,1,28672]{2,1,0:T(1,128)}, u32[]{:S(2)}, u32[]{:S(2)}) %all-to-all-start.2) | async-done | bytes 1835040 | tf_op jit(solution)/shard_map/all_to_all | solution.py:126
  212.2 2.7 reduce_sum.76
  215.0 0.2 multiply_reduce_fusion
  215.2 0.5 convolution_convert_fusion.3
  215.7 2.1 all_to_all.40
  217.8 8.2 %reduce.6 = bf16[32,14336]{1,0:T(8,128)(2,1)} reduce(bf16[32,1,14336]{2,1,0:T(2,128)(2,1)} %all_to_all.40, bf16[]{:T(256)} %broadcast.105), dimensions={1}, to_apply=%all_to_all.40.reduce_sub_computation | reduce | bytes 1835010 | tf_op jit(solution)/shard_map/all_to_all | solution.py:158
  225.9 2.9 reshape.168
  228.8 32.3 %all_to_all.49 = bf16[32,2,7168]{2,1,0:T(2,128)(2,1)} all-to-all(bf16[32,2,7168]{2,1,0:T(2,128)(2,1)S(1)} %reshape.168), channel_id=1, replica_groups=mesh['rep'=8,'epo'=16,'core'=2] {'epo','core'}, dimensions={0} | all-to-all | bytes 1835008 | tf_op jit(solution)/shard_map/all_to_all | solution.py:158
  261.1 6.1 %reshape.169 = bf16[32,1,14336]{2,1,0:T(2,128)(2,1)} reshape(bf16[32,2,7168]{2,1,0:T(2,128)(2,1)} %all_to_all.49) | data formatting | bytes 1835008
  267.2 6.6 %reduce.2 = bf16[32,14336]{1,0:T(8,128)(2,1)S(1)} reduce(bf16[32,1,14336]{2,1,0:T(2,128)(2,1)} %reshape.169, bf16[]{:T(256)} %constant.91), dimensions={1}, to_apply=%all_to_all.35.reduce_sub_computation | reduce | bytes 1835010 | tf_op jit(solution)/shard_map/all_to_all | solution.py:158
  273.8 1.3 broadcast_in_dim.34
  275.1 2.1 broadcast_in_dim.35
  277.2 89.7 %all_to_all.50 = bf16[8,64,7168]{2,1,0:T(8,128)(2,1)S(1)} all-to-all(bf16[8,64,7168]{2,1,0:T(8,128)(2,1)S(1)} %broadcast_in_dim.35), channel_id=1, replica_groups=mesh['rep'=8,'epo'=16,'core'=2] {'rep'}, dimensions={0} | all-to-all | bytes 14680064 | tf_op jit(solution)/shard_map/all_to_all | solution.py:161
  366.9 3.0 copy-done.1
  369.9 2.1 fusion.14
  371.9 15.3 %convolution_convert_fusion.2 = bf16[512,7168]{1,0:T(8,128)(2,1)} fusion(bf16[1,128,7168]{2,1,0:T(8,128)(2,1)S(1)} %copy-done, bf16[512,7168]{1,0:T(8,128)(2,1)} %bitcast.105, bf16[1,7168,128]{2,1,0:T(8,128)(2,1)} %param.28, f32[512,128]{1,0:T(8,128)S(1)} %fusion.14), kind=kOutput, calls=%fused_computation.5 | convolution fusion | flops 1883111424 | bytes 18612224 | tf_op jit(solution)/shard_map/dot_general | solution.py:163
  387.3 86.1 %all_to_all.51 = bf16[8,64,7168]{2,1,0:T(8,128)(2,1)S(1)} all-to-all(bf16[8,64,7168]{2,1,0:T(8,128)(2,1)} %bitcast.106), channel_id=1, replica_groups=mesh['rep'=8,'epo'=16,'core'=2] {'rep'}, dimensions={0} | all-to-all | bytes 14680064 | tf_op jit(solution)/shard_map/all_to_all | solution.py:164
  473.3 2.5 convert_reduce_fusion
  475.8 4.4 all_to_all.38
  480.2 8.8 %all-to-all-start.6 = ((f32[32,1,14336]{2,1,0:T(1,128)}), f32[32,1,14336]{2,1,0:T(1,128)}, u32[]{:S(2)}, u32[]{:S(2)}) async-start(f32[32,1,14336]{2,1,0:T(1,128)} %all_to_all.38), calls=%async_computation.6 | async-start | bytes 3670016 | tf_op jit(solution)/shard_map/all_to_all | solution.py:166
  489.1 0.1 reshape.154
  489.1 0.3 fusion.50
  489.4 44.1 %all-to-all-done.6 = f32[32,1,14336]{2,1,0:T(1,128)} async-done(((f32[32,1,14336]{2,1,0:T(1,128)}), f32[32,1,14336]{2,1,0:T(1,128)}, u32[]{:S(2)}, u32[]{:S(2)}) %all-to-all-start.6) | async-done | bytes 1835040 | tf_op jit(solution)/shard_map/all_to_all | solution.py:166
  533.6 7.1 %reduce.3 = f32[32,14336]{1,0:T(8,128)} reduce(f32[32,1,14336]{2,1,0:T(1,128)} %all-to-all-done.6, f32[]{:T(128)} %constant.92), dimensions={1}, to_apply=%all_to_all.39.reduce_sub_computation | reduce | bytes 3670020 | tf_op jit(solution)/shard_map/all_to_all | solution.py:166
  540.6 2.8 reshape.152
  543.5 3.1 fusion.2
  (41 shorter events, 0.5 us)
Async XLA Ops:
  6.5 365.4 %copy-start = (bf16[1,128,7168]{2,1,0:T(8,128)(2,1)S(1)}, bf16[1,128,7168]{2,1,0:T(8,128)(2,1)}, u32[]{:S(2)}) copy-start(bf16[1,128,7168]{2,1,0:T(8,128)(2,1)} %param.29) | copy-start | bytes 5505028
  7.9 27.5 %copy-start.5 = (bf16[1,2304]{1,0:T(2,128)(2,1)S(1)}, bf16[1,2304]{1,0:T(2,128)(2,1)}, u32[]{:S(2)}) copy-start(bf16[1,2304]{1,0:T(2,128)(2,1)} %param.16) | copy-start | bytes 13828
  9.8 26.7 %copy-start.3 = (bf16[1,128,1152]{2,1,0:T(8,128)(2,1)S(1)}, bf16[1,128,1152]{2,1,0:T(8,128)(2,1)}, u32[]{:S(2)}) copy-start(bf16[1,128,1152]{2,1,0:T(8,128)(2,1)} %param.15) | copy-start | bytes 884740
  12.2 20.0 %all-to-all-start = ((bf16[8,2,18432]{2,1,0:T(2,128)(2,1)}), bf16[8,2,18432]{2,1,0:T(2,128)(2,1)}, u32[]{:S(2)}, u32[]{:S(2)}) async-start(bf16[8,2,18432]{2,1,0:T(2,128)(2,1)} %reshape.166), calls=%async_computation | async-start | bytes 1179648 | tf_op jit(solution)/shard_map/all_to_all | solution.py:69
  19.7 90.0 %all-gather.3.cloned.1.call-start = ((), (), s32[]{:S(2)}) async-start(), calls=%async_computation.7 | async-start | bytes 10036224 | tf_op jit(solution)/shard_map/all_gather | solution.py:83
  125.5 5.9 %slice-start = ((s8[5242880]{0:T(1024)(128)(4,1)}), s8[4194304]{0:T(1024)(128)(4,1)S(1)}, s32[]{:S(2)}) async-start(s8[5242880]{0:T(1024)(128)(4,1)} %bitcast.109), calls=%async_computation.8 | async-start | bytes 8388608
  125.5 5.9 %slice-start.1 = ((s8[5242880]{0:T(1024)(128)(4,1)}), s8[1048576]{0:T(1024)(128)(4,1)S(1)}, s32[]{:S(2)}) async-start(s8[5242880]{0:T(1024)(128)(4,1)} %bitcast.109), calls=%async_computation.9 | async-start | bytes 2097152
  131.4 1.4 copy-start.8
  159.4 10.0 %copy-start.6 = (s32[1,4,8]{2,1,0:T(4,128)S(1)}, s32[1,4,8]{2,1,0:T(4,128)}, u32[]{:S(2)}) copy-start(s32[1,4,8]{2,1,0:T(4,128)} %param.25) | copy-start | bytes 388
  159.4 10.3 %copy-start.4 = (bf16[7168]{0:T(1024)(128)(2,1)S(1)}, bf16[7168]{0:T(1024)(128)(2,1)}, u32[]{:S(2)}) copy-start(bf16[7168]{0:T(1024)(128)(2,1)} %param.24) | copy-start | bytes 43012
  164.1 50.9 %copy-start.2 = (bf16[1,4,7168]{2,1,0:T(4,128)(2,1)S(1)}, bf16[1,4,7168]{2,1,0:T(4,128)(2,1)}, u32[]{:S(2)}) copy-start(bf16[1,4,7168]{2,1,0:T(4,128)(2,1)} %param.21) | copy-start | bytes 172036
  164.1 48.1 %all-to-all-start.2 = ((f32[16,1,28672]{2,1,0:T(1,128)}), f32[16,1,28672]{2,1,0:T(1,128)}, u32[]{:S(2)}, u32[]{:S(2)}) async-start(f32[16,1,28672]{2,1,0:T(1,128)} %all_to_all.32), calls=%async_computation.2 | async-start | bytes 3670016 | tf_op jit(solution)/shard_map/all_to_all | solution.py:126
  277.1 92.7 %copy-start.7 = (bf16[1,7168,128]{2,1,0:T(8,128)(2,1)S(1)}, bf16[1,7168,128]{2,1,0:T(8,128)(2,1)}, u32[]{:S(2)}) copy-start(bf16[1,7168,128]{2,1,0:T(8,128)(2,1)} %param.27) | copy-start | bytes 5505028
  366.9 3.0 copy-start.1
  475.8 13.2 %copy-start.9 = (bf16[1,4,8]{2,1,0:T(4,128)(2,1)S(1)}, bf16[1,4,8]{2,1,0:T(4,128)(2,1)}, u32[]{:S(2)}) copy-start(bf16[1,4,8]{2,1,0:T(4,128)(2,1)} %param.26) | copy-start | bytes 196
  480.2 53.3 %all-to-all-start.6 = ((f32[32,1,14336]{2,1,0:T(1,128)}), f32[32,1,14336]{2,1,0:T(1,128)}, u32[]{:S(2)}, u32[]{:S(2)}) async-start(f32[32,1,14336]{2,1,0:T(1,128)} %all_to_all.38), calls=%async_computation.6 | async-start | bytes 3670016 | tf_op jit(solution)/shard_map/all_to_all | solution.py:166
Sparse Core Ops, SparseCore 0:
  36.7 72.9 all-gather.2

commit v3 on v2

--- a/solution.py
+++ b/solution.py
@@ -78,53 +78,61 @@
         incoming.reshape(rep_count * per_holder, block_width),
         preferred_element_type=jnp.float32,
     ).astype(jnp.bfloat16)
-    prefix_width = own_blocks.shape[0] * block_width
-    packed = jnp.concatenate([own_blocks.reshape(1, prefix_width), suffix_latent], axis=1)
-    gathered = lax.all_gather(packed, EP, axis=0, tiled=True)
-    prefix_all = gathered[:, :prefix_width]
-    suffix_all = gathered[:, prefix_width:]
-    prefix_keys = prefix_all.reshape(-1, latent_width)
-    suffix_keys = suffix_all.reshape(-1, latent_width)
+    core_count = lax.axis_size("core")
+    outer_count = ep_count // core_count
+    pre_rows = per_device * (block_width // latent_width)
+    suf_rows = SUF // ep_count
+    pad_rows = -(pre_rows + suf_rows) % 16
+    packed = jnp.concatenate(
+        [
+            own_blocks.reshape(pre_rows, latent_width),
+            suffix_latent.reshape(suf_rows, latent_width),
+            jnp.zeros((pad_rows, latent_width), own_blocks.dtype),
+        ],
+        axis=0,
+    )
+    row_count = packed.shape[0]
+    chip_keys = lax.all_gather(packed[None], "epo", axis=0, tiled=True)
+    chip_keys = jnp.broadcast_to(chip_keys[None], (core_count,) + chip_keys.shape)
+    all_keys = lax.all_to_all(chip_keys, "core", 0, 0, tiled=True)
+    keys = all_keys.reshape(-1, latent_width)
+    core_of = lax.broadcasted_iota(jnp.int32, all_keys.shape[:3], 0)
+    outer_of = lax.broadcasted_iota(jnp.int32, all_keys.shape[:3], 1)
+    row_of = lax.broadcasted_iota(jnp.int32, all_keys.shape[:3], 2)
+    device_of = (outer_of * core_count + core_of).reshape(-1)
+    row_of = row_of.reshape(-1)
+    is_prefix = (row_of < pre_rows) & (device_of * pre_rows + row_of < prefix_len[0])
+    suffix_pos = device_of * suf_rows + row_of - pre_rows
+    is_suffix = (row_of >= pre_rows) & (row_of < pre_rows + suf_rows)
+    token_pos = jnp.arange(SUF, dtype=jnp.int32)
+    visible = is_prefix[None, :] | (is_suffix[None, :] & (suffix_pos[None, :] <= token_pos[:, None]))
     query_rows = queries[0].reshape(SUF, -1, latent_width)
-    pre_scores = (
-        jnp.einsum("thc,kc->htk", query_rows, prefix_keys, preferred_element_type=jnp.float32)
+    scores = (
+        jnp.einsum("thc,kc->htk", query_rows, keys, preferred_element_type=jnp.float32)
         * score_scale
     )
-    suf_scores = (
-        jnp.einsum("thc,kc->htk", query_rows, suffix_keys, preferred_element_type=jnp.float32)
-        * score_scale
-    )
-    key_index = jnp.arange(prefix_keys.shape[0], dtype=jnp.int32)
-    pre_scores = jnp.where(key_index[None, None, :] < prefix_len[0], pre_scores, -1e30)
-    causal = jnp.arange(SUF)[None, :] <= jnp.arange(SUF)[:, None]
-    suf_scores = jnp.where(causal[None, :, :], suf_scores, -1e30)
-    highest = jnp.maximum(jnp.max(pre_scores, axis=2), jnp.max(suf_scores, axis=2))
-    pre_exps = jnp.exp(pre_scores - highest[:, :, None])
-    suf_exps = jnp.exp(suf_scores - highest[:, :, None])
-    denominator = jnp.sum(pre_exps, axis=2) + jnp.sum(suf_exps, axis=2)
+    scores = jnp.where(visible[None, :, :], scores, -1e30)
+    highest = jnp.max(scores, axis=2)
+    exps = jnp.exp(scores - highest[:, :, None])
+    denominator = jnp.sum(exps, axis=2)
     latent = jnp.einsum(
         "htk,kc->thc",
-        pre_exps.astype(jnp.bfloat16),
-        prefix_keys[:, :KVR],
-        preferred_element_type=jnp.float32,
-    )
-    latent = latent + jnp.einsum(
-        "htk,kc->thc",
-        suf_exps.astype(jnp.bfloat16),
-        suffix_keys[:, :KVR],
+        exps.astype(jnp.bfloat16),
+        keys[:, :KVR],
         preferred_element_type=jnp.float32,
     )
     latent = (latent / jnp.transpose(denominator)[:, :, None]).astype(jnp.bfloat16)
     head_values = jnp.einsum(
         "thc,hcv->thv", latent, w_value, preferred_element_type=jnp.float32
     ).astype(jnp.bfloat16)
-    head_values = head_values.reshape(SUF, -1)
+    head_values = head_values.reshape(outer_count, core_count, suf_rows, -1)
+    head_values = jnp.transpose(head_values, (1, 0, 2, 3)).reshape(SUF, -1)
     partial = jnp.dot(head_values, w_out, preferred_element_type=jnp.float32)
-    core_count = lax.axis_size("core")
-    partial = partial.reshape(ep_count // core_count, core_count, -1)
-    partial = jnp.sum(lax.all_to_all(partial, "core", 1, 1, tiled=True), axis=1)
+    partial = partial.reshape(core_count, SUF // core_count, -1)
+    partial = jnp.sum(lax.all_to_all(partial, "core", 0, 0, tiled=True), axis=0)
+    partial = partial.reshape(outer_count, 8, -1)
     attention = jnp.sum(lax.all_to_all(partial, "epo", 0, 0, tiled=True), axis=0)
-    attention = attention.reshape(SUF // ep_count, -1)
+    attention = attention.reshape(suf_rows, -1)
     residual = hidden[0].astype(jnp.float32) + attention
     scale_rows = lax.rsqrt(jnp.mean(residual * residual, axis=1, keepdims=True) + norm_eps)
     normed = (residual * scale_rows * norm_gain.astype(jnp.float32)).astype(jnp.bfloat16)
@@ -154,7 +162,7 @@
         placing.astype(jnp.bfloat16), normed, preferred_element_type=jnp.float32
     ).astype(jnp.bfloat16)
     width = grouped.shape[1]
-    grouped = grouped.reshape(expert_count, capacity * width)
+    grouped = grouped.reshape(expert_count, 16, -1)
     mine = lax.all_to_all(grouped, EP, split_axis=0, concat_axis=0, tiled=True)
     mine = mine.reshape(slot_count, width)
     copies = jnp.broadcast_to(mine[None], (rep_count,) + mine.shape)
@@ -162,7 +170,7 @@
     units = expert_units(batch.reshape(-1, width), w_gate[0], w_up[0])
     outputs = jnp.dot(units, w_down[0], preferred_element_type=jnp.float32).astype(jnp.bfloat16)
     back = lax.all_to_all(outputs.reshape(batch.shape), "rep", split_axis=0, concat_axis=0, tiled=True)
-    slice_sum = jnp.sum(back.astype(jnp.float32), axis=0).reshape(expert_count, capacity * width)
+    slice_sum = jnp.sum(back.astype(jnp.float32), axis=0).reshape(expert_count, 8, -1)
     served = lax.all_to_all(slice_sum, EP, split_axis=0, concat_axis=0, tiled=True)
     mixture = jnp.dot(
         combine, served.reshape(slot_count, width), precision=lax.Precision.HIGHEST

time: 565 us -> 510 us (0.903); the launches traced: 554 us -> 509 us
  local copies, waits for them, and re-layouts: 61.9 us -> 28.4 us
  other arithmetic: 34.3 us -> 15.2 us
  blocking collectives: 216 us -> 230 us
    all_to_all x3 -> x0, other arithmetic: 21.8 us -> none  [the longest x2 14.7 us: local(): mine = lax.all_to_all(grouped, EP, split_axis=0, concat_axis=0, tiled=True)]
    all_to_all x1 -> x2, blocking collectives: 7.79 us -> 21.2 us  [the longest x1 13.5 us: local(): all_keys = lax.all_to_all(chip_keys, 'core', 0, 0, tiled=True)]
    reshape x5 -> x7, local copies, waits for them, and re-layouts: 19.1 us -> 7.31 us  [the longest x1 2.85 us: local(): jnp.sum(back.astype(jnp.float32), axis=0).reshape(expert_count, 8, -1)]
    all_to_all x3 -> x0, local copies, waits for them, and re-layouts: 11.2 us -> none  [the longest x1 4.67 us: local(): lax.all_to_all(partial, 'epo', 0, 0, tiled=True)]
    unnamed x33 -> x29, local copies, waits for them, and re-layouts: 20.4 us -> 9.58 us
  transfers between devices with their start and end apart: 4 -> 4, of which waited for: 4 -> 4; matrix products, arithmetic and copies ran while one was open for 0% -> 1% of each run, Pallas kernels for 0% -> 0%
where the time goes in v3:
time: 510 us; the launch traced here: 509 us
  blocking collectives  230 us (45%)
  waiting for transfers between devices  166 us (33%)
  matrix products  34 us (7%)
  local copies, waits for them, and re-layouts  28.4 us (6%)
  starting transfers between devices  20.9 us (4%)
  other arithmetic  15.2 us (3%)
  between operations  14.3 us (3%)
    all_to_all x1, blocking collectives, local(): lax.all_to_all(copies, 'rep', split_axis=0, concat_axis=0, tiled=True)  90.8 us
    all_to_all x1, blocking collectives, local(): lax.all_to_all(outputs.reshape(batch.shape), 'rep', split_axis=0, concat_...  86.1 us
    all_gather x1, waiting for transfers between devices, local(): chip_keys = lax.all_gather(packed[None], 'epo', axis=0, tiled=True)  68.3 us
    all_to_all x1, waiting for transfers between devices, local(): lax.all_to_all(slice_sum, EP, split_axis=0, concat_axis=0, tiled=True)  44.3 us
    all_to_all x1, waiting for transfers between devices, local(): lax.all_to_all(partial, 'epo', 0, 0, tiled=True)  42 us
    all_to_all x1, blocking collectives, local(): mine = lax.all_to_all(grouped, EP, split_axis=0, concat_axis=0, tiled=True)  32.4 us
    dot_general x1, matrix products, local(): jnp.dot(units, w_down[0], preferred_element_type=jnp.float32)  15.3 us
    all_to_all x1, blocking collectives, local(): all_keys = lax.all_to_all(chip_keys, 'core', 0, 0, tiled=True)  13.5 us
  transfers between devices with their start and end apart: 4, of which 4 were waited for; matrix products, arithmetic and copies ran while one was open for 1% of the time, Pallas kernels for 0%

profile of v3, /device:TPU:1, one launch (start us, length us, event | category | flops | bytes accessed | tf_op | source)
XLA Modules:
  0.0 509.3 jit_solution(7525389396893715211)
XLA Ops:
  6.6 0.9 constant_dynamic-slice_fusion
  7.5 0.1 copy.76
  7.6 0.1 fusion.68
  7.7 0.1 copy.69
  7.8 0.2 fusion.58
  8.0 1.4 fusion
  9.3 0.5 broadcast.185
  9.9 1.1 reduce.5
  10.9 1.3 reshape.268
  12.2 7.5 %all-to-all-start = ((bf16[8,2,18432]{2,1,0:T(2,128)(2,1)}), bf16[8,2,18432]{2,1,0:T(2,128)(2,1)}, u32[]{:S(2)}, u32[]{:S(2)}) async-start(bf16[8,2,18432]{2,1,0:T(2,128)(2,1)} %reshape.268), calls=%async_computation | async-start | bytes 1179648 | tf_op jit(solution)/shard_map/all_to_all | solution.py:69
  19.7 0.8 dynamic_slice.13
  20.5 0.1 copy.77
  20.6 0.1 reshape.246
  20.8 0.2 add_reduce_fusion
  21.0 11.2 %all-to-all-done = bf16[8,2,18432]{2,1,0:T(2,128)(2,1)} async-done(((bf16[8,2,18432]{2,1,0:T(2,128)(2,1)}), bf16[8,2,18432]{2,1,0:T(2,128)(2,1)}, u32[]{:S(2)}, u32[]{:S(2)}) %all-to-all-start) | async-done | bytes 589856 | tf_op jit(solution)/shard_map/all_to_all | solution.py:69
  32.2 2.3 reshape.269
  34.4 0.8 convolution_convert_fusion.1
  35.2 0.2 reshape.245
  35.4 0.8 maximum_maximum_fusion
  36.3 0.1 sub.25
  37.0 0.1 fusion.53
  37.1 0.1 reshape.257
  37.2 0.1 and.64
  37.3 0.2 copy.62
  37.5 3.9 fusion.12
  41.4 68.3 %all-gather.3.cloned.1.call-done = bf16[2304,576]{1,0:T(8,128)(2,1)} async-done(((bf16[144,576]{1,0:T(8,128)(2,1)}), bf16[2304,576]{1,0:T(8,128)(2,1)}) %all-gather.3.cloned.1.call-update) | async-done | bytes 2654224 | tf_op jit(solution)/shard_map/all_gather | solution.py:95
  109.8 2.3 broadcast_in_dim.22
  112.1 13.5 %all_to_all.40 = bf16[2,16,144,576]{3,2,1,0:T(8,128)(2,1)S(1)} all-to-all(bf16[2,16,144,576]{3,2,1,0:T(8,128)(2,1)S(1)} %broadcast_in_dim.22), channel_id=1, replica_groups=mesh['rep'=8,'epo'=16,'core'=2] {'core'}, dimensions={0} | all-to-all | bytes 10616832 | tf_op jit(solution)/shard_map/all_to_all | solution.py:97
  125.6 2.0 fusion.75
  127.6 0.5 copy-done.2
  128.1 2.2 copy-done.3
  130.3 0.6 fusion.5
  130.9 5.5 %fusion.29 = bf16[128,2,128]{2,0,1:T(8,128)(2,1)S(1)} fusion(bf16[2,512,128]{2,1,0:T(8,128)(2,1)S(1)} %copy-done.10, f32[2,128,4608]{1,2,0:T(8,128)} %copy-done.3, f32[2,128]{1,0:T(2,128)S(1)} %get-tuple-element.5, bf16[4608,576]{1,0:T(8,128)(2,1)} %bitcast.90, f32[128,2]{0,1:T(2,128)S(1)} %bitcast.96), kind=kOutput, calls=%fused_computation.31 | convolution fusion | flops 1244168192 | bytes 9766912 | tf_op jit(solution)/shard_map/thc,hcv->thv/dot_general | solution.py:125
  136.6 2.7 fusion.7
  139.3 7.7 %all_to_all.41 = f32[2,64,7168]{2,1,0:T(8,128)} all-to-all(f32[2,64,7168]{2,1,0:T(8,128)S(1)} %fusion.7), channel_id=1, replica_groups=mesh['rep'=8,'epo'=16,'core'=2] {'core'}, dimensions={0} | all-to-all | bytes 7340032 | tf_op jit(solution)/shard_map/all_to_all | solution.py:132
  147.0 3.7 reduce_sum.72
  150.7 2.7 reshape.249
  153.4 4.4 all-to-all-start.3
  157.9 0.1 reshape_squeeze.7
  158.1 0.2 select_reduce_fusion
  158.3 0.3 convolution_convert_fusion.5
  158.6 42.0 %all-to-all-done.3 = f32[16,8,3584]{2,1,0:T(8,128)} async-done(((f32[16,8,3584]{2,1,0:T(8,128)}), f32[16,8,3584]{2,1,0:T(8,128)}, u32[]{:S(2)}, u32[]{:S(2)}) %all-to-all-start.3) | async-done | bytes 1835040 | tf_op jit(solution)/shard_map/all_to_all | solution.py:134
  200.6 1.6 reduce_sum.73
  202.2 0.1 multiply_reduce_fusion
  202.4 0.1 reduce_sum.76
  202.5 0.1 reduce_sum.77
  202.6 0.5 convolution_convert_fusion.3
  203.1 1.3 reshape.251
  204.4 32.4 %all_to_all.42 = bf16[32,16,896]{2,1,0:T(8,128)(2,1)S(1)} all-to-all(bf16[32,16,896]{2,1,0:T(8,128)(2,1)} %reshape.251), channel_id=1, replica_groups=mesh['rep'=8,'epo'=16,'core'=2] {'epo','core'}, dimensions={0} | all-to-all | bytes 1835008 | tf_op jit(solution)/shard_map/all_to_all | solution.py:166
  236.8 1.3 broadcast_in_dim.25
  238.1 2.1 broadcast_in_dim.30
  240.2 90.8 %all_to_all.43 = bf16[8,64,7168]{2,1,0:T(8,128)(2,1)S(1)} all-to-all(bf16[8,64,7168]{2,1,0:T(8,128)(2,1)S(1)} %broadcast_in_dim.30), channel_id=1, replica_groups=mesh['rep'=8,'epo'=16,'core'=2] {'rep'}, dimensions={0} | all-to-all | bytes 14680064 | tf_op jit(solution)/shard_map/all_to_all | solution.py:169
  331.0 3.0 copy-done.1
  334.0 2.1 fusion.16
  336.1 15.3 %convolution_convert_fusion.2 = bf16[512,7168]{1,0:T(8,128)(2,1)} fusion(bf16[1,128,7168]{2,1,0:T(8,128)(2,1)S(1)} %copy-done, bf16[512,7168]{1,0:T(8,128)(2,1)} %bitcast.87, bf16[1,7168,128]{2,1,0:T(8,128)(2,1)} %param.28, f32[512,128]{1,0:T(8,128)S(1)} %fusion.16), kind=kOutput, calls=%fused_computation.4 | convolution fusion | flops 1883111424 | bytes 18612224 | tf_op jit(solution)/shard_map/dot_general | solution.py:171
  351.4 86.1 %all_to_all.44 = bf16[8,64,7168]{2,1,0:T(8,128)(2,1)S(1)} all-to-all(bf16[8,64,7168]{2,1,0:T(8,128)(2,1)} %bitcast.88), channel_id=1, replica_groups=mesh['rep'=8,'epo'=16,'core'=2] {'rep'}, dimensions={0} | all-to-all | bytes 14680064 | tf_op jit(solution)/shard_map/all_to_all | solution.py:172
  437.5 2.5 convert_reduce_fusion
  440.0 2.9 reshape.254
  442.8 9.0 %all-to-all-start.7 = ((f32[32,8,1792]{2,1,0:T(8,128)}), f32[32,8,1792]{2,1,0:T(8,128)}, u32[]{:S(2)}, u32[]{:S(2)}) async-start(f32[32,8,1792]{2,1,0:T(8,128)} %reshape.254), calls=%async_computation.7 | async-start | bytes 3670016 | tf_op jit(solution)/shard_map/all_to_all | solution.py:174
  451.9 0.1 reshape.258
  452.0 0.3 fusion.55
  452.2 44.3 %all-to-all-done.7 = f32[32,8,1792]{2,1,0:T(8,128)} async-done(((f32[32,8,1792]{2,1,0:T(8,128)}), f32[32,8,1792]{2,1,0:T(8,128)}, u32[]{:S(2)}, u32[]{:S(2)}) %all-to-all-start.7) | async-done | bytes 1835040 | tf_op jit(solution)/shard_map/all_to_all | solution.py:174
  496.5 2.8 reshape.255
  499.4 3.1 fusion.1
  (41 shorter events, 0.7 us)
Async XLA Ops:
  6.5 329.5 %copy-start = (bf16[1,128,7168]{2,1,0:T(8,128)(2,1)S(1)}, bf16[1,128,7168]{2,1,0:T(8,128)(2,1)}, u32[]{:S(2)}) copy-start(bf16[1,128,7168]{2,1,0:T(8,128)(2,1)} %param.29) | copy-start | bytes 5505028
  6.5 14.0 %copy-start.7 = (bf16[1,2304]{1,0:T(2,128)(2,1)S(1)}, bf16[1,2304]{1,0:T(2,128)(2,1)}, u32[]{:S(2)}) copy-start(bf16[1,2304]{1,0:T(2,128)(2,1)} %param.16) | copy-start | bytes 13828
  9.3 28.0 %copy-start.5 = (bf16[1,128,1152]{2,1,0:T(8,128)(2,1)S(1)}, bf16[1,128,1152]{2,1,0:T(8,128)(2,1)}, u32[]{:S(2)}) copy-start(bf16[1,128,1152]{2,1,0:T(8,128)(2,1)} %param.15) | copy-start | bytes 884740
  12.2 20.0 %all-to-all-start = ((bf16[8,2,18432]{2,1,0:T(2,128)(2,1)}), bf16[8,2,18432]{2,1,0:T(2,128)(2,1)}, u32[]{:S(2)}, u32[]{:S(2)}) async-start(bf16[8,2,18432]{2,1,0:T(2,128)(2,1)} %reshape.268), calls=%async_computation | async-start | bytes 1179648 | tf_op jit(solution)/shard_map/all_to_all | solution.py:69
  19.7 90.1 %all-gather.3.cloned.1.call-start = ((), (), s32[]{:S(2)}) async-start(), calls=%async_computation.8 | async-start | bytes 3133440 | tf_op jit(solution)/shard_map/all_gather | solution.py:95
  125.6 2.5 copy-start.2
  128.1 2.2 copy-start.3
  128.1 2.8 copy-start.10
  150.7 7.2 %copy-start.4 = (bf16[1,4,7168]{2,1,0:T(4,128)(2,1)S(1)}, bf16[1,4,7168]{2,1,0:T(4,128)(2,1)}, u32[]{:S(2)}) copy-start(bf16[1,4,7168]{2,1,0:T(4,128)(2,1)} %param.21) | copy-start | bytes 172036
  150.7 7.2 %copy-start.8 = (s32[1,4,8]{2,1,0:T(4,128)S(1)}, s32[1,4,8]{2,1,0:T(4,128)}, u32[]{:S(2)}) copy-start(s32[1,4,8]{2,1,0:T(4,128)} %param.25) | copy-start | bytes 388
  150.7 7.4 %copy-start.6 = (bf16[7168]{0:T(1024)(128)(2,1)S(1)}, bf16[7168]{0:T(1024)(128)(2,1)}, u32[]{:S(2)}) copy-start(bf16[7168]{0:T(1024)(128)(2,1)} %param.24) | copy-start | bytes 43012
  153.4 47.1 %all-to-all-start.3 = ((f32[16,8,3584]{2,1,0:T(8,128)}), f32[16,8,3584]{2,1,0:T(8,128)}, u32[]{:S(2)}, u32[]{:S(2)}) async-start(f32[16,8,3584]{2,1,0:T(8,128)} %reshape.249), calls=%async_computation.3 | async-start | bytes 3670016 | tf_op jit(solution)/shard_map/all_to_all | solution.py:134
  240.2 93.8 %copy-start.9 = (bf16[1,7168,128]{2,1,0:T(8,128)(2,1)S(1)}, bf16[1,7168,128]{2,1,0:T(8,128)(2,1)}, u32[]{:S(2)}) copy-start(bf16[1,7168,128]{2,1,0:T(8,128)(2,1)} %param.27) | copy-start | bytes 5505028
  331.0 3.0 copy-start.1
  440.0 11.9 %copy-start.11 = (bf16[1,4,8]{2,1,0:T(4,128)(2,1)S(1)}, bf16[1,4,8]{2,1,0:T(4,128)(2,1)}, u32[]{:S(2)}) copy-start(bf16[1,4,8]{2,1,0:T(4,128)(2,1)} %param.26) | copy-start | bytes 196
  442.8 53.7 %all-to-all-start.7 = ((f32[32,8,1792]{2,1,0:T(8,128)}), f32[32,8,1792]{2,1,0:T(8,128)}, u32[]{:S(2)}, u32[]{:S(2)}) async-start(f32[32,8,1792]{2,1,0:T(8,128)} %reshape.254), calls=%async_computation.7 | async-start | bytes 3670016 | tf_op jit(solution)/shard_map/all_to_all | solution.py:174
Sparse Core Ops, SparseCore 0:
  36.3 73.3 all-gather.2

commit v4 on v3

--- a/solution.py
+++ b/solution.py
@@ -93,6 +93,12 @@
     )
     row_count = packed.shape[0]
     chip_keys = lax.all_gather(packed[None], "epo", axis=0, tiled=True)
+    hidden_width, width = w_down.shape[1], w_down.shape[2]
+    chunk = width // rep_count
+    down_cols = w_down[0].reshape(hidden_width, rep_count, chunk)
+    down_cols = jnp.transpose(down_cols, (1, 0, 2))
+    down_cols = lax.all_to_all(down_cols, "rep", 0, 0, tiled=True)
+    chip_keys, down_cols = lax.optimization_barrier((chip_keys, down_cols))
     chip_keys = jnp.broadcast_to(chip_keys[None], (core_count,) + chip_keys.shape)
     all_keys = lax.all_to_all(chip_keys, "core", 0, 0, tiled=True)
     keys = all_keys.reshape(-1, latent_width)
@@ -168,10 +174,15 @@
     copies = jnp.broadcast_to(mine[None], (rep_count,) + mine.shape)
     batch = lax.all_to_all(copies, "rep", split_axis=0, concat_axis=0, tiled=True)
     units = expert_units(batch.reshape(-1, width), w_gate[0], w_up[0])
-    outputs = jnp.dot(units, w_down[0], preferred_element_type=jnp.float32).astype(jnp.bfloat16)
-    back = lax.all_to_all(outputs.reshape(batch.shape), "rep", split_axis=0, concat_axis=0, tiled=True)
-    slice_sum = jnp.sum(back.astype(jnp.float32), axis=0).reshape(expert_count, 8, -1)
-    served = lax.all_to_all(slice_sum, EP, split_axis=0, concat_axis=0, tiled=True)
+    hidden_width = units.shape[1]
+    unit_copies = jnp.broadcast_to(units[None], (rep_count,) + units.shape)
+    units_all = lax.all_to_all(unit_copies, "rep", 0, 0, tiled=True)
+    pieces = jnp.einsum("rnk,rkc->rnc", units_all, down_cols, preferred_element_type=jnp.float32)
+    out_cols = jnp.sum(pieces.astype(jnp.bfloat16).astype(jnp.float32), axis=0)
+    out_cols = out_cols.reshape(rep_count, slot_count, chunk)
+    back = lax.all_to_all(out_cols, "rep", 0, 0, tiled=True)
+    back = jnp.transpose(back, (1, 0, 2)).reshape(expert_count, capacity * rep_count, chunk)
+    served = lax.all_to_all(back, EP, split_axis=0, concat_axis=0, tiled=True)
     mixture = jnp.dot(
         combine, served.reshape(slot_count, width), precision=lax.Precision.HIGHEST
     )

time: 510 us -> 471 us (0.924)
  blocking collectives: 230 us -> 186 us
  waiting for transfers between devices: 166 us -> 177 us
  matrix products: 34 us -> 24.5 us
  starting transfers between devices: 20.9 us -> 27.6 us
    all_to_all x1 -> x2, blocking collectives: 86.1 us -> 41.7 us  [the longest x1 24.4 us: local(): back = lax.all_to_all(out_cols, 'rep', 0, 0, tiled=True)]
    all_to_all x1 -> x2, waiting for transfers between devices: 44.3 us -> 66.9 us  [the longest x1 44.3 us: local(): served = lax.all_to_all(back, EP, split_axis=0, concat_axis=0, tiled=True)]
    all_gather x1, waiting for transfers between devices: 68.3 us -> 56.3 us  [local(): chip_keys = lax.all_gather(packed[None], 'epo', axis=0, tiled=True)]
    dot_general x1 -> x2, matrix products: 15.3 us -> 5.77 us  [the longest x1 3.71 us: local(): jnp.einsum('rnk,rkc->rnc', units_all, down_cols, preferred_element_type=j...]
    all_to_all x1 -> x2, starting transfers between devices: 9 us -> 15.5 us  [the longest x1 11.2 us: local(): served = lax.all_to_all(back, EP, split_axis=0, concat_axis=0, tiled=True)]
  transfers between devices with their start and end apart: 4 -> 5, of which waited for: 4 -> 5; matrix products, arithmetic and copies ran while one was open for 1% -> 2% of each run, Pallas kernels for 0% -> 0%
where the time goes in v4:
time: 471 us; the launch traced here: 470 us
  blocking collectives  186 us (39%)
  waiting for transfers between devices  177 us (38%)
  local copies, waits for them, and re-layouts  28.3 us (6%)
  starting transfers between devices  27.6 us (6%)
  matrix products  24.5 us (5%)
  between operations  14.3 us (3%)
  other arithmetic  12.8 us (3%)
    all_to_all x1, blocking collectives, local(): lax.all_to_all(copies, 'rep', split_axis=0, concat_axis=0, tiled=True)  90.5 us
    all_gather x1, waiting for transfers between devices, local(): chip_keys = lax.all_gather(packed[None], 'epo', axis=0, tiled=True)  56.3 us
    all_to_all x1, waiting for transfers between devices, local(): served = lax.all_to_all(back, EP, split_axis=0, concat_axis=0, tiled=True)  44.3 us
    all_to_all x1, waiting for transfers between devices, local(): lax.all_to_all(partial, 'epo', 0, 0, tiled=True)  42.4 us
    all_to_all x1, blocking collectives, local(): mine = lax.all_to_all(grouped, EP, split_axis=0, concat_axis=0, tiled=True)  32.3 us
    all_to_all x1, blocking collectives, local(): back = lax.all_to_all(out_cols, 'rep', 0, 0, tiled=True)  24.4 us
    all_to_all x1, waiting for transfers between devices, local(): down_cols = lax.all_to_all(down_cols, 'rep', 0, 0, tiled=True)  22.6 us
    all_to_all x1, blocking collectives, local(): units_all = lax.all_to_all(unit_copies, 'rep', 0, 0, tiled=True)  17.3 us
  transfers between devices with their start and end apart: 5, of which 5 were waited for; matrix products, arithmetic and copies ran while one was open for 2% of the time, Pallas kernels for 0%

profile of v4, /device:TPU:1, one launch (start us, length us, event | category | flops | bytes accessed | tf_op | source)
XLA Modules:
  0.0 470.0 jit_solution(79788672847348190)
XLA Ops:
  6.6 0.9 constant_dynamic-slice_fusion
  7.6 0.1 fusion.59
  7.7 0.1 copy.81
  7.8 0.2 fusion.49
  8.0 1.4 fusion
  9.3 0.5 broadcast.186
  9.8 1.1 reduce.5
  10.9 1.3 reshape.269
  12.2 7.5 %all-to-all-start = ((bf16[8,2,18432]{2,1,0:T(2,128)(2,1)}), bf16[8,2,18432]{2,1,0:T(2,128)(2,1)}, u32[]{:S(2)}, u32[]{:S(2)}) async-start(bf16[8,2,18432]{2,1,0:T(2,128)(2,1)} %reshape.269), calls=%async_computation | async-start | bytes 1179648 | tf_op jit(solution)/shard_map/all_to_all | solution.py:69
  19.7 0.8 dynamic_slice.13
  20.5 0.1 copy.89
  20.6 0.1 reshape.247
  20.8 0.2 add_reduce_fusion
  21.0 11.2 %all-to-all-done = bf16[8,2,18432]{2,1,0:T(2,128)(2,1)} async-done(((bf16[8,2,18432]{2,1,0:T(2,128)(2,1)}), bf16[8,2,18432]{2,1,0:T(2,128)(2,1)}, u32[]{:S(2)}, u32[]{:S(2)}) %all-to-all-start) | async-done | bytes 589856 | tf_op jit(solution)/shard_map/all_to_all | solution.py:69
  32.2 2.3 reshape.270
  34.4 0.8 convolution_convert_fusion.1
  35.2 0.2 reshape.246
  35.4 0.8 maximum_maximum_fusion
  36.2 1.8 copy.91
  38.0 1.5 copy.99
  39.6 4.3 all-to-all-start.1
  44.0 0.1 sub.25
  44.8 0.1 reshape.258
  44.9 0.1 and.64
  45.0 0.2 copy.73
  45.2 3.9 fusion.12
  49.1 22.6 %all-to-all-done.1 = bf16[8,128,896]{2,1,0:T(8,128)(2,1)} async-done(((bf16[8,128,896]{2,1,0:T(8,128)(2,1)}), bf16[8,128,896]{2,1,0:T(8,128)(2,1)}, u32[]{:S(2)}, u32[]{:S(2)}) %all-to-all-start.1) | async-done | bytes 1835040 | tf_op jit(solution)/shard_map/all_to_all | solution.py:100
  71.7 56.3 %all-gather.3.cloned.1.call-done = bf16[2304,576]{1,0:T(8,128)(2,1)} async-done(((bf16[144,576]{1,0:T(8,128)(2,1)}), bf16[2304,576]{1,0:T(8,128)(2,1)}) %all-gather.3.cloned.1.call-update) | async-done | bytes 2654224 | tf_op jit(solution)/shard_map/all_gather | solution.py:95
  128.1 2.3 broadcast_in_dim.24
  130.4 13.5 %all_to_all.50 = bf16[2,16,144,576]{3,2,1,0:T(8,128)(2,1)S(1)} all-to-all(bf16[2,16,144,576]{3,2,1,0:T(8,128)(2,1)S(1)} %broadcast_in_dim.24), channel_id=1, replica_groups=mesh['rep'=8,'epo'=16,'core'=2] {'core'}, dimensions={0} | all-to-all | bytes 10616832 | tf_op jit(solution)/shard_map/all_to_all | solution.py:103
  143.9 2.0 fusion.65
  145.9 0.5 copy-done.1
  146.4 2.2 copy-done.2
  148.6 0.6 fusion.5
  149.2 5.5 %fusion.26 = bf16[128,2,128]{2,0,1:T(8,128)(2,1)S(1)} fusion(bf16[2,512,128]{2,1,0:T(8,128)(2,1)S(1)} %copy-done.9, f32[2,128,4608]{1,2,0:T(8,128)} %copy-done.2, f32[2,128]{1,0:T(2,128)S(1)} %get-tuple-element.9, bf16[4608,576]{1,0:T(8,128)(2,1)} %bitcast.98, f32[128,2]{0,1:T(2,128)S(1)} %bitcast.106), kind=kOutput, calls=%fused_computation.30 | convolution fusion | flops 1244168192 | bytes 9766912 | tf_op jit(solution)/shard_map/thc,hcv->thv/dot_general | solution.py:131
  154.9 2.7 fusion.7
  157.6 7.7 %all_to_all.51 = f32[2,64,7168]{2,1,0:T(8,128)} all-to-all(f32[2,64,7168]{2,1,0:T(8,128)S(1)} %fusion.7), channel_id=1, replica_groups=mesh['rep'=8,'epo'=16,'core'=2] {'core'}, dimensions={0} | all-to-all | bytes 7340032 | tf_op jit(solution)/shard_map/all_to_all | solution.py:138
  165.3 3.7 reduce_sum.72
  169.1 2.7 reshape.250
  171.8 4.6 all-to-all-start.4
  176.7 0.2 select_reduce_fusion
  176.8 0.3 convolution_convert_fusion.4
  177.1 42.4 %all-to-all-done.4 = f32[16,8,3584]{2,1,0:T(8,128)} async-done(((f32[16,8,3584]{2,1,0:T(8,128)}), f32[16,8,3584]{2,1,0:T(8,128)}, u32[]{:S(2)}, u32[]{:S(2)}) %all-to-all-start.4) | async-done | bytes 1835040 | tf_op jit(solution)/shard_map/all_to_all | solution.py:140
  219.5 1.6 reduce_sum.73
  221.2 0.1 multiply_reduce_fusion
  221.4 0.1 reduce_sum.77
  221.5 0.5 convolution_convert_fusion.2
  222.0 1.3 reshape.252
  223.4 32.3 %all_to_all.52 = bf16[32,16,896]{2,1,0:T(8,128)(2,1)S(1)} all-to-all(bf16[32,16,896]{2,1,0:T(8,128)(2,1)} %reshape.252), channel_id=1, replica_groups=mesh['rep'=8,'epo'=16,'core'=2] {'epo','core'}, dimensions={0} | all-to-all | bytes 1835008 | tf_op jit(solution)/shard_map/all_to_all | solution.py:172
  255.7 1.3 broadcast_in_dim.31
  257.0 2.1 broadcast_in_dim.32
  259.1 90.5 %all_to_all.53 = bf16[8,64,7168]{2,1,0:T(8,128)(2,1)S(1)} all-to-all(bf16[8,64,7168]{2,1,0:T(8,128)(2,1)S(1)} %broadcast_in_dim.32), channel_id=1, replica_groups=mesh['rep'=8,'epo'=16,'core'=2] {'rep'}, dimensions={0} | all-to-all | bytes 14680064 | tf_op jit(solution)/shard_map/all_to_all | solution.py:175
  349.5 2.1 fusion.15
  351.6 2.1 fusion.23
  353.7 0.1 broadcast_in_dim.33
  353.8 17.3 %all_to_all.54 = bf16[8,512,128]{2,1,0:T(8,128)(2,1)S(1)} all-to-all(bf16[8,512,128]{2,1,0:T(8,128)(2,1)S(1)} %broadcast_in_dim.33), channel_id=1, replica_groups=mesh['rep'=8,'epo'=16,'core'=2] {'rep'}, dimensions={0} | all-to-all | bytes 2097152 | tf_op jit(solution)/shard_map/all_to_all | solution.py:179
  371.1 3.7 convert_reduce_fusion
  374.8 24.4 %all_to_all.55 = f32[8,64,896]{2,1,0:T(8,128)S(1)} all-to-all(f32[8,64,896]{2,1,0:T(8,128)S(1)} %bitcast.101), channel_id=1, replica_groups=mesh['rep'=8,'epo'=16,'core'=2] {'rep'}, dimensions={0} | all-to-all | bytes 3670016 | tf_op jit(solution)/shard_map/all_to_all | solution.py:183
  399.2 2.3 copy.80
  401.5 11.2 %all-to-all-start.9 = ((f32[32,16,896]{2,1,0:T(8,128)}), f32[32,16,896]{2,1,0:T(8,128)}, u32[]{:S(2)}, u32[]{:S(2)}) async-start(f32[32,16,896]{2,1,0:T(8,128)} %bitcast.94), calls=%async_computation.9 | async-start | bytes 3670016 | tf_op jit(solution)/shard_map/all_to_all | solution.py:185
  412.8 0.3 fusion.46
  413.1 44.3 %all-to-all-done.9 = f32[32,16,896]{2,1,0:T(8,128)} async-done(((f32[32,16,896]{2,1,0:T(8,128)}), f32[32,16,896]{2,1,0:T(8,128)}, u32[]{:S(2)}, u32[]{:S(2)}) %all-to-all-start.9) | async-done | bytes 1835040 | tf_op jit(solution)/shard_map/all_to_all | solution.py:185
  457.4 2.7 reshape.256
  460.1 3.1 fusion.1
  (45 shorter events, 1.1 us)
Async XLA Ops:
  6.5 343.0 %copy-start = (bf16[1,7168,128]{2,1,0:T(8,128)(2,1)S(1)}, bf16[1,7168,128]{2,1,0:T(8,128)(2,1)}, u32[]{:S(2)}) copy-start(bf16[1,7168,128]{2,1,0:T(8,128)(2,1)} %param.27) | copy-start | bytes 5505028
  6.5 14.0 %copy-start.6 = (bf16[1,2304]{1,0:T(2,128)(2,1)S(1)}, bf16[1,2304]{1,0:T(2,128)(2,1)}, u32[]{:S(2)}) copy-start(bf16[1,2304]{1,0:T(2,128)(2,1)} %param.16) | copy-start | bytes 13828
  12.2 20.0 %all-to-all-start = ((bf16[8,2,18432]{2,1,0:T(2,128)(2,1)}), bf16[8,2,18432]{2,1,0:T(2,128)(2,1)}, u32[]{:S(2)}, u32[]{:S(2)}) async-start(bf16[8,2,18432]{2,1,0:T(2,128)(2,1)} %reshape.269), calls=%async_computation | async-start | bytes 1179648 | tf_op jit(solution)/shard_map/all_to_all | solution.py:69
  19.7 108.4 %all-gather.3.cloned.1.call-start = ((), (), s32[]{:S(2)}) async-start(), calls=%async_computation.10 | async-start | bytes 3133440 | tf_op jit(solution)/shard_map/all_gather | solution.py:95
  38.0 7.0 %copy-start.4 = (bf16[1,128,1152]{2,1,0:T(8,128)(2,1)S(1)}, bf16[1,128,1152]{2,1,0:T(8,128)(2,1)}, u32[]{:S(2)}) copy-start(bf16[1,128,1152]{2,1,0:T(8,128)(2,1)} %param.15) | copy-start | bytes 884740
  39.6 32.2 %all-to-all-start.1 = ((bf16[8,128,896]{2,1,0:T(8,128)(2,1)}), bf16[8,128,896]{2,1,0:T(8,128)(2,1)}, u32[]{:S(2)}, u32[]{:S(2)}) async-start(bf16[8,128,896]{2,1,0:T(8,128)(2,1)} %bitcast.93), calls=%async_computation.1 | async-start | bytes 3670016 | tf_op jit(solution)/shard_map/all_to_all | solution.py:100
  143.9 2.5 copy-start.1
  146.4 2.2 copy-start.2
  146.4 2.8 copy-start.9
  169.0 7.3 %copy-start.3 = (bf16[1,4,7168]{2,1,0:T(4,128)(2,1)S(1)}, bf16[1,4,7168]{2,1,0:T(4,128)(2,1)}, u32[]{:S(2)}) copy-start(bf16[1,4,7168]{2,1,0:T(4,128)(2,1)} %param.21) | copy-start | bytes 172036
  169.0 7.4 %copy-start.7 = (s32[1,4,8]{2,1,0:T(4,128)S(1)}, s32[1,4,8]{2,1,0:T(4,128)}, u32[]{:S(2)}) copy-start(s32[1,4,8]{2,1,0:T(4,128)} %param.25) | copy-start | bytes 388
  169.0 7.6 %copy-start.5 = (bf16[7168]{0:T(1024)(128)(2,1)S(1)}, bf16[7168]{0:T(1024)(128)(2,1)}, u32[]{:S(2)}) copy-start(bf16[7168]{0:T(1024)(128)(2,1)} %param.24) | copy-start | bytes 43012
  171.8 47.7 %all-to-all-start.4 = ((f32[16,8,3584]{2,1,0:T(8,128)}), f32[16,8,3584]{2,1,0:T(8,128)}, u32[]{:S(2)}, u32[]{:S(2)}) async-start(f32[16,8,3584]{2,1,0:T(8,128)} %reshape.250), calls=%async_computation.4 | async-start | bytes 3670016 | tf_op jit(solution)/shard_map/all_to_all | solution.py:140
  349.5 2.1 copy-start.8
  399.2 13.5 %copy-start.10 = (bf16[1,4,8]{2,1,0:T(4,128)(2,1)S(1)}, bf16[1,4,8]{2,1,0:T(4,128)(2,1)}, u32[]{:S(2)}) copy-start(bf16[1,4,8]{2,1,0:T(4,128)(2,1)} %param.26) | copy-start | bytes 196
  401.5 55.9 %all-to-all-start.9 = ((f32[32,16,896]{2,1,0:T(8,128)}), f32[32,16,896]{2,1,0:T(8,128)}, u32[]{:S(2)}, u32[]{:S(2)}) async-start(f32[32,16,896]{2,1,0:T(8,128)} %bitcast.94), calls=%async_computation.9 | async-start | bytes 3670016 | tf_op jit(solution)/shard_map/all_to_all | solution.py:185
Sparse Core Ops, SparseCore 0:
  36.3 91.7 all-gather.2

commit v5 on v4

--- a/solution.py
+++ b/solution.py
@@ -6,7 +6,7 @@
 KVR = 512
 ROPE = 64
 SUF = 128
-EP = ("epo", "core")
+EP = ("z", "ylo", "core")
 
 
 score_scale = 0.07216878364870323
@@ -39,7 +39,9 @@
     rep_count = lax.axis_size("rep")
     ep_count = lax.axis_size(EP)
     rep_index = lax.axis_index("rep")
-    ep_index = lax.axis_index("epo") * lax.axis_size("core") + lax.axis_index("core")
+    ep_index = (lax.axis_index("z") * lax.axis_size("ylo") + lax.axis_index("ylo")) * lax.axis_size(
+        "core"
+    ) + lax.axis_index("core")
     pool_count = cache_pool.shape[1]
     block_width = cache_pool.shape[2]
     per_device = holders.shape[1] // ep_count
@@ -92,7 +94,7 @@
         axis=0,
     )
     row_count = packed.shape[0]
-    chip_keys = lax.all_gather(packed[None], "epo", axis=0, tiled=True)
+    chip_keys = lax.all_gather(packed[None], ("z", "ylo"), axis=0, tiled=True)
     hidden_width, width = w_down.shape[1], w_down.shape[2]
     chunk = width // rep_count
     down_cols = w_down[0].reshape(hidden_width, rep_count, chunk)
@@ -131,13 +133,16 @@
     head_values = jnp.einsum(
         "thc,hcv->thv", latent, w_value, preferred_element_type=jnp.float32
     ).astype(jnp.bfloat16)
-    head_values = head_values.reshape(outer_count, core_count, suf_rows, -1)
-    head_values = jnp.transpose(head_values, (1, 0, 2, 3)).reshape(SUF, -1)
+    z_count, pair_count = lax.axis_size("z"), lax.axis_size("ylo")
+    head_values = head_values.reshape(z_count, pair_count, core_count, suf_rows, -1)
+    head_values = jnp.transpose(head_values, (2, 1, 0, 3, 4)).reshape(SUF, -1)
     partial = jnp.dot(head_values, w_out, preferred_element_type=jnp.float32)
     partial = partial.reshape(core_count, SUF // core_count, -1)
     partial = jnp.sum(lax.all_to_all(partial, "core", 0, 0, tiled=True), axis=0)
-    partial = partial.reshape(outer_count, 8, -1)
-    attention = jnp.sum(lax.all_to_all(partial, "epo", 0, 0, tiled=True), axis=0)
+    partial = partial.reshape(pair_count, SUF // core_count // pair_count, -1)
+    partial = jnp.sum(lax.all_to_all(partial, "ylo", 0, 0, tiled=True), axis=0)
+    partial = partial.reshape(z_count, 8, -1)
+    attention = jnp.sum(lax.all_to_all(partial, "z", 0, 0, tiled=True), axis=0)
     attention = attention.reshape(suf_rows, -1)
     residual = hidden[0].astype(jnp.float32) + attention
     scale_rows = lax.rsqrt(jnp.mean(residual * residual, axis=1, keepdims=True) + norm_eps)
@@ -191,7 +196,7 @@
 
 def solution(mesh):
     rep_n, ep_n = mesh.devices.shape
-    fine = Mesh(mesh.devices.reshape(rep_n, ep_n // 2, 2), ("rep", "epo", "core"))
+    fine = Mesh(mesh.devices.reshape(rep_n, ep_n // 4, 2, 2), ("rep", "z", "ylo", "core"))
     return jax.shard_map(
         local,
         mesh=fine,

time: 471 us -> 476 us (1.011)
  blocking collectives: 186 us -> 212 us
  waiting for transfers between devices: 177 us -> 158 us
    all_to_all x0 -> x1, blocking collectives: none -> 27.3 us  [local(): partial = jnp.sum(lax.all_to_all(partial, 'ylo', 0, 0, tiled=True), axis=0)]
    all_to_all x1, waiting for transfers between devices: 42.4 us -> 23.3 us  [local(): attention = jnp.sum(lax.all_to_all(partial, 'z', 0, 0, tiled=True), axis=0)]
where the time goes in v5:
time: 476 us; the launch traced here: 475 us
  blocking collectives  212 us (45%)
  waiting for transfers between devices  158 us (33%)
  local copies, waits for them, and re-layouts  26.6 us (6%)
  starting transfers between devices  26.4 us (6%)
  matrix products  24.5 us (5%)
  between operations  14.4 us (3%)
  other arithmetic  12.9 us (3%)
    all_to_all x1, blocking collectives, local(): lax.all_to_all(copies, 'rep', split_axis=0, concat_axis=0, tiled=True)  91.1 us
    all_gather x1, waiting for transfers between devices, local(): chip_keys = lax.all_gather(packed[None], ('z', 'ylo'), axis=0, tiled=True)  57 us
    all_to_all x1, waiting for transfers between devices, local(): served = lax.all_to_all(back, EP, split_axis=0, concat_axis=0, tiled=True)  44.3 us
    all_to_all x1, blocking collectives, local(): mine = lax.all_to_all(grouped, EP, split_axis=0, concat_axis=0, tiled=True)  30.1 us
    all_to_all x1, blocking collectives, local(): partial = jnp.sum(lax.all_to_all(partial, 'ylo', 0, 0, tiled=True), axis=0)  27.3 us
    all_to_all x1, blocking collectives, local(): back = lax.all_to_all(out_cols, 'rep', 0, 0, tiled=True)  24.7 us
    all_to_all x1, waiting for transfers between devices, local(): attention = jnp.sum(lax.all_to_all(partial, 'z', 0, 0, tiled=True), axis=0)  23.3 us
    all_to_all x1, waiting for transfers between devices, local(): down_cols = lax.all_to_all(down_cols, 'rep', 0, 0, tiled=True)  22.6 us
  transfers between devices with their start and end apart: 5, of which 5 were waited for; matrix products, arithmetic and copies ran while one was open for 2% of the time, Pallas kernels for 0%

profile of v5, /device:TPU:1, one launch (start us, length us, event | category | flops | bytes accessed | tf_op | source)
XLA Modules:
  0.0 474.9 jit_solution(4708662156110184293)
XLA Ops:
  6.6 0.9 constant_dynamic-slice_fusion
  7.6 0.1 fusion.59
  7.7 0.1 copy.81
  7.8 0.2 fusion.49
  8.0 1.4 fusion
  9.3 0.5 broadcast.186
  9.8 1.1 reduce.5
  10.9 1.3 reshape.273
  12.2 7.5 %all-to-all-start = ((bf16[8,2,18432]{2,1,0:T(2,128)(2,1)}), bf16[8,2,18432]{2,1,0:T(2,128)(2,1)}, u32[]{:S(2)}, u32[]{:S(2)}) async-start(bf16[8,2,18432]{2,1,0:T(2,128)(2,1)} %reshape.273), calls=%async_computation | async-start | bytes 1179648 | tf_op jit(solution)/shard_map/all_to_all | solution.py:71
  19.7 0.8 dynamic_slice.13
  20.5 0.1 copy.89
  20.6 0.1 reshape.250
  20.8 0.2 add_reduce_fusion
  21.0 11.2 %all-to-all-done = bf16[8,2,18432]{2,1,0:T(2,128)(2,1)} async-done(((bf16[8,2,18432]{2,1,0:T(2,128)(2,1)}), bf16[8,2,18432]{2,1,0:T(2,128)(2,1)}, u32[]{:S(2)}, u32[]{:S(2)}) %all-to-all-start) | async-done | bytes 589856 | tf_op jit(solution)/shard_map/all_to_all | solution.py:71
  32.2 2.3 reshape.274
  34.4 0.8 convolution_convert_fusion.1
  35.2 0.2 reshape.249
  35.4 0.8 maximum_maximum_fusion
  36.2 1.8 copy.91
  38.0 1.5 copy.99
  39.6 4.3 all-to-all-start.1
  44.8 0.1 reshape.262
  44.9 0.1 and.65
  45.0 0.2 copy.73
  45.2 3.9 fusion.12
  49.1 22.6 %all-to-all-done.1 = bf16[8,128,896]{2,1,0:T(8,128)(2,1)} async-done(((bf16[8,128,896]{2,1,0:T(8,128)(2,1)}), bf16[8,128,896]{2,1,0:T(8,128)(2,1)}, u32[]{:S(2)}, u32[]{:S(2)}) %all-to-all-start.1) | async-done | bytes 1835040 | tf_op jit(solution)/shard_map/all_to_all | solution.py:102
  71.7 57.0 %all-gather.3.cloned.1.call-done = bf16[2304,576]{1,0:T(8,128)(2,1)} async-done(((bf16[144,576]{1,0:T(8,128)(2,1)}), bf16[2304,576]{1,0:T(8,128)(2,1)}) %all-gather.3.cloned.1.call-update) | async-done | bytes 2654224 | tf_op jit(solution)/shard_map/all_gather | solution.py:97
  128.7 2.3 broadcast_in_dim.24
  131.0 13.6 %all_to_all.55 = bf16[2,16,144,576]{3,2,1,0:T(8,128)(2,1)S(1)} all-to-all(bf16[2,16,144,576]{3,2,1,0:T(8,128)(2,1)S(1)} %broadcast_in_dim.24), channel_id=1, replica_groups=mesh['rep'=8,'z'=8,'ylo'=2,'core'=2] {'core'}, dimensions={0} | all-to-all | bytes 10616832 | tf_op jit(solution)/shard_map/all_to_all | solution.py:105
  144.6 2.0 fusion.65
  146.6 0.5 copy-done.1
  147.1 2.2 copy-done.2
  149.3 0.6 fusion.5
  149.9 5.5 %fusion.26 = bf16[128,2,128]{2,0,1:T(8,128)(2,1)S(1)} fusion(bf16[2,512,128]{2,1,0:T(8,128)(2,1)S(1)} %copy-done.9, f32[2,128,4608]{1,2,0:T(8,128)} %copy-done.2, f32[2,128]{1,0:T(2,128)S(1)} %get-tuple-element.9, bf16[4608,576]{1,0:T(8,128)(2,1)} %bitcast.100, f32[128,2]{0,1:T(2,128)S(1)} %bitcast.108), kind=kOutput, calls=%fused_computation.30 | convolution fusion | flops 1244168192 | bytes 9766912 | tf_op jit(solution)/shard_map/thc,hcv->thv/dot_general | solution.py:133
  155.6 2.7 fusion.7
  158.3 7.7 %all_to_all.56 = f32[2,64,7168]{2,1,0:T(8,128)} all-to-all(f32[2,64,7168]{2,1,0:T(8,128)S(1)} %fusion.7), channel_id=1, replica_groups=mesh['rep'=8,'z'=8,'ylo'=2,'core'=2] {'core'}, dimensions={0} | all-to-all | bytes 7340032 | tf_op jit(solution)/shard_map/all_to_all | solution.py:141
  166.0 3.7 reduce_sum.81
  169.7 27.3 %all_to_all.57 = f32[2,32,7168]{2,1,0:T(8,128)} all-to-all(f32[2,32,7168]{2,1,0:T(8,128)} %bitcast.98), channel_id=1, replica_groups=mesh['rep'=8,'z'=8,'ylo'=2,'core'=2] {'ylo'}, dimensions={0} | all-to-all | bytes 3670016 | tf_op jit(solution)/shard_map/all_to_all | solution.py:143
  197.1 1.7 reduce_sum.82
  198.8 1.1 reshape.254
  199.8 3.7 all-to-all-start.5
  203.9 0.2 select_reduce_fusion
  204.0 0.3 convolution_convert_fusion.4
  204.3 23.3 %all-to-all-done.5 = f32[8,8,3584]{2,1,0:T(8,128)S(1)} async-done(((f32[8,8,3584]{2,1,0:T(8,128)}), f32[8,8,3584]{2,1,0:T(8,128)S(1)}, u32[]{:S(2)}, u32[]{:S(2)}) %all-to-all-start.5) | async-done | bytes 917536 | tf_op jit(solution)/shard_map/all_to_all | solution.py:145
  227.7 0.1 multiply_reduce_fusion
  228.0 0.1 reduce_sum.87
  228.1 0.5 convolution_convert_fusion.2
  228.6 1.3 reshape.256
  229.9 30.1 %all_to_all.58 = bf16[32,16,896]{2,1,0:T(8,128)(2,1)S(1)} all-to-all(bf16[32,16,896]{2,1,0:T(8,128)(2,1)} %reshape.256), channel_id=1, replica_groups=mesh['rep'=8,'z'=8,'ylo'=2,'core'=2] {'z','ylo','core'}, dimensions={0} | all-to-all | bytes 1835008 | tf_op jit(solution)/shard_map/all_to_all | solution.py:177
  260.0 1.3 broadcast_in_dim.31
  261.3 2.1 broadcast_in_dim.32
  263.4 91.1 %all_to_all.59 = bf16[8,64,7168]{2,1,0:T(8,128)(2,1)S(1)} all-to-all(bf16[8,64,7168]{2,1,0:T(8,128)(2,1)S(1)} %broadcast_in_dim.32), channel_id=1, replica_groups=mesh['rep'=8,'z'=8,'ylo'=2,'core'=2] {'rep'}, dimensions={0} | all-to-all | bytes 14680064 | tf_op jit(solution)/shard_map/all_to_all | solution.py:180
  354.5 2.1 fusion.15
  356.6 2.1 fusion.23
  358.6 0.1 broadcast_in_dim.33
  358.8 17.3 %all_to_all.60 = bf16[8,512,128]{2,1,0:T(8,128)(2,1)S(1)} all-to-all(bf16[8,512,128]{2,1,0:T(8,128)(2,1)S(1)} %broadcast_in_dim.33), channel_id=1, replica_groups=mesh['rep'=8,'z'=8,'ylo'=2,'core'=2] {'rep'}, dimensions={0} | all-to-all | bytes 2097152 | tf_op jit(solution)/shard_map/all_to_all | solution.py:184
  376.1 3.7 convert_reduce_fusion
  379.8 24.7 %all_to_all.61 = f32[8,64,896]{2,1,0:T(8,128)S(1)} all-to-all(f32[8,64,896]{2,1,0:T(8,128)S(1)} %bitcast.103), channel_id=1, replica_groups=mesh['rep'=8,'z'=8,'ylo'=2,'core'=2] {'rep'}, dimensions={0} | all-to-all | bytes 3670016 | tf_op jit(solution)/shard_map/all_to_all | solution.py:188
  404.5 2.3 copy.80
  406.8 10.8 %all-to-all-start.10 = ((f32[32,16,896]{2,1,0:T(8,128)}), f32[32,16,896]{2,1,0:T(8,128)}, u32[]{:S(2)}, u32[]{:S(2)}) async-start(f32[32,16,896]{2,1,0:T(8,128)} %bitcast.95), calls=%async_computation.10 | async-start | bytes 3670016 | tf_op jit(solution)/shard_map/all_to_all | solution.py:190
  417.7 0.3 fusion.46
  417.9 44.3 %all-to-all-done.10 = f32[32,16,896]{2,1,0:T(8,128)} async-done(((f32[32,16,896]{2,1,0:T(8,128)}), f32[32,16,896]{2,1,0:T(8,128)}, u32[]{:S(2)}, u32[]{:S(2)}) %all-to-all-start.10) | async-done | bytes 1835040 | tf_op jit(solution)/shard_map/all_to_all | solution.py:190
  462.3 2.7 reshape.260
  464.9 3.1 fusion.1
  (47 shorter events, 1.3 us)
Async XLA Ops:
  6.5 347.9 %copy-start = (bf16[1,7168,128]{2,1,0:T(8,128)(2,1)S(1)}, bf16[1,7168,128]{2,1,0:T(8,128)(2,1)}, u32[]{:S(2)}) copy-start(bf16[1,7168,128]{2,1,0:T(8,128)(2,1)} %param.27) | copy-start | bytes 5505028
  6.5 14.0 %copy-start.6 = (bf16[1,2304]{1,0:T(2,128)(2,1)S(1)}, bf16[1,2304]{1,0:T(2,128)(2,1)}, u32[]{:S(2)}) copy-start(bf16[1,2304]{1,0:T(2,128)(2,1)} %param.16) | copy-start | bytes 13828
  12.2 20.0 %all-to-all-start = ((bf16[8,2,18432]{2,1,0:T(2,128)(2,1)}), bf16[8,2,18432]{2,1,0:T(2,128)(2,1)}, u32[]{:S(2)}, u32[]{:S(2)}) async-start(bf16[8,2,18432]{2,1,0:T(2,128)(2,1)} %reshape.273), calls=%async_computation | async-start | bytes 1179648 | tf_op jit(solution)/shard_map/all_to_all | solution.py:71
  19.6 109.1 %all-gather.3.cloned.1.call-start = ((), (), s32[]{:S(2)}) async-start(), calls=%async_computation.11 | async-start | bytes 3133440 | tf_op jit(solution)/shard_map/all_gather | solution.py:97
  38.0 7.0 %copy-start.4 = (bf16[1,128,1152]{2,1,0:T(8,128)(2,1)S(1)}, bf16[1,128,1152]{2,1,0:T(8,128)(2,1)}, u32[]{:S(2)}) copy-start(bf16[1,128,1152]{2,1,0:T(8,128)(2,1)} %param.15) | copy-start | bytes 884740
  39.6 32.2 %all-to-all-start.1 = ((bf16[8,128,896]{2,1,0:T(8,128)(2,1)}), bf16[8,128,896]{2,1,0:T(8,128)(2,1)}, u32[]{:S(2)}, u32[]{:S(2)}) async-start(bf16[8,128,896]{2,1,0:T(8,128)(2,1)} %bitcast.94), calls=%async_computation.1 | async-start | bytes 3670016 | tf_op jit(solution)/shard_map/all_to_all | solution.py:102
  144.6 2.5 copy-start.1
  147.1 2.2 copy-start.2
  147.1 2.8 copy-start.9
  197.1 6.5 %copy-start.3 = (bf16[1,4,7168]{2,1,0:T(4,128)(2,1)S(1)}, bf16[1,4,7168]{2,1,0:T(4,128)(2,1)}, u32[]{:S(2)}) copy-start(bf16[1,4,7168]{2,1,0:T(4,128)(2,1)} %param.21) | copy-start | bytes 172036
  197.1 6.6 %copy-start.7 = (s32[1,4,8]{2,1,0:T(4,128)S(1)}, s32[1,4,8]{2,1,0:T(4,128)}, u32[]{:S(2)}) copy-start(s32[1,4,8]{2,1,0:T(4,128)} %param.25) | copy-start | bytes 388
  197.1 6.8 %copy-start.5 = (bf16[7168]{0:T(1024)(128)(2,1)S(1)}, bf16[7168]{0:T(1024)(128)(2,1)}, u32[]{:S(2)}) copy-start(bf16[7168]{0:T(1024)(128)(2,1)} %param.24) | copy-start | bytes 43012
  199.8 27.8 %all-to-all-start.5 = ((f32[8,8,3584]{2,1,0:T(8,128)}), f32[8,8,3584]{2,1,0:T(8,128)S(1)}, u32[]{:S(2)}, u32[]{:S(2)}) async-start(f32[8,8,3584]{2,1,0:T(8,128)} %reshape.254), calls=%async_computation.5 | async-start | bytes 1835008 | tf_op jit(solution)/shard_map/all_to_all | solution.py:145
  354.5 2.1 copy-start.8
  404.5 13.1 %copy-start.10 = (bf16[1,4,8]{2,1,0:T(4,128)(2,1)S(1)}, bf16[1,4,8]{2,1,0:T(4,128)(2,1)}, u32[]{:S(2)}) copy-start(bf16[1,4,8]{2,1,0:T(4,128)(2,1)} %param.26) | copy-start | bytes 196
  406.8 55.5 %all-to-all-start.10 = ((f32[32,16,896]{2,1,0:T(8,128)}), f32[32,16,896]{2,1,0:T(8,128)}, u32[]{:S(2)}, u32[]{:S(2)}) async-start(f32[32,16,896]{2,1,0:T(8,128)} %bitcast.95), calls=%async_computation.10 | async-start | bytes 3670016 | tf_op jit(solution)/shard_map/all_to_all | solution.py:190
Sparse Core Ops, SparseCore 0:
  36.3 92.3 all-gather.2

commit v6 on v4

--- a/solution.py
+++ b/solution.py
@@ -136,8 +136,10 @@
     partial = jnp.dot(head_values, w_out, preferred_element_type=jnp.float32)
     partial = partial.reshape(core_count, SUF // core_count, -1)
     partial = jnp.sum(lax.all_to_all(partial, "core", 0, 0, tiled=True), axis=0)
-    partial = partial.reshape(outer_count, 8, -1)
-    attention = jnp.sum(lax.all_to_all(partial, "epo", 0, 0, tiled=True), axis=0)
+    partial = partial.reshape(outer_count, 16, -1).astype(jnp.bfloat16)
+    attention = jnp.sum(
+        lax.all_to_all(partial, "epo", 0, 0, tiled=True).astype(jnp.float32), axis=0
+    )
     attention = attention.reshape(suf_rows, -1)
     residual = hidden[0].astype(jnp.float32) + attention
     scale_rows = lax.rsqrt(jnp.mean(residual * residual, axis=1, keepdims=True) + norm_eps)
@@ -179,12 +181,13 @@
     units_all = lax.all_to_all(unit_copies, "rep", 0, 0, tiled=True)
     pieces = jnp.einsum("rnk,rkc->rnc", units_all, down_cols, preferred_element_type=jnp.float32)
     out_cols = jnp.sum(pieces.astype(jnp.bfloat16).astype(jnp.float32), axis=0)
+    out_cols = out_cols.astype(jnp.bfloat16)
     out_cols = out_cols.reshape(rep_count, slot_count, chunk)
     back = lax.all_to_all(out_cols, "rep", 0, 0, tiled=True)
     back = jnp.transpose(back, (1, 0, 2)).reshape(expert_count, capacity * rep_count, chunk)
     served = lax.all_to_all(back, EP, split_axis=0, concat_axis=0, tiled=True)
     mixture = jnp.dot(
-        combine, served.reshape(slot_count, width), precision=lax.Precision.HIGHEST
+        combine, served.reshape(slot_count, width).astype(jnp.float32), precision=lax.Precision.HIGHEST
     )
     return (residual + mixture)[None]
 

time: 471 us -> 416 us (0.88)
  waiting for transfers between devices: 177 us -> 137 us
  blocking collectives: 186 us -> 178 us
    all_to_all x1, waiting for transfers between devices: 42.4 us -> 22.5 us  [local(): lax.all_to_all(partial, 'epo', 0, 0, tiled=True).astype(jnp.float32)]
    all_to_all x1, waiting for transfers between devices: 44.3 us -> 25 us  [local(): served = lax.all_to_all(back, EP, split_axis=0, concat_axis=0, tiled=True)]
    all_to_all x1, blocking collectives: 24.4 us -> 15.1 us  [local(): back = lax.all_to_all(out_cols, 'rep', 0, 0, tiled=True)]
where the time goes in v6:
time: 416 us; the launch traced here: 415 us
  blocking collectives  178 us (43%)
  waiting for transfers between devices  137 us (33%)
  starting transfers between devices  26 us (6%)
  local copies, waits for them, and re-layouts  25 us (6%)
  matrix products  23.6 us (6%)
  between operations  14.4 us (3%)
  other arithmetic  9.97 us (2%)
    all_to_all x1, blocking collectives, local(): lax.all_to_all(copies, 'rep', split_axis=0, concat_axis=0, tiled=True)  90.7 us
    all_gather x1, waiting for transfers between devices, local(): chip_keys = lax.all_gather(packed[None], 'epo', axis=0, tiled=True)  56.1 us
    all_to_all x1, blocking collectives, local(): mine = lax.all_to_all(grouped, EP, split_axis=0, concat_axis=0, tiled=True)  32.6 us
    all_to_all x1, waiting for transfers between devices, local(): served = lax.all_to_all(back, EP, split_axis=0, concat_axis=0, tiled=True)  25 us
    all_to_all x1, waiting for transfers between devices, local(): down_cols = lax.all_to_all(down_cols, 'rep', 0, 0, tiled=True)  22.7 us
    all_to_all x1, waiting for transfers between devices, local(): lax.all_to_all(partial, 'epo', 0, 0, tiled=True).astype(jnp.float32)  22.5 us
    all_to_all x1, blocking collectives, local(): units_all = lax.all_to_all(unit_copies, 'rep', 0, 0, tiled=True)  17.3 us
    all_to_all x1, blocking collectives, local(): back = lax.all_to_all(out_cols, 'rep', 0, 0, tiled=True)  15.1 us
  transfers between devices with their start and end apart: 5, of which 5 were waited for; matrix products, arithmetic and copies ran while one was open for 2% of the time, Pallas kernels for 0%

profile of v6, /device:TPU:1, one launch (start us, length us, event | category | flops | bytes accessed | tf_op | source)
XLA Modules:
  0.0 414.6 jit_solution(3642556181402393107)
XLA Ops:
  6.6 0.9 constant_dynamic-slice_fusion
  7.6 0.1 fusion.59
  7.7 0.1 copy.81
  7.8 0.2 fusion.49
  8.0 1.4 fusion
  9.3 0.5 broadcast.186
  9.8 1.1 reduce.6
  10.9 1.3 reshape.267
  12.2 7.5 %all-to-all-start = ((bf16[8,2,18432]{2,1,0:T(2,128)(2,1)}), bf16[8,2,18432]{2,1,0:T(2,128)(2,1)}, u32[]{:S(2)}, u32[]{:S(2)}) async-start(bf16[8,2,18432]{2,1,0:T(2,128)(2,1)} %reshape.267), calls=%async_computation | async-start | bytes 1179648 | tf_op jit(solution)/shard_map/all_to_all | solution.py:69
  19.7 0.8 dynamic_slice.13
  20.5 0.1 copy.89
  20.6 0.1 reshape.246
  20.8 0.2 add_reduce_fusion
  21.0 11.2 %all-to-all-done = bf16[8,2,18432]{2,1,0:T(2,128)(2,1)} async-done(((bf16[8,2,18432]{2,1,0:T(2,128)(2,1)}), bf16[8,2,18432]{2,1,0:T(2,128)(2,1)}, u32[]{:S(2)}, u32[]{:S(2)}) %all-to-all-start) | async-done | bytes 589856 | tf_op jit(solution)/shard_map/all_to_all | solution.py:69
  32.2 2.3 reshape.268
  34.4 0.8 convolution_convert_fusion.1
  35.2 0.2 reshape.245
  35.4 0.8 maximum_maximum_fusion
  36.2 1.9 copy.91
  38.1 1.5 copy.99
  39.6 4.3 %all-to-all-start.1 = ((bf16[8,128,896]{2,1,0:T(8,128)(2,1)}), bf16[8,128,896]{2,1,0:T(8,128)(2,1)}, u32[]{:S(2)}, u32[]{:S(2)}) async-start(bf16[8,128,896]{2,1,0:T(8,128)(2,1)} %bitcast.93), calls=%async_computation.1 | async-start | bytes 3670016 | tf_op jit(solution)/shard_map/all_to_all | solution.py:100
  44.0 0.1 sub.25
  44.8 0.1 reshape.256
  45.0 0.1 and.64
  45.1 0.2 copy.73
  45.3 3.9 fusion.12
  49.2 22.7 %all-to-all-done.1 = bf16[8,128,896]{2,1,0:T(8,128)(2,1)} async-done(((bf16[8,128,896]{2,1,0:T(8,128)(2,1)}), bf16[8,128,896]{2,1,0:T(8,128)(2,1)}, u32[]{:S(2)}, u32[]{:S(2)}) %all-to-all-start.1) | async-done | bytes 1835040 | tf_op jit(solution)/shard_map/all_to_all | solution.py:100
  71.8 56.1 %all-gather.3.cloned.1.call-done = bf16[2304,576]{1,0:T(8,128)(2,1)} async-done(((bf16[144,576]{1,0:T(8,128)(2,1)}), bf16[2304,576]{1,0:T(8,128)(2,1)}) %all-gather.3.cloned.1.call-update) | async-done | bytes 2654224 | tf_op jit(solution)/shard_map/all_gather | solution.py:95
  127.9 2.3 broadcast_in_dim.24
  130.2 14.7 %all_to_all.50 = bf16[2,16,144,576]{3,2,1,0:T(8,128)(2,1)S(1)} all-to-all(bf16[2,16,144,576]{3,2,1,0:T(8,128)(2,1)S(1)} %broadcast_in_dim.24), channel_id=1, replica_groups=mesh['rep'=8,'epo'=16,'core'=2] {'core'}, dimensions={0} | all-to-all | bytes 10616832 | tf_op jit(solution)/shard_map/all_to_all | solution.py:103
  144.9 2.0 fusion.65
  146.9 0.5 copy-done.1
  147.4 2.2 copy-done.2
  149.6 0.6 fusion.5
  150.2 5.5 %fusion.26 = bf16[128,2,128]{2,0,1:T(8,128)(2,1)S(1)} fusion(bf16[2,512,128]{2,1,0:T(8,128)(2,1)S(1)} %copy-done.9, f32[2,128,4608]{1,2,0:T(8,128)} %copy-done.2, f32[2,128]{1,0:T(2,128)S(1)} %get-tuple-element.9, bf16[4608,576]{1,0:T(8,128)(2,1)} %bitcast.96, f32[128,2]{0,1:T(2,128)S(1)} %bitcast.106), kind=kOutput, calls=%fused_computation.31 | convolution fusion | flops 1244168192 | bytes 9766912 | tf_op jit(solution)/shard_map/thc,hcv->thv/dot_general | solution.py:131
  155.9 2.7 fusion.7
  158.6 7.7 %all_to_all.51 = f32[2,64,7168]{2,1,0:T(8,128)} all-to-all(f32[2,64,7168]{2,1,0:T(8,128)S(1)} %fusion.7), channel_id=1, replica_groups=mesh['rep'=8,'epo'=16,'core'=2] {'core'}, dimensions={0} | all-to-all | bytes 7340032 | tf_op jit(solution)/shard_map/all_to_all | solution.py:138
  166.3 2.4 reduce_sum.75
  168.7 1.5 convert_element_type.99
  170.3 3.8 all-to-all-start.4
  174.4 0.2 select_reduce_fusion
  174.6 0.3 convolution_convert_fusion.4
  174.8 22.5 %all-to-all-done.4 = bf16[16,16,1792]{2,1,0:T(8,128)(2,1)S(1)} async-done(((bf16[16,16,1792]{2,1,0:T(8,128)(2,1)}), bf16[16,16,1792]{2,1,0:T(8,128)(2,1)S(1)}, u32[]{:S(2)}, u32[]{:S(2)}) %all-to-all-start.4) | async-done | bytes 917536 | tf_op jit(solution)/shard_map/all_to_all | solution.py:141
  197.3 0.1 convert_reduce_fusion.1
  197.5 0.1 multiply_reduce_fusion
  197.7 0.1 reduce_sum.80
  197.9 0.5 convolution_convert_fusion.2
  198.3 1.3 reshape.250
  199.7 32.6 %all_to_all.52 = bf16[32,16,896]{2,1,0:T(8,128)(2,1)S(1)} all-to-all(bf16[32,16,896]{2,1,0:T(8,128)(2,1)} %reshape.250), channel_id=1, replica_groups=mesh['rep'=8,'epo'=16,'core'=2] {'epo','core'}, dimensions={0} | all-to-all | bytes 1835008 | tf_op jit(solution)/shard_map/all_to_all | solution.py:174
  232.3 1.3 broadcast_in_dim.31
  233.6 2.1 broadcast_in_dim.32
  235.7 90.7 %all_to_all.53 = bf16[8,64,7168]{2,1,0:T(8,128)(2,1)S(1)} all-to-all(bf16[8,64,7168]{2,1,0:T(8,128)(2,1)S(1)} %broadcast_in_dim.32), channel_id=1, replica_groups=mesh['rep'=8,'epo'=16,'core'=2] {'rep'}, dimensions={0} | all-to-all | bytes 14680064 | tf_op jit(solution)/shard_map/all_to_all | solution.py:177
  326.4 2.1 fusion.15
  328.5 2.1 fusion.23
  330.6 0.1 broadcast_in_dim.33
  330.7 17.3 %all_to_all.54 = bf16[8,512,128]{2,1,0:T(8,128)(2,1)S(1)} all-to-all(bf16[8,512,128]{2,1,0:T(8,128)(2,1)S(1)} %broadcast_in_dim.33), channel_id=1, replica_groups=mesh['rep'=8,'epo'=16,'core'=2] {'rep'}, dimensions={0} | all-to-all | bytes 2097152 | tf_op jit(solution)/shard_map/all_to_all | solution.py:181
  348.1 3.7 convert_reduce_fusion
  351.7 15.1 %all_to_all.55 = bf16[8,64,896]{2,1,0:T(8,128)(2,1)S(1)} all-to-all(bf16[8,64,896]{2,1,0:T(8,128)(2,1)S(1)} %bitcast.101), channel_id=1, replica_groups=mesh['rep'=8,'epo'=16,'core'=2] {'rep'}, dimensions={0} | all-to-all | bytes 1835008 | tf_op jit(solution)/shard_map/all_to_all | solution.py:186
  366.9 1.4 copy.80
  368.3 10.4 %all-to-all-start.9 = ((bf16[32,16,896]{2,1,0:T(8,128)(2,1)}), bf16[32,16,896]{2,1,0:T(8,128)(2,1)S(1)}, u32[]{:S(2)}, u32[]{:S(2)}) async-start(bf16[32,16,896]{2,1,0:T(8,128)(2,1)} %bitcast.97), calls=%async_computation.9 | async-start | bytes 1835008 | tf_op jit(solution)/shard_map/all_to_all | solution.py:188
  378.8 0.3 fusion.46
  379.1 25.0 %all-to-all-done.9 = bf16[32,16,896]{2,1,0:T(8,128)(2,1)S(1)} async-done(((bf16[32,16,896]{2,1,0:T(8,128)(2,1)}), bf16[32,16,896]{2,1,0:T(8,128)(2,1)S(1)}, u32[]{:S(2)}, u32[]{:S(2)}) %all-to-all-start.9) | async-done | bytes 917536 | tf_op jit(solution)/shard_map/all_to_all | solution.py:188
  404.1 1.3 reshape.254
  405.4 2.3 fusion.1
  (45 shorter events, 1.1 us)
Async XLA Ops:
  6.5 319.9 %copy-start = (bf16[1,7168,128]{2,1,0:T(8,128)(2,1)S(1)}, bf16[1,7168,128]{2,1,0:T(8,128)(2,1)}, u32[]{:S(2)}) copy-start(bf16[1,7168,128]{2,1,0:T(8,128)(2,1)} %param.27) | copy-start | bytes 5505028
  6.5 14.0 %copy-start.6 = (bf16[1,2304]{1,0:T(2,128)(2,1)S(1)}, bf16[1,2304]{1,0:T(2,128)(2,1)}, u32[]{:S(2)}) copy-start(bf16[1,2304]{1,0:T(2,128)(2,1)} %param.16) | copy-start | bytes 13828
  12.2 20.0 %all-to-all-start = ((bf16[8,2,18432]{2,1,0:T(2,128)(2,1)}), bf16[8,2,18432]{2,1,0:T(2,128)(2,1)}, u32[]{:S(2)}, u32[]{:S(2)}) async-start(bf16[8,2,18432]{2,1,0:T(2,128)(2,1)} %reshape.267), calls=%async_computation | async-start | bytes 1179648 | tf_op jit(solution)/shard_map/all_to_all | solution.py:69
  19.7 108.2 %all-gather.3.cloned.1.call-start = ((), (), s32[]{:S(2)}) async-start(), calls=%async_computation.10 | async-start | bytes 3133440 | tf_op jit(solution)/shard_map/all_gather | solution.py:95
  36.2 8.9 %copy-start.4 = (bf16[1,128,1152]{2,1,0:T(8,128)(2,1)S(1)}, bf16[1,128,1152]{2,1,0:T(8,128)(2,1)}, u32[]{:S(2)}) copy-start(bf16[1,128,1152]{2,1,0:T(8,128)(2,1)} %param.15) | copy-start | bytes 884740
  39.6 32.2 %all-to-all-start.1 = ((bf16[8,128,896]{2,1,0:T(8,128)(2,1)}), bf16[8,128,896]{2,1,0:T(8,128)(2,1)}, u32[]{:S(2)}, u32[]{:S(2)}) async-start(bf16[8,128,896]{2,1,0:T(8,128)(2,1)} %bitcast.93), calls=%async_computation.1 | async-start | bytes 3670016 | tf_op jit(solution)/shard_map/all_to_all | solution.py:100
  144.9 2.5 copy-start.1
  147.4 2.2 copy-start.2
  147.4 2.8 copy-start.9
  166.3 7.8 %copy-start.3 = (bf16[1,4,7168]{2,1,0:T(4,128)(2,1)S(1)}, bf16[1,4,7168]{2,1,0:T(4,128)(2,1)}, u32[]{:S(2)}) copy-start(bf16[1,4,7168]{2,1,0:T(4,128)(2,1)} %param.21) | copy-start | bytes 172036
  166.3 7.8 %copy-start.7 = (s32[1,4,8]{2,1,0:T(4,128)S(1)}, s32[1,4,8]{2,1,0:T(4,128)}, u32[]{:S(2)}) copy-start(s32[1,4,8]{2,1,0:T(4,128)} %param.25) | copy-start | bytes 388
  166.3 8.1 %copy-start.5 = (bf16[7168]{0:T(1024)(128)(2,1)S(1)}, bf16[7168]{0:T(1024)(128)(2,1)}, u32[]{:S(2)}) copy-start(bf16[7168]{0:T(1024)(128)(2,1)} %param.24) | copy-start | bytes 43012
  170.3 27.1 %all-to-all-start.4 = ((bf16[16,16,1792]{2,1,0:T(8,128)(2,1)}), bf16[16,16,1792]{2,1,0:T(8,128)(2,1)S(1)}, u32[]{:S(2)}, u32[]{:S(2)}) async-start(bf16[16,16,1792]{2,1,0:T(8,128)(2,1)} %convert_element_type.99), calls=%async_computation.4 | async-start | bytes 1835008 | tf_op jit(solution)/shard_map/all_to_all | solution.py:141
  326.4 2.1 copy-start.8
  348.1 30.6 %copy-start.10 = (bf16[1,4,8]{2,1,0:T(4,128)(2,1)S(1)}, bf16[1,4,8]{2,1,0:T(4,128)(2,1)}, u32[]{:S(2)}) copy-start(bf16[1,4,8]{2,1,0:T(4,128)(2,1)} %param.26) | copy-start | bytes 196
  368.3 35.8 %all-to-all-start.9 = ((bf16[32,16,896]{2,1,0:T(8,128)(2,1)}), bf16[32,16,896]{2,1,0:T(8,128)(2,1)S(1)}, u32[]{:S(2)}, u32[]{:S(2)}) async-start(bf16[32,16,896]{2,1,0:T(8,128)(2,1)} %bitcast.97), calls=%async_computation.9 | async-start | bytes 1835008 | tf_op jit(solution)/shard_map/all_to_all | solution.py:188
Sparse Core Ops, SparseCore 0:
  36.3 91.5 all-gather.2

commit v7 on v6

--- a/solution.py
+++ b/solution.py
@@ -170,11 +170,10 @@
         placing.astype(jnp.bfloat16), normed, preferred_element_type=jnp.float32
     ).astype(jnp.bfloat16)
     width = grouped.shape[1]
-    grouped = grouped.reshape(expert_count, 16, -1)
-    mine = lax.all_to_all(grouped, EP, split_axis=0, concat_axis=0, tiled=True)
-    mine = mine.reshape(slot_count, width)
-    copies = jnp.broadcast_to(mine[None], (rep_count,) + mine.shape)
-    batch = lax.all_to_all(copies, "rep", split_axis=0, concat_axis=0, tiled=True)
+    spread = jnp.broadcast_to(grouped.reshape(1, expert_count, 16, -1), (rep_count, expert_count, 16, width * capacity // 16))
+    spread = spread.reshape(rep_count * expert_count, 16, -1)
+    batch = lax.all_to_all(spread, ("rep",) + EP, split_axis=0, concat_axis=0, tiled=True)
+    batch = batch.reshape(rep_count, slot_count, width)
     units = expert_units(batch.reshape(-1, width), w_gate[0], w_up[0])
     hidden_width = units.shape[1]
     unit_copies = jnp.broadcast_to(units[None], (rep_count,) + units.shape)

time: 416 us -> 484 us (1.16)
  blocking collectives: 178 us -> 233 us
  local copies, waits for them, and re-layouts: 25 us -> 35.4 us
    all_to_all x2 -> x1, blocking collectives: 123 us -> 177 us  [local(): lax.all_to_all(spread, ('rep',) + EP, split_axis=0, concat_axis=0, tiled=...]
    another operation x0 -> x1, local copies, waits for them, and re-layouts: none -> 11.7 us  [local(): units = expert_units(batch.reshape(-1, width), w_gate[0], w_up[0])]
where the time goes in v7:
time: 484 us; the launch traced here: 483 us
  blocking collectives  233 us (48%)
  waiting for transfers between devices  137 us (28%)
  local copies, waits for them, and re-layouts  35.4 us (7%)
  matrix products  26.8 us (6%)
  starting transfers between devices  25.7 us (5%)
  between operations  14.4 us (3%)
  other arithmetic  9.97 us (2%)
    all_to_all x1, blocking collectives, local(): lax.all_to_all(spread, ('rep',) + EP, split_axis=0, concat_axis=0, tiled=...  177 us
    all_gather x1, waiting for transfers between devices, local(): chip_keys = lax.all_gather(packed[None], 'epo', axis=0, tiled=True)  56.1 us
    all_to_all x1, waiting for transfers between devices, local(): served = lax.all_to_all(back, EP, split_axis=0, concat_axis=0, tiled=True)  25 us
    all_to_all x1, waiting for transfers between devices, local(): down_cols = lax.all_to_all(down_cols, 'rep', 0, 0, tiled=True)  22.7 us
    all_to_all x1, waiting for transfers between devices, local(): lax.all_to_all(partial, 'epo', 0, 0, tiled=True).astype(jnp.float32)  22.4 us
    all_to_all x1, blocking collectives, local(): units_all = lax.all_to_all(unit_copies, 'rep', 0, 0, tiled=True)  19.2 us
    all_to_all x1, blocking collectives, local(): back = lax.all_to_all(out_cols, 'rep', 0, 0, tiled=True)  15.3 us
    all_to_all x1, blocking collectives, local(): all_keys = lax.all_to_all(chip_keys, 'core', 0, 0, tiled=True)  14.1 us
  transfers between devices with their start and end apart: 5, of which 5 were waited for; matrix products, arithmetic and copies ran while one was open for 2% of the time, Pallas kernels for 0%

profile of v7, /device:TPU:1, one launch (start us, length us, event | category | flops | bytes accessed | tf_op | source)
XLA Modules:
  0.0 482.7 jit_solution(8995221848154498470)
XLA Ops:
  6.6 0.9 constant_dynamic-slice_fusion
  7.6 0.1 fusion.59
  7.7 0.1 copy.81
  7.8 0.2 fusion.49
  8.0 1.4 fusion
  9.3 0.5 broadcast.186
  9.8 1.1 reduce.6
  10.9 1.3 reshape.264
  12.2 7.5 %all-to-all-start = ((bf16[8,2,18432]{2,1,0:T(2,128)(2,1)}), bf16[8,2,18432]{2,1,0:T(2,128)(2,1)}, u32[]{:S(2)}, u32[]{:S(2)}) async-start(bf16[8,2,18432]{2,1,0:T(2,128)(2,1)} %reshape.264), calls=%async_computation | async-start | bytes 1179648 | tf_op jit(solution)/shard_map/all_to_all | solution.py:69
  19.7 0.8 dynamic_slice.13
  20.5 0.1 copy.89
  20.6 0.1 reshape.244
  20.8 0.2 add_reduce_fusion
  21.0 11.2 %all-to-all-done = bf16[8,2,18432]{2,1,0:T(2,128)(2,1)} async-done(((bf16[8,2,18432]{2,1,0:T(2,128)(2,1)}), bf16[8,2,18432]{2,1,0:T(2,128)(2,1)}, u32[]{:S(2)}, u32[]{:S(2)}) %all-to-all-start) | async-done | bytes 589856 | tf_op jit(solution)/shard_map/all_to_all | solution.py:69
  32.2 2.3 reshape.265
  34.4 0.8 convolution_convert_fusion.1
  35.2 0.2 reshape.243
  35.4 0.8 maximum_maximum_fusion
  36.2 1.9 copy.91
  38.1 1.5 copy.99
  39.6 4.3 all-to-all-start.1
  44.0 0.1 sub.25
  44.8 0.1 reshape.253
  45.0 0.1 and.64
  45.1 0.2 copy.73
  45.3 3.9 fusion.12
  49.2 22.7 %all-to-all-done.1 = bf16[8,128,896]{2,1,0:T(8,128)(2,1)} async-done(((bf16[8,128,896]{2,1,0:T(8,128)(2,1)}), bf16[8,128,896]{2,1,0:T(8,128)(2,1)}, u32[]{:S(2)}, u32[]{:S(2)}) %all-to-all-start.1) | async-done | bytes 1835040 | tf_op jit(solution)/shard_map/all_to_all | solution.py:100
  71.8 56.1 %all-gather.3.cloned.1.call-done = bf16[2304,576]{1,0:T(8,128)(2,1)} async-done(((bf16[144,576]{1,0:T(8,128)(2,1)}), bf16[2304,576]{1,0:T(8,128)(2,1)}) %all-gather.3.cloned.1.call-update) | async-done | bytes 2654224 | tf_op jit(solution)/shard_map/all_gather | solution.py:95
  127.9 2.3 broadcast_in_dim.24
  130.2 14.1 %all_to_all.45 = bf16[2,16,144,576]{3,2,1,0:T(8,128)(2,1)S(1)} all-to-all(bf16[2,16,144,576]{3,2,1,0:T(8,128)(2,1)S(1)} %broadcast_in_dim.24), channel_id=1, replica_groups=mesh['rep'=8,'epo'=16,'core'=2] {'core'}, dimensions={0} | all-to-all | bytes 10616832 | tf_op jit(solution)/shard_map/all_to_all | solution.py:103
  144.3 2.0 fusion.65
  146.4 0.5 copy-done.2
  146.8 2.2 copy-done.3
  149.0 0.6 fusion.5
  149.7 5.5 %fusion.26 = bf16[128,2,128]{2,0,1:T(8,128)(2,1)S(1)} fusion(bf16[2,512,128]{2,1,0:T(8,128)(2,1)S(1)} %copy-done.10, f32[2,128,4608]{1,2,0:T(8,128)} %copy-done.3, f32[2,128]{1,0:T(2,128)S(1)} %get-tuple-element.9, bf16[4608,576]{1,0:T(8,128)(2,1)} %bitcast.95, f32[128,2]{0,1:T(2,128)S(1)} %bitcast.105), kind=kOutput, calls=%fused_computation.31 | convolution fusion | flops 1244168192 | bytes 9766912 | tf_op jit(solution)/shard_map/thc,hcv->thv/dot_general | solution.py:131
  155.3 2.7 fusion.7
  158.0 7.7 %all_to_all.46 = f32[2,64,7168]{2,1,0:T(8,128)} all-to-all(f32[2,64,7168]{2,1,0:T(8,128)S(1)} %fusion.7), channel_id=1, replica_groups=mesh['rep'=8,'epo'=16,'core'=2] {'core'}, dimensions={0} | all-to-all | bytes 7340032 | tf_op jit(solution)/shard_map/all_to_all | solution.py:138
  165.7 2.4 reduce_sum.75
  168.2 1.5 convert_element_type.99
  169.7 3.8 all-to-all-start.4
  173.9 0.2 select_reduce_fusion
  174.0 0.3 convolution_convert_fusion.4
  174.3 22.4 %all-to-all-done.4 = bf16[16,16,1792]{2,1,0:T(8,128)(2,1)S(1)} async-done(((bf16[16,16,1792]{2,1,0:T(8,128)(2,1)}), bf16[16,16,1792]{2,1,0:T(8,128)(2,1)S(1)}, u32[]{:S(2)}, u32[]{:S(2)}) %all-to-all-start.4) | async-done | bytes 917536 | tf_op jit(solution)/shard_map/all_to_all | solution.py:141
  196.7 0.1 convert_reduce_fusion.1
  196.9 0.1 multiply_reduce_fusion
  197.1 0.1 reduce_sum.80
  197.2 0.5 convolution_convert_fusion.2
  197.7 1.3 broadcast_in_dim.31
  199.0 1.7 broadcast_in_dim.32
  200.8 176.9 %all_to_all.47 = bf16[256,16,896]{2,1,0:T(8,128)(2,1)} all-to-all(bf16[256,16,896]{2,1,0:T(8,128)(2,1)S(1)} %bitcast.91), channel_id=1, replica_groups=mesh['rep'=8,'epo'=16,'core'=2] {'rep','epo','core'}, dimensions={0} | all-to-all | bytes 14680064 | tf_op jit(solution)/shard_map/all_to_all | solution.py:175
  377.7 11.7 %reshape_reshape.3 = bf16[512,7168]{1,0:T(8,128)(2,1)} reshape(bf16[256,16,896]{2,1,0:T(8,128)(2,1)} %all_to_all.47) | data formatting | bytes 14680064 | tf_op jit(solution)/shard_map/reshape;reshape | solution.py:177
  389.4 5.3 %fusion.15 = f32[512,128]{1,0:T(8,128)S(1)} fusion(bf16[512,7168]{1,0:T(8,128)(2,1)} %reshape_reshape.3, bf16[1,7168,128]{2,1,0:T(8,128)(2,1)S(1)} %copy-done), kind=kOutput, calls=%fused_computation.23 | convolution fusion | flops 939524096 | bytes 9437184 | tf_op jit(solution)/shard_map/dot_general | solution.py:17
  394.7 0.4 copy-done.9
  395.1 2.1 fusion.23
  397.1 0.1 broadcast_in_dim.33
  397.3 19.2 %all_to_all.48 = bf16[8,512,128]{2,1,0:T(8,128)(2,1)S(1)} all-to-all(bf16[8,512,128]{2,1,0:T(8,128)(2,1)S(1)} %broadcast_in_dim.33), channel_id=1, replica_groups=mesh['rep'=8,'epo'=16,'core'=2] {'rep'}, dimensions={0} | all-to-all | bytes 2097152 | tf_op jit(solution)/shard_map/all_to_all | solution.py:180
  416.5 3.6 convert_reduce_fusion
  420.1 15.3 %all_to_all.49 = bf16[8,64,896]{2,1,0:T(8,128)(2,1)S(1)} all-to-all(bf16[8,64,896]{2,1,0:T(8,128)(2,1)S(1)} %bitcast.100), channel_id=1, replica_groups=mesh['rep'=8,'epo'=16,'core'=2] {'rep'}, dimensions={0} | all-to-all | bytes 1835008 | tf_op jit(solution)/shard_map/all_to_all | solution.py:185
  435.4 1.4 copy.80
  436.8 10.0 %all-to-all-start.8 = ((bf16[32,16,896]{2,1,0:T(8,128)(2,1)}), bf16[32,16,896]{2,1,0:T(8,128)(2,1)S(1)}, u32[]{:S(2)}, u32[]{:S(2)}) async-start(bf16[32,16,896]{2,1,0:T(8,128)(2,1)} %bitcast.96), calls=%async_computation.8 | async-start | bytes 1835008 | tf_op jit(solution)/shard_map/all_to_all | solution.py:187
  447.0 0.3 fusion.46
  447.2 25.0 %all-to-all-done.8 = bf16[32,16,896]{2,1,0:T(8,128)(2,1)S(1)} async-done(((bf16[32,16,896]{2,1,0:T(8,128)(2,1)}), bf16[32,16,896]{2,1,0:T(8,128)(2,1)S(1)}, u32[]{:S(2)}, u32[]{:S(2)}) %all-to-all-start.8) | async-done | bytes 917536 | tf_op jit(solution)/shard_map/all_to_all | solution.py:187
  472.3 1.3 reshape.251
  473.6 2.3 fusion.1
  (46 shorter events, 1.1 us)
Async XLA Ops:
  6.5 382.9 %copy-start = (bf16[1,7168,128]{2,1,0:T(8,128)(2,1)S(1)}, bf16[1,7168,128]{2,1,0:T(8,128)(2,1)}, u32[]{:S(2)}) copy-start(bf16[1,7168,128]{2,1,0:T(8,128)(2,1)} %param.27) | copy-start | bytes 5505028
  6.5 14.0 %copy-start.7 = (bf16[1,2304]{1,0:T(2,128)(2,1)S(1)}, bf16[1,2304]{1,0:T(2,128)(2,1)}, u32[]{:S(2)}) copy-start(bf16[1,2304]{1,0:T(2,128)(2,1)} %param.16) | copy-start | bytes 13828
  12.2 20.0 %all-to-all-start = ((bf16[8,2,18432]{2,1,0:T(2,128)(2,1)}), bf16[8,2,18432]{2,1,0:T(2,128)(2,1)}, u32[]{:S(2)}, u32[]{:S(2)}) async-start(bf16[8,2,18432]{2,1,0:T(2,128)(2,1)} %reshape.264), calls=%async_computation | async-start | bytes 1179648 | tf_op jit(solution)/shard_map/all_to_all | solution.py:69
  19.7 108.3 %all-gather.3.cloned.1.call-start = ((), (), s32[]{:S(2)}) async-start(), calls=%async_computation.9 | async-start | bytes 3133440 | tf_op jit(solution)/shard_map/all_gather | solution.py:95
  36.2 8.9 %copy-start.5 = (bf16[1,128,1152]{2,1,0:T(8,128)(2,1)S(1)}, bf16[1,128,1152]{2,1,0:T(8,128)(2,1)}, u32[]{:S(2)}) copy-start(bf16[1,128,1152]{2,1,0:T(8,128)(2,1)} %param.15) | copy-start | bytes 884740
  39.6 32.2 %all-to-all-start.1 = ((bf16[8,128,896]{2,1,0:T(8,128)(2,1)}), bf16[8,128,896]{2,1,0:T(8,128)(2,1)}, u32[]{:S(2)}, u32[]{:S(2)}) async-start(bf16[8,128,896]{2,1,0:T(8,128)(2,1)} %bitcast.92), calls=%async_computation.1 | async-start | bytes 3670016 | tf_op jit(solution)/shard_map/all_to_all | solution.py:100
  144.3 2.5 copy-start.2
  146.8 2.2 copy-start.3
  146.8 2.8 copy-start.10
  165.7 7.8 %copy-start.4 = (bf16[1,4,7168]{2,1,0:T(4,128)(2,1)S(1)}, bf16[1,4,7168]{2,1,0:T(4,128)(2,1)}, u32[]{:S(2)}) copy-start(bf16[1,4,7168]{2,1,0:T(4,128)(2,1)} %param.21) | copy-start | bytes 172036
  165.7 7.9 %copy-start.8 = (s32[1,4,8]{2,1,0:T(4,128)S(1)}, s32[1,4,8]{2,1,0:T(4,128)}, u32[]{:S(2)}) copy-start(s32[1,4,8]{2,1,0:T(4,128)} %param.25) | copy-start | bytes 388
  165.7 8.1 %copy-start.6 = (bf16[7168]{0:T(1024)(128)(2,1)S(1)}, bf16[7168]{0:T(1024)(128)(2,1)}, u32[]{:S(2)}) copy-start(bf16[7168]{0:T(1024)(128)(2,1)} %param.24) | copy-start | bytes 43012
  169.7 27.0 %all-to-all-start.4 = ((bf16[16,16,1792]{2,1,0:T(8,128)(2,1)}), bf16[16,16,1792]{2,1,0:T(8,128)(2,1)S(1)}, u32[]{:S(2)}, u32[]{:S(2)}) async-start(bf16[16,16,1792]{2,1,0:T(8,128)(2,1)} %convert_element_type.99), calls=%async_computation.4 | async-start | bytes 1835008 | tf_op jit(solution)/shard_map/all_to_all | solution.py:141
  389.4 5.3 %copy-start.1 = (bf16[512,7168]{1,0:T(8,128)(2,1)S(1)}, bf16[512,7168]{1,0:T(8,128)(2,1)}, u32[]{:S(2)}) copy-start(bf16[512,7168]{1,0:T(8,128)(2,1)} %reshape_reshape.3) | copy-start | bytes 22020100
  389.4 5.7 %copy-start.9 = (bf16[1,7168,128]{2,1,0:T(8,128)(2,1)S(1)}, bf16[1,7168,128]{2,1,0:T(8,128)(2,1)}, u32[]{:S(2)}) copy-start(bf16[1,7168,128]{2,1,0:T(8,128)(2,1)} %param.28) | copy-start | bytes 5505028
  416.5 30.4 %copy-start.11 = (bf16[1,4,8]{2,1,0:T(4,128)(2,1)S(1)}, bf16[1,4,8]{2,1,0:T(4,128)(2,1)}, u32[]{:S(2)}) copy-start(bf16[1,4,8]{2,1,0:T(4,128)(2,1)} %param.26) | copy-start | bytes 196
  436.8 35.4 %all-to-all-start.8 = ((bf16[32,16,896]{2,1,0:T(8,128)(2,1)}), bf16[32,16,896]{2,1,0:T(8,128)(2,1)S(1)}, u32[]{:S(2)}, u32[]{:S(2)}) async-start(bf16[32,16,896]{2,1,0:T(8,128)(2,1)} %bitcast.96), calls=%async_computation.8 | async-start | bytes 1835008 | tf_op jit(solution)/shard_map/all_to_all | solution.py:187
Sparse Core Ops, SparseCore 0:
  36.3 91.5 all-gather.2

commit v8 on v6

--- a/solution.py
+++ b/solution.py
@@ -92,21 +92,16 @@
         axis=0,
     )
     row_count = packed.shape[0]
-    chip_keys = lax.all_gather(packed[None], "epo", axis=0, tiled=True)
+    chip_keys = lax.all_gather(packed[None], EP, axis=0, tiled=True)
     hidden_width, width = w_down.shape[1], w_down.shape[2]
     chunk = width // rep_count
     down_cols = w_down[0].reshape(hidden_width, rep_count, chunk)
     down_cols = jnp.transpose(down_cols, (1, 0, 2))
     down_cols = lax.all_to_all(down_cols, "rep", 0, 0, tiled=True)
     chip_keys, down_cols = lax.optimization_barrier((chip_keys, down_cols))
-    chip_keys = jnp.broadcast_to(chip_keys[None], (core_count,) + chip_keys.shape)
-    all_keys = lax.all_to_all(chip_keys, "core", 0, 0, tiled=True)
-    keys = all_keys.reshape(-1, latent_width)
-    core_of = lax.broadcasted_iota(jnp.int32, all_keys.shape[:3], 0)
-    outer_of = lax.broadcasted_iota(jnp.int32, all_keys.shape[:3], 1)
-    row_of = lax.broadcasted_iota(jnp.int32, all_keys.shape[:3], 2)
-    device_of = (outer_of * core_count + core_of).reshape(-1)
-    row_of = row_of.reshape(-1)
+    keys = chip_keys.reshape(-1, latent_width)
+    device_of = lax.broadcasted_iota(jnp.int32, chip_keys.shape[:2], 0).reshape(-1)
+    row_of = lax.broadcasted_iota(jnp.int32, chip_keys.shape[:2], 1).reshape(-1)
     is_prefix = (row_of < pre_rows) & (device_of * pre_rows + row_of < prefix_len[0])
     suffix_pos = device_of * suf_rows + row_of - pre_rows
     is_suffix = (row_of >= pre_rows) & (row_of < pre_rows + suf_rows)

time: 416 us -> 392 us (0.942)
  blocking collectives: 178 us -> 162 us
  waiting for transfers between devices: 137 us -> 129 us
    all_to_all x1 -> x0, blocking collectives: 14.7 us -> none  [local(): all_keys = lax.all_to_all(chip_keys, 'core', 0, 0, tiled=True)]
    all_gather x1, waiting for transfers between devices: 56.1 us -> 49.4 us  [local(): chip_keys = lax.all_gather(packed[None], EP, axis=0, tiled=True)]
    unnamed x28 -> x26, local copies, waits for them, and re-layouts: 8.46 us -> 7.97 us
  transfers between devices with their start and end apart: 5 -> 5, of which waited for: 5 -> 5; matrix products, arithmetic and copies ran while one was open for 2% -> 3% of each run, Pallas kernels for 0% -> 0%
where the time goes in v8:
time: 392 us; the launch traced here: 391 us
  blocking collectives  162 us (41%)
  waiting for transfers between devices  129 us (33%)
  starting transfers between devices  27.7 us (7%)
  matrix products  26.3 us (7%)
  local copies, waits for them, and re-layouts  22.2 us (6%)
  between operations  14.4 us (4%)
  other arithmetic  9.83 us (3%)
    all_to_all x1, blocking collectives, local(): lax.all_to_all(copies, 'rep', split_axis=0, concat_axis=0, tiled=True)  89 us
    all_gather x1, waiting for transfers between devices, local(): chip_keys = lax.all_gather(packed[None], EP, axis=0, tiled=True)  49.4 us
    all_to_all x1, blocking collectives, local(): mine = lax.all_to_all(grouped, EP, split_axis=0, concat_axis=0, tiled=True)  32.7 us
    all_to_all x1, waiting for transfers between devices, local(): served = lax.all_to_all(back, EP, split_axis=0, concat_axis=0, tiled=True)  25 us
    all_to_all x1, waiting for transfers between devices, local(): lax.all_to_all(partial, 'epo', 0, 0, tiled=True).astype(jnp.float32)  22.4 us
    all_to_all x1, waiting for transfers between devices, local(): down_cols = lax.all_to_all(down_cols, 'rep', 0, 0, tiled=True)  20.7 us
    all_to_all x1, blocking collectives, local(): units_all = lax.all_to_all(unit_copies, 'rep', 0, 0, tiled=True)  17.3 us
    all_to_all x1, blocking collectives, local(): back = lax.all_to_all(out_cols, 'rep', 0, 0, tiled=True)  15.1 us
  transfers between devices with their start and end apart: 5, of which 5 were waited for; matrix products, arithmetic and copies ran while one was open for 3% of the time, Pallas kernels for 0%

profile of v8, /device:TPU:1, one launch (start us, length us, event | category | flops | bytes accessed | tf_op | source)
XLA Modules:
  0.0 391.1 jit_solution(17919544719584128423)
XLA Ops:
  6.6 0.9 constant_dynamic-slice_fusion
  7.5 0.1 copy.88
  7.6 0.1 fusion.59
  7.7 0.1 copy.81
  7.8 0.2 fusion.49
  8.0 1.4 fusion
  9.3 0.5 broadcast.180
  9.8 1.1 reduce.6
  10.9 1.3 reshape.256
  12.2 7.5 %all-to-all-start = ((bf16[8,2,18432]{2,1,0:T(2,128)(2,1)}), bf16[8,2,18432]{2,1,0:T(2,128)(2,1)}, u32[]{:S(2)}, u32[]{:S(2)}) async-start(bf16[8,2,18432]{2,1,0:T(2,128)(2,1)} %reshape.256), calls=%async_computation | async-start | bytes 1179648 | tf_op jit(solution)/shard_map/all_to_all | solution.py:69
  19.7 0.8 dynamic_slice.13
  20.5 0.1 copy.89
  20.6 0.1 reshape.236
  20.8 0.2 add_reduce_fusion
  21.0 11.2 %all-to-all-done = bf16[8,2,18432]{2,1,0:T(2,128)(2,1)} async-done(((bf16[8,2,18432]{2,1,0:T(2,128)(2,1)}), bf16[8,2,18432]{2,1,0:T(2,128)(2,1)}, u32[]{:S(2)}, u32[]{:S(2)}) %all-to-all-start) | async-done | bytes 589856 | tf_op jit(solution)/shard_map/all_to_all | solution.py:69
  32.2 2.3 reshape.257
  34.4 0.8 convolution_convert_fusion.1
  35.2 0.2 reshape.235
  35.4 0.8 maximum_maximum_fusion
  36.2 1.9 copy.91
  38.1 1.6 copy.99
  39.6 4.3 %all-to-all-start.1 = ((bf16[8,128,896]{2,1,0:T(8,128)(2,1)}), bf16[8,128,896]{2,1,0:T(8,128)(2,1)}, u32[]{:S(2)}, u32[]{:S(2)}) async-start(bf16[8,128,896]{2,1,0:T(8,128)(2,1)} %bitcast.93), calls=%async_computation.1 | async-start | bytes 3670016 | tf_op jit(solution)/shard_map/all_to_all | solution.py:100
  44.0 0.1 sub.25
  44.7 0.1 and.66
  44.8 0.1 and.68
  44.9 0.2 copy.73
  45.2 3.9 fusion.12
  49.0 20.7 %all-to-all-done.1 = bf16[8,128,896]{2,1,0:T(8,128)(2,1)} async-done(((bf16[8,128,896]{2,1,0:T(8,128)(2,1)}), bf16[8,128,896]{2,1,0:T(8,128)(2,1)}, u32[]{:S(2)}, u32[]{:S(2)}) %all-to-all-start.1) | async-done | bytes 1835040 | tf_op jit(solution)/shard_map/all_to_all | solution.py:100
  69.8 49.4 %all-gather.3.cloned.1.call-done = bf16[4608,576]{1,0:T(8,128)(2,1)} async-done(((bf16[144,576]{1,0:T(8,128)(2,1)}), bf16[4608,576]{1,0:T(8,128)(2,1)}) %all-gather.3.cloned.1.call-update) | async-done | bytes 5308432 | tf_op jit(solution)/shard_map/all_gather | solution.py:95
  119.2 4.7 %fusion.65 = (f32[2,128]{1,0:T(2,128)S(1)}, f32[2,128,4608]{1,2,0:T(8,128)S(1)}) fusion(bf16[4608,576,1]{1,0,2:T(8,128)(2,1)} %bitcast.104, bf16[128,2,576]{0,2,1:T(8,128)(2,1)S(1)} %bitcast.99, pred[128,4608]{0,1:T(8,128)(4,1)S(1)} %fusion.12), kind=kOutput, calls=%fused_computation.90 | convolution fusion | flops 1362493184 | bytes 10912768 | tf_op jit(solution)/shard_map/thc,kc->htk/dot_general | solution.py:112
  124.0 2.1 copy-done.1
  126.1 0.6 fusion.5
  126.7 5.5 %fusion.26 = bf16[128,2,128]{2,0,1:T(8,128)(2,1)S(1)} fusion(bf16[2,512,128]{2,1,0:T(8,128)(2,1)S(1)} %copy-done.8, f32[2,128,4608]{1,2,0:T(8,128)} %copy-done.1, f32[2,128]{1,0:T(2,128)S(1)} %get-tuple-element.9, bf16[4608,576]{1,0:T(8,128)(2,1)} %all-gather.3.cloned.1.call-done, f32[128,2]{0,1:T(2,128)S(1)} %bitcast.103), kind=kOutput, calls=%fused_computation.31 | convolution fusion | flops 1244168192 | bytes 9766912 | tf_op jit(solution)/shard_map/thc,hcv->thv/dot_general | solution.py:126
  132.4 2.7 fusion.7
  135.1 7.6 %all_to_all.45 = f32[2,64,7168]{2,1,0:T(8,128)} all-to-all(f32[2,64,7168]{2,1,0:T(8,128)S(1)} %fusion.7), channel_id=1, replica_groups=mesh['rep'=8,'epo'=16,'core'=2] {'core'}, dimensions={0} | all-to-all | bytes 7340032 | tf_op jit(solution)/shard_map/all_to_all | solution.py:133
  142.7 2.4 reduce_sum.75
  145.2 1.5 convert_element_type.99
  146.7 5.5 %all-to-all-start.3 = ((bf16[16,16,1792]{2,1,0:T(8,128)(2,1)}), bf16[16,16,1792]{2,1,0:T(8,128)(2,1)S(1)}, u32[]{:S(2)}, u32[]{:S(2)}) async-start(bf16[16,16,1792]{2,1,0:T(8,128)(2,1)} %convert_element_type.99), calls=%async_computation.3 | async-start | bytes 1835008 | tf_op jit(solution)/shard_map/all_to_all | solution.py:136
  152.5 0.2 select_reduce_fusion
  152.7 0.3 convolution_convert_fusion.4
  152.9 22.4 %all-to-all-done.3 = bf16[16,16,1792]{2,1,0:T(8,128)(2,1)S(1)} async-done(((bf16[16,16,1792]{2,1,0:T(8,128)(2,1)}), bf16[16,16,1792]{2,1,0:T(8,128)(2,1)S(1)}, u32[]{:S(2)}, u32[]{:S(2)}) %all-to-all-start.3) | async-done | bytes 917536 | tf_op jit(solution)/shard_map/all_to_all | solution.py:136
  175.4 0.1 convert_reduce_fusion.1
  175.5 0.1 multiply_reduce_fusion
  175.7 0.1 reduce_sum.79
  175.8 0.1 reduce_sum.80
  175.9 0.5 convolution_convert_fusion.2
  176.4 1.3 reshape.240
  177.7 32.7 %all_to_all.46 = bf16[32,16,896]{2,1,0:T(8,128)(2,1)S(1)} all-to-all(bf16[32,16,896]{2,1,0:T(8,128)(2,1)} %reshape.240), channel_id=1, replica_groups=mesh['rep'=8,'epo'=16,'core'=2] {'epo','core'}, dimensions={0} | all-to-all | bytes 1835008 | tf_op jit(solution)/shard_map/all_to_all | solution.py:169
  210.5 1.3 broadcast_in_dim.28
  211.8 2.1 broadcast_in_dim.29
  213.9 89.0 %all_to_all.47 = bf16[8,64,7168]{2,1,0:T(8,128)(2,1)S(1)} all-to-all(bf16[8,64,7168]{2,1,0:T(8,128)(2,1)S(1)} %broadcast_in_dim.29), channel_id=1, replica_groups=mesh['rep'=8,'epo'=16,'core'=2] {'rep'}, dimensions={0} | all-to-all | bytes 14680064 | tf_op jit(solution)/shard_map/all_to_all | solution.py:172
  302.9 2.1 fusion.15
  305.0 2.1 fusion.23
  307.1 0.1 broadcast_in_dim.30
  307.2 17.3 %all_to_all.48 = bf16[8,512,128]{2,1,0:T(8,128)(2,1)S(1)} all-to-all(bf16[8,512,128]{2,1,0:T(8,128)(2,1)S(1)} %broadcast_in_dim.30), channel_id=1, replica_groups=mesh['rep'=8,'epo'=16,'core'=2] {'rep'}, dimensions={0} | all-to-all | bytes 2097152 | tf_op jit(solution)/shard_map/all_to_all | solution.py:176
  324.6 3.7 convert_reduce_fusion
  328.2 15.1 %all_to_all.49 = bf16[8,64,896]{2,1,0:T(8,128)(2,1)S(1)} all-to-all(bf16[8,64,896]{2,1,0:T(8,128)(2,1)S(1)} %bitcast.98), channel_id=1, replica_groups=mesh['rep'=8,'epo'=16,'core'=2] {'rep'}, dimensions={0} | all-to-all | bytes 1835008 | tf_op jit(solution)/shard_map/all_to_all | solution.py:181
  343.4 1.4 copy.80
  344.8 10.4 %all-to-all-start.8 = ((bf16[32,16,896]{2,1,0:T(8,128)(2,1)}), bf16[32,16,896]{2,1,0:T(8,128)(2,1)S(1)}, u32[]{:S(2)}, u32[]{:S(2)}) async-start(bf16[32,16,896]{2,1,0:T(8,128)(2,1)} %bitcast.95), calls=%async_computation.8 | async-start | bytes 1835008 | tf_op jit(solution)/shard_map/all_to_all | solution.py:183
  355.2 0.1 reshape.246
  355.3 0.3 fusion.46
  355.6 25.0 %all-to-all-done.8 = bf16[32,16,896]{2,1,0:T(8,128)(2,1)S(1)} async-done(((bf16[32,16,896]{2,1,0:T(8,128)(2,1)}), bf16[32,16,896]{2,1,0:T(8,128)(2,1)S(1)}, u32[]{:S(2)}, u32[]{:S(2)}) %all-to-all-start.8) | async-done | bytes 917536 | tf_op jit(solution)/shard_map/all_to_all | solution.py:183
  380.6 1.3 reshape.244
  382.0 2.3 fusion.1
  (40 shorter events, 0.8 us)
Async XLA Ops:
  6.5 296.4 %copy-start = (bf16[1,7168,128]{2,1,0:T(8,128)(2,1)S(1)}, bf16[1,7168,128]{2,1,0:T(8,128)(2,1)}, u32[]{:S(2)}) copy-start(bf16[1,7168,128]{2,1,0:T(8,128)(2,1)} %param.27) | copy-start | bytes 5505028
  6.5 14.0 %copy-start.5 = (bf16[1,2304]{1,0:T(2,128)(2,1)S(1)}, bf16[1,2304]{1,0:T(2,128)(2,1)}, u32[]{:S(2)}) copy-start(bf16[1,2304]{1,0:T(2,128)(2,1)} %param.16) | copy-start | bytes 13828
  12.2 20.0 %all-to-all-start = ((bf16[8,2,18432]{2,1,0:T(2,128)(2,1)}), bf16[8,2,18432]{2,1,0:T(2,128)(2,1)}, u32[]{:S(2)}, u32[]{:S(2)}) async-start(bf16[8,2,18432]{2,1,0:T(2,128)(2,1)} %reshape.256), calls=%async_computation | async-start | bytes 1179648 | tf_op jit(solution)/shard_map/all_to_all | solution.py:69
  19.7 99.5 %all-gather.3.cloned.1.call-start = ((), (), s32[]{:S(2)}) async-start(), calls=%async_computation.9 | async-start | bytes 6082560 | tf_op jit(solution)/shard_map/all_gather | solution.py:95
  36.2 8.8 %copy-start.3 = (bf16[1,128,1152]{2,1,0:T(8,128)(2,1)S(1)}, bf16[1,128,1152]{2,1,0:T(8,128)(2,1)}, u32[]{:S(2)}) copy-start(bf16[1,128,1152]{2,1,0:T(8,128)(2,1)} %param.15) | copy-start | bytes 884740
  39.6 30.2 %all-to-all-start.1 = ((bf16[8,128,896]{2,1,0:T(8,128)(2,1)}), bf16[8,128,896]{2,1,0:T(8,128)(2,1)}, u32[]{:S(2)}, u32[]{:S(2)}) async-start(bf16[8,128,896]{2,1,0:T(8,128)(2,1)} %bitcast.93), calls=%async_computation.1 | async-start | bytes 3670016 | tf_op jit(solution)/shard_map/all_to_all | solution.py:100
  123.9 2.2 copy-start.1
  123.9 2.8 copy-start.8
  142.7 9.4 %copy-start.2 = (bf16[1,4,7168]{2,1,0:T(4,128)(2,1)S(1)}, bf16[1,4,7168]{2,1,0:T(4,128)(2,1)}, u32[]{:S(2)}) copy-start(bf16[1,4,7168]{2,1,0:T(4,128)(2,1)} %param.21) | copy-start | bytes 172036
  142.7 9.5 %copy-start.6 = (s32[1,4,8]{2,1,0:T(4,128)S(1)}, s32[1,4,8]{2,1,0:T(4,128)}, u32[]{:S(2)}) copy-start(s32[1,4,8]{2,1,0:T(4,128)} %param.25) | copy-start | bytes 388
  142.7 9.7 %copy-start.4 = (bf16[7168]{0:T(1024)(128)(2,1)S(1)}, bf16[7168]{0:T(1024)(128)(2,1)}, u32[]{:S(2)}) copy-start(bf16[7168]{0:T(1024)(128)(2,1)} %param.24) | copy-start | bytes 43012
  146.7 28.7 %all-to-all-start.3 = ((bf16[16,16,1792]{2,1,0:T(8,128)(2,1)}), bf16[16,16,1792]{2,1,0:T(8,128)(2,1)S(1)}, u32[]{:S(2)}, u32[]{:S(2)}) async-start(bf16[16,16,1792]{2,1,0:T(8,128)(2,1)} %convert_element_type.99), calls=%async_computation.3 | async-start | bytes 1835008 | tf_op jit(solution)/shard_map/all_to_all | solution.py:136
  302.9 2.1 copy-start.7
  324.6 30.7 %copy-start.9 = (bf16[1,4,8]{2,1,0:T(4,128)(2,1)S(1)}, bf16[1,4,8]{2,1,0:T(4,128)(2,1)}, u32[]{:S(2)}) copy-start(bf16[1,4,8]{2,1,0:T(4,128)(2,1)} %param.26) | copy-start | bytes 196
  344.8 35.8 %all-to-all-start.8 = ((bf16[32,16,896]{2,1,0:T(8,128)(2,1)}), bf16[32,16,896]{2,1,0:T(8,128)(2,1)S(1)}, u32[]{:S(2)}, u32[]{:S(2)}) async-start(bf16[32,16,896]{2,1,0:T(8,128)(2,1)} %bitcast.95), calls=%async_computation.8 | async-start | bytes 1835008 | tf_op jit(solution)/shard_map/all_to_all | solution.py:183
Sparse Core Ops, SparseCore 0:
  36.3 82.8 all-gather.2

commit v9 on v8

--- a/solution.py
+++ b/solution.py
@@ -98,7 +98,11 @@
     down_cols = w_down[0].reshape(hidden_width, rep_count, chunk)
     down_cols = jnp.transpose(down_cols, (1, 0, 2))
     down_cols = lax.all_to_all(down_cols, "rep", 0, 0, tiled=True)
-    chip_keys, down_cols = lax.optimization_barrier((chip_keys, down_cols))
+    gate_rows = lax.all_to_all(w_gate[0].reshape(rep_count, chunk, hidden_width), "rep", 0, 0, tiled=True)
+    up_rows = lax.all_to_all(w_up[0].reshape(rep_count, chunk, hidden_width), "rep", 0, 0, tiled=True)
+    chip_keys, down_cols, gate_rows, up_rows = lax.optimization_barrier(
+        (chip_keys, down_cols, gate_rows, up_rows)
+    )
     keys = chip_keys.reshape(-1, latent_width)
     device_of = lax.broadcasted_iota(jnp.int32, chip_keys.shape[:2], 0).reshape(-1)
     row_of = lax.broadcasted_iota(jnp.int32, chip_keys.shape[:2], 1).reshape(-1)
@@ -167,10 +171,16 @@
     width = grouped.shape[1]
     grouped = grouped.reshape(expert_count, 16, -1)
     mine = lax.all_to_all(grouped, EP, split_axis=0, concat_axis=0, tiled=True)
-    mine = mine.reshape(slot_count, width)
-    copies = jnp.broadcast_to(mine[None], (rep_count,) + mine.shape)
-    batch = lax.all_to_all(copies, "rep", split_axis=0, concat_axis=0, tiled=True)
-    units = expert_units(batch.reshape(-1, width), w_gate[0], w_up[0])
+    mine = mine.reshape(slot_count, rep_count, chunk)
+    mine = jnp.transpose(mine, (1, 0, 2))
+    columns = lax.all_to_all(mine, "rep", 0, 0, tiled=True).reshape(-1, chunk)
+    gate_part = jnp.einsum("nd,rdk->rnk", columns, gate_rows, preferred_element_type=jnp.float32)
+    up_part = jnp.einsum("nd,rdk->rnk", columns, up_rows, preferred_element_type=jnp.float32)
+    parts = jnp.concatenate([gate_part, up_part], axis=2).astype(jnp.bfloat16)
+    parts = lax.all_to_all(parts, "rep", 0, 0, tiled=True)
+    sums = jnp.sum(parts.astype(jnp.float32), axis=0)
+    gate_sum, up_sum = sums[:, :hidden_width], sums[:, hidden_width:]
+    units = (jax.nn.silu(gate_sum) * up_sum).astype(jnp.bfloat16)
     hidden_width = units.shape[1]
     unit_copies = jnp.broadcast_to(units[None], (rep_count,) + units.shape)
     units_all = lax.all_to_all(unit_copies, "rep", 0, 0, tiled=True)

time: 392 us -> 372 us (0.949)
  blocking collectives: 162 us -> 119 us
  starting transfers between devices: 27.7 us -> 42.3 us
  waiting for transfers between devices: 129 us -> 140 us
    all_to_all x0 -> x2, waiting for transfers between devices: none -> 48.7 us  [the longest x1 25.6 us: local(): lax.all_to_all(w_gate[0].reshape(rep_count, chunk, hidden_width), 'rep',...]
    all_gather x1, waiting for transfers between devices: 49.4 us -> 9.68 us  [local(): chip_keys = lax.all_gather(packed[None], EP, axis=0, tiled=True)]
    all_to_all x1 -> x2, blocking collectives: 89 us -> 49.4 us  [the longest x1 28.6 us: local(): parts = lax.all_to_all(parts, 'rep', 0, 0, tiled=True)]
    all_to_all x0 -> x2, starting transfers between devices: none -> 11.5 us  [the longest x1 6.83 us: local(): lax.all_to_all(w_gate[0].reshape(rep_count, chunk, hidden_width), 'rep',...]
    another operation x0 -> x2, local copies, waits for them, and re-layouts: none -> 5.36 us  [the longest x1 2.7 us: local(): w_up[0].reshape(rep_count, chunk, hidden_width)]
    unnamed x26 -> x34, local copies, waits for them, and re-layouts: 7.97 us -> 6.26 us
  transfers between devices with their start and end apart: 5 -> 7, of which waited for: 5 -> 7; matrix products, arithmetic and copies ran while one was open for 3% -> 4% of each run, Pallas kernels for 0% -> 0%
where the time goes in v9:
time: 372 us; the launch traced here: 371 us
  waiting for transfers between devices  140 us (38%)
  blocking collectives  119 us (32%)
  starting transfers between devices  42.3 us (11%)
  matrix products  24 us (6%)
  local copies, waits for them, and re-layouts  20.8 us (6%)
  between operations  14.5 us (4%)
  other arithmetic  10.3 us (3%)
    all_to_all x1, blocking collectives, local(): mine = lax.all_to_all(grouped, EP, split_axis=0, concat_axis=0, tiled=True)  31.8 us
    all_to_all x1, blocking collectives, local(): parts = lax.all_to_all(parts, 'rep', 0, 0, tiled=True)  28.6 us
    all_to_all x1, waiting for transfers between devices, local(): lax.all_to_all(w_gate[0].reshape(rep_count, chunk, hidden_width), 'rep',...  25.6 us
    all_to_all x1, waiting for transfers between devices, local(): served = lax.all_to_all(back, EP, split_axis=0, concat_axis=0, tiled=True)  25 us
    all_to_all x1, waiting for transfers between devices, local(): down_cols = lax.all_to_all(down_cols, 'rep', 0, 0, tiled=True)  23.2 us
    all_to_all x1, waiting for transfers between devices, local(): lax.all_to_all(w_up[0].reshape(rep_count, chunk, hidden_width), 'rep', 0,...  23 us
    all_to_all x1, waiting for transfers between devices, local(): lax.all_to_all(partial, 'epo', 0, 0, tiled=True).astype(jnp.float32)  22.4 us
    all_to_all x1, blocking collectives, local(): columns = lax.all_to_all(mine, 'rep', 0, 0, tiled=True).reshape(-1, chunk)  20.8 us
  transfers between devices with their start and end apart: 7, of which 7 were waited for; matrix products, arithmetic and copies ran while one was open for 4% of the time, Pallas kernels for 0%

profile of v9, /device:TPU:1, one launch (start us, length us, event | category | flops | bytes accessed | tf_op | source)
XLA Modules:
  0.0 370.6 jit_solution(10448583940322703208)
XLA Ops:
  6.6 0.8 constant_dynamic-slice_fusion
  7.6 0.1 copy.106
  7.7 0.2 fusion.42
  7.9 0.3 fusion
  8.2 0.5 broadcast.180
  8.7 1.1 reduce.6
  9.8 1.2 reshape.260
  11.0 7.5 %all-to-all-start = ((bf16[8,2,18432]{2,1,0:T(2,128)(2,1)}), bf16[8,2,18432]{2,1,0:T(2,128)(2,1)S(1)}, u32[]{:S(2)}, u32[]{:S(2)}) async-start(bf16[8,2,18432]{2,1,0:T(2,128)(2,1)} %reshape.260), calls=%async_computation | async-start | bytes 1179648 | tf_op jit(solution)/shard_map/all_to_all | solution.py:69
  18.6 0.8 dynamic_slice.13
  19.7 0.2 add_reduce_fusion
  19.8 11.1 %all-to-all-done = bf16[8,2,18432]{2,1,0:T(2,128)(2,1)S(1)} async-done(((bf16[8,2,18432]{2,1,0:T(2,128)(2,1)}), bf16[8,2,18432]{2,1,0:T(2,128)(2,1)S(1)}, u32[]{:S(2)}, u32[]{:S(2)}) %all-to-all-start) | async-done | bytes 589856 | tf_op jit(solution)/shard_map/all_to_all | solution.py:69
  30.9 0.6 reshape.261
  31.5 0.8 convolution_convert_fusion.1
  32.3 0.2 reshape.237
  32.5 0.8 maximum_maximum_fusion
  33.2 1.8 copy.116
  35.1 1.6 copy.125
  36.7 4.3 %all-to-all-start.1 = ((bf16[8,128,896]{2,1,0:T(8,128)(2,1)}), bf16[8,128,896]{2,1,0:T(8,128)(2,1)}, u32[]{:S(2)}, u32[]{:S(2)}) async-start(bf16[8,128,896]{2,1,0:T(8,128)(2,1)} %bitcast.92), calls=%async_computation.1 | async-start | bytes 3670016 | tf_op jit(solution)/shard_map/all_to_all | solution.py:100
  41.0 2.7 copy.93
  43.7 23.2 %all-to-all-done.1 = bf16[8,128,896]{2,1,0:T(8,128)(2,1)} async-done(((bf16[8,128,896]{2,1,0:T(8,128)(2,1)}), bf16[8,128,896]{2,1,0:T(8,128)(2,1)}, u32[]{:S(2)}, u32[]{:S(2)}) %all-to-all-start.1) | async-done | bytes 1835040 | tf_op jit(solution)/shard_map/all_to_all | solution.py:100
  66.8 6.8 %all-to-all-start.2 = ((bf16[8,896,128]{1,2,0:T(8,128)(2,1)}), bf16[8,896,128]{1,2,0:T(8,128)(2,1)}, u32[]{:S(2)}, u32[]{:S(2)}) async-start(bf16[8,896,128]{1,2,0:T(8,128)(2,1)} %copy.93), calls=%async_computation.2 | async-start | bytes 3670016 | tf_op jit(solution)/shard_map/all_to_all | solution.py:101
  73.7 2.7 copy.94
  76.4 25.6 %all-to-all-done.2 = bf16[8,896,128]{1,2,0:T(8,128)(2,1)} async-done(((bf16[8,896,128]{1,2,0:T(8,128)(2,1)}), bf16[8,896,128]{1,2,0:T(8,128)(2,1)}, u32[]{:S(2)}, u32[]{:S(2)}) %all-to-all-start.2) | async-done | bytes 1835040 | tf_op jit(solution)/shard_map/all_to_all | solution.py:101
  102.0 4.6 %all-to-all-start.3 = ((bf16[8,896,128]{1,2,0:T(8,128)(2,1)}), bf16[8,896,128]{1,2,0:T(8,128)(2,1)S(1)}, u32[]{:S(2)}, u32[]{:S(2)}) async-start(bf16[8,896,128]{1,2,0:T(8,128)(2,1)} %copy.94), calls=%async_computation.3 | async-start | bytes 3670016 | tf_op jit(solution)/shard_map/all_to_all | solution.py:102
  107.6 0.2 copy.96
  107.9 3.9 %fusion.12 = pred[128,4608]{0,1:T(8,128)(4,1)S(1)} fusion(s32[4608]{0:T(1024)S(1)} %sub.25, pred[4608]{0:T(1024)(128)(4,1)S(1)} %and.68, pred[4608]{0:T(1024)(128)(4,1)S(1)} %and.66), kind=kLoop, calls=%fused_computation.21 | loop fusion | flops 1769472 | bytes 617472 | tf_op jit(solution)/shard_map/or | solution.py:113
  111.7 23.0 %all-to-all-done.3 = bf16[8,896,128]{1,2,0:T(8,128)(2,1)S(1)} async-done(((bf16[8,896,128]{1,2,0:T(8,128)(2,1)}), bf16[8,896,128]{1,2,0:T(8,128)(2,1)S(1)}, u32[]{:S(2)}, u32[]{:S(2)}) %all-to-all-start.3) | async-done | bytes 1835040 | tf_op jit(solution)/shard_map/all_to_all | solution.py:102
  134.8 9.7 %all-gather.3.cloned.1.call-done = bf16[4608,576]{1,0:T(8,128)(2,1)} async-done(((bf16[144,576]{1,0:T(8,128)(2,1)}), bf16[4608,576]{1,0:T(8,128)(2,1)}) %all-gather.3.cloned.1.call-update) | async-done | bytes 5308432 | tf_op jit(solution)/shard_map/all_gather | solution.py:95
  144.4 4.7 %fusion.58 = (f32[2,128]{1,0:T(2,128)S(1)}, f32[2,128,4608]{1,2,0:T(8,128)S(1)}) fusion(bf16[4608,576,1]{1,0,2:T(8,128)(2,1)} %bitcast.110, bf16[128,2,576]{0,2,1:T(8,128)(2,1)S(1)} %bitcast.105, pred[128,4608]{0,1:T(8,128)(4,1)S(1)} %fusion.12), kind=kOutput, calls=%fused_computation.93 | convolution fusion | flops 1362493184 | bytes 10912768 | tf_op jit(solution)/shard_map/thc,kc->htk/dot_general | solution.py:116
  149.2 2.1 copy-done.2
  151.4 0.6 fusion.5
  152.0 5.5 %fusion.18 = bf16[128,2,128]{2,0,1:T(8,128)(2,1)S(1)} fusion(bf16[2,512,128]{2,1,0:T(8,128)(2,1)S(1)} %copy-done.12, f32[2,128,4608]{1,2,0:T(8,128)} %copy-done.2, f32[2,128]{1,0:T(2,128)S(1)} %get-tuple-element.13, bf16[4608,576]{1,0:T(8,128)(2,1)} %all-gather.3.cloned.1.call-done, f32[128,2]{0,1:T(2,128)S(1)} %bitcast.109), kind=kOutput, calls=%fused_computation.31 | convolution fusion | flops 1244168192 | bytes 9766912 | tf_op jit(solution)/shard_map/thc,hcv->thv/dot_general | solution.py:130
  157.7 2.7 fusion.7
  160.4 7.6 %all_to_all.60 = f32[2,64,7168]{2,1,0:T(8,128)} all-to-all(f32[2,64,7168]{2,1,0:T(8,128)S(1)} %fusion.7), channel_id=1, replica_groups=mesh['rep'=8,'epo'=16,'core'=2] {'core'}, dimensions={0} | all-to-all | bytes 7340032 | tf_op jit(solution)/shard_map/all_to_all | solution.py:137
  168.0 2.4 reduce_sum.84
  170.4 1.5 convert_element_type.103
  172.0 6.0 %all-to-all-start.5 = ((bf16[16,16,1792]{2,1,0:T(8,128)(2,1)}), bf16[16,16,1792]{2,1,0:T(8,128)(2,1)S(1)}, u32[]{:S(2)}, u32[]{:S(2)}) async-start(bf16[16,16,1792]{2,1,0:T(8,128)(2,1)} %convert_element_type.103), calls=%async_computation.5 | async-start | bytes 1835008 | tf_op jit(solution)/shard_map/all_to_all | solution.py:140
  178.2 0.2 select_reduce_fusion
  178.4 0.3 convolution_convert_fusion.6
  178.7 22.4 %all-to-all-done.5 = bf16[16,16,1792]{2,1,0:T(8,128)(2,1)S(1)} async-done(((bf16[16,16,1792]{2,1,0:T(8,128)(2,1)}), bf16[16,16,1792]{2,1,0:T(8,128)(2,1)S(1)}, u32[]{:S(2)}, u32[]{:S(2)}) %all-to-all-start.5) | async-done | bytes 917536 | tf_op jit(solution)/shard_map/all_to_all | solution.py:140
  201.1 0.1 convert_reduce_fusion.2
  201.3 0.1 multiply_reduce_fusion
  201.6 0.1 reduce_sum.89
  201.7 0.5 convolution_convert_fusion.2
  202.2 0.4 reshape.242
  202.6 31.8 %all_to_all.61 = bf16[32,16,896]{2,1,0:T(8,128)(2,1)S(1)} all-to-all(bf16[32,16,896]{2,1,0:T(8,128)(2,1)S(1)} %reshape.242), channel_id=1, replica_groups=mesh['rep'=8,'epo'=16,'core'=2] {'epo','core'}, dimensions={0} | all-to-all | bytes 1835008 | tf_op jit(solution)/shard_map/all_to_all | solution.py:173
  234.4 0.1 copy.126
  234.6 20.8 %all_to_all.62 = bf16[8,64,896]{2,1,0:T(8,128)(2,1)S(1)} all-to-all(bf16[8,64,896]{2,1,0:T(8,128)(2,1)S(1)} %bitcast.97), channel_id=1, replica_groups=mesh['rep'=8,'epo'=16,'core'=2] {'rep'}, dimensions={0} | all-to-all | bytes 1835008 | tf_op jit(solution)/shard_map/all_to_all | solution.py:176
  255.4 2.8 fusion.13
  258.2 1.3 fusion.14
  259.5 0.1 pad_maximum_fusion
  259.7 28.6 %all_to_all.63 = bf16[8,512,256]{1,2,0:T(8,128)(2,1)S(1)} all-to-all(bf16[8,512,256]{1,2,0:T(8,128)(2,1)S(1)} %pad_maximum_fusion), channel_id=1, replica_groups=mesh['rep'=8,'epo'=16,'core'=2] {'rep'}, dimensions={0} | all-to-all | bytes 4194304 | tf_op jit(solution)/shard_map/all_to_all | solution.py:180
  288.2 0.3 convert_reduce_fusion.1
  288.6 0.1 copy.104
  288.7 0.1 broadcast_in_dim.20
  288.9 15.9 %all_to_all.64 = bf16[8,512,128]{2,1,0:T(8,128)(2,1)S(1)} all-to-all(bf16[8,512,128]{2,1,0:T(8,128)(2,1)S(1)} %broadcast_in_dim.20), channel_id=1, replica_groups=mesh['rep'=8,'epo'=16,'core'=2] {'rep'}, dimensions={0} | all-to-all | bytes 2097152 | tf_op jit(solution)/shard_map/all_to_all | solution.py:186
  304.8 3.6 convert_reduce_fusion
  308.5 13.9 %all_to_all.65 = bf16[8,64,896]{2,1,0:T(8,128)(2,1)S(1)} all-to-all(bf16[8,64,896]{2,1,0:T(8,128)(2,1)S(1)} %bitcast.104), channel_id=1, replica_groups=mesh['rep'=8,'epo'=16,'core'=2] {'rep'}, dimensions={0} | all-to-all | bytes 1835008 | tf_op jit(solution)/shard_map/all_to_all | solution.py:191
  322.4 1.4 copy.105
  323.8 13.0 %all-to-all-start.11 = ((bf16[32,16,896]{2,1,0:T(8,128)(2,1)}), bf16[32,16,896]{2,1,0:T(8,128)(2,1)S(1)}, u32[]{:S(2)}, u32[]{:S(2)}) async-start(bf16[32,16,896]{2,1,0:T(8,128)(2,1)} %bitcast.31), calls=%async_computation.11 | async-start | bytes 1835008 | tf_op jit(solution)/shard_map/all_to_all | solution.py:193
  336.9 0.3 fusion.39
  337.2 25.0 %all-to-all-done.11 = bf16[32,16,896]{2,1,0:T(8,128)(2,1)S(1)} async-done(((bf16[32,16,896]{2,1,0:T(8,128)(2,1)}), bf16[32,16,896]{2,1,0:T(8,128)(2,1)S(1)}, u32[]{:S(2)}, u32[]{:S(2)}) %all-to-all-start.11) | async-done | bytes 917536 | tf_op jit(solution)/shard_map/all_to_all | solution.py:193
  362.2 0.4 reshape.247
  362.6 1.1 fusion.1
  (58 shorter events, 1.7 us)
Async XLA Ops:
  6.5 1.4 copy-start
  6.5 12.9 %copy-start.10 = (bf16[1,2304]{1,0:T(2,128)(2,1)S(1)}, bf16[1,2304]{1,0:T(2,128)(2,1)}, u32[]{:S(2)}) copy-start(bf16[1,2304]{1,0:T(2,128)(2,1)} %param.16) | copy-start | bytes 13828
  11.0 19.9 %all-to-all-start = ((bf16[8,2,18432]{2,1,0:T(2,128)(2,1)}), bf16[8,2,18432]{2,1,0:T(2,128)(2,1)S(1)}, u32[]{:S(2)}, u32[]{:S(2)}) async-start(bf16[8,2,18432]{2,1,0:T(2,128)(2,1)} %reshape.260), calls=%async_computation | async-start | bytes 1179648 | tf_op jit(solution)/shard_map/all_to_all | solution.py:69
  18.5 125.9 %all-gather.3.cloned.1.call-start = ((), (), s32[]{:S(2)}) async-start(), calls=%async_computation.12 | async-start | bytes 6082560 | tf_op jit(solution)/shard_map/all_gather | solution.py:95
  35.1 5.9 %copy-start.3 = (bf16[1,7168,128]{2,1,0:T(8,128)(2,1)S(1)}, bf16[1,7168,128]{2,1,0:T(8,128)(2,1)}, u32[]{:S(2)}) copy-start(bf16[1,7168,128]{2,1,0:T(8,128)(2,1)} %param.27) | copy-start | bytes 5505028
  36.7 30.2 %all-to-all-start.1 = ((bf16[8,128,896]{2,1,0:T(8,128)(2,1)}), bf16[8,128,896]{2,1,0:T(8,128)(2,1)}, u32[]{:S(2)}, u32[]{:S(2)}) async-start(bf16[8,128,896]{2,1,0:T(8,128)(2,1)} %bitcast.92), calls=%async_computation.1 | async-start | bytes 3670016 | tf_op jit(solution)/shard_map/all_to_all | solution.py:100
  43.7 30.0 %copy-start.4 = (bf16[1,7168,128]{2,1,0:T(8,128)(2,1)S(1)}, bf16[1,7168,128]{2,1,0:T(8,128)(2,1)}, u32[]{:S(2)}) copy-start(bf16[1,7168,128]{2,1,0:T(8,128)(2,1)} %param.28) | copy-start | bytes 5505028
  66.8 35.2 %all-to-all-start.2 = ((bf16[8,896,128]{1,2,0:T(8,128)(2,1)}), bf16[8,896,128]{1,2,0:T(8,128)(2,1)}, u32[]{:S(2)}, u32[]{:S(2)}) async-start(bf16[8,896,128]{1,2,0:T(8,128)(2,1)} %copy.93), calls=%async_computation.2 | async-start | bytes 3670016 | tf_op jit(solution)/shard_map/all_to_all | solution.py:101
  73.7 34.0 %copy-start.8 = (bf16[1,128,1152]{2,1,0:T(8,128)(2,1)S(1)}, bf16[1,128,1152]{2,1,0:T(8,128)(2,1)}, u32[]{:S(2)}) copy-start(bf16[1,128,1152]{2,1,0:T(8,128)(2,1)} %param.15) | copy-start | bytes 884740
  102.0 32.7 %all-to-all-start.3 = ((bf16[8,896,128]{1,2,0:T(8,128)(2,1)}), bf16[8,896,128]{1,2,0:T(8,128)(2,1)S(1)}, u32[]{:S(2)}, u32[]{:S(2)}) async-start(bf16[8,896,128]{1,2,0:T(8,128)(2,1)} %copy.94), calls=%async_computation.3 | async-start | bytes 3670016 | tf_op jit(solution)/shard_map/all_to_all | solution.py:102
  134.8 14.4 %copy-start.5 = (bf16[8,896,128]{1,2,0:T(8,128)(2,1)}, bf16[8,896,128]{1,2,0:T(8,128)(2,1)S(1)}, u32[]{:S(2)}) copy-start(bf16[8,896,128]{1,2,0:T(8,128)(2,1)S(1)} %all-to-all-done.3) | copy-start | bytes 5505028
  149.2 2.2 copy-start.2
  149.2 2.8 copy-start.12
  168.0 10.0 %copy-start.7 = (bf16[1,4,7168]{2,1,0:T(4,128)(2,1)S(1)}, bf16[1,4,7168]{2,1,0:T(4,128)(2,1)}, u32[]{:S(2)}) copy-start(bf16[1,4,7168]{2,1,0:T(4,128)(2,1)} %param.21) | copy-start | bytes 172036
  168.0 10.0 %copy-start.11 = (s32[1,4,8]{2,1,0:T(4,128)S(1)}, s32[1,4,8]{2,1,0:T(4,128)}, u32[]{:S(2)}) copy-start(s32[1,4,8]{2,1,0:T(4,128)} %param.25) | copy-start | bytes 388
  168.0 10.2 %copy-start.9 = (bf16[7168]{0:T(1024)(128)(2,1)S(1)}, bf16[7168]{0:T(1024)(128)(2,1)}, u32[]{:S(2)}) copy-start(bf16[7168]{0:T(1024)(128)(2,1)} %param.24) | copy-start | bytes 43012
  172.0 29.2 %all-to-all-start.5 = ((bf16[16,16,1792]{2,1,0:T(8,128)(2,1)}), bf16[16,16,1792]{2,1,0:T(8,128)(2,1)S(1)}, u32[]{:S(2)}, u32[]{:S(2)}) async-start(bf16[16,16,1792]{2,1,0:T(8,128)(2,1)} %convert_element_type.103), calls=%async_computation.5 | async-start | bytes 1835008 | tf_op jit(solution)/shard_map/all_to_all | solution.py:140
  234.6 23.6 %copy-start.6 = (bf16[8,896,128]{1,2,0:T(8,128)(2,1)S(1)}, bf16[8,896,128]{1,2,0:T(8,128)(2,1)}, u32[]{:S(2)}) copy-start(bf16[8,896,128]{1,2,0:T(8,128)(2,1)} %copy-done.5) | copy-start | bytes 5505028
  308.4 28.4 %copy-start.13 = (bf16[1,4,8]{2,1,0:T(4,128)(2,1)S(1)}, bf16[1,4,8]{2,1,0:T(4,128)(2,1)}, u32[]{:S(2)}) copy-start(bf16[1,4,8]{2,1,0:T(4,128)(2,1)} %param.26) | copy-start | bytes 196
  308.5 55.3 %copy-start.1 = (bf16[1,8,36864]{2,1,0:T(8,128)(2,1)S(1)}, bf16[1,8,36864]{2,1,0:T(8,128)(2,1)}, u32[]{:S(2)}) copy-start(bf16[1,8,36864]{2,1,0:T(8,128)(2,1)} %param.17) | copy-start | bytes 1769476
  323.8 38.4 %all-to-all-start.11 = ((bf16[32,16,896]{2,1,0:T(8,128)(2,1)}), bf16[32,16,896]{2,1,0:T(8,128)(2,1)S(1)}, u32[]{:S(2)}, u32[]{:S(2)}) async-start(bf16[32,16,896]{2,1,0:T(8,128)(2,1)} %bitcast.31), calls=%async_computation.11 | async-start | bytes 1835008 | tf_op jit(solution)/shard_map/all_to_all | solution.py:193
Sparse Core Ops, SparseCore 0:
  33.4 111.0 all-gather.2

commit v10 on v9

--- a/solution.py
+++ b/solution.py
@@ -169,11 +169,9 @@
         placing.astype(jnp.bfloat16), normed, preferred_element_type=jnp.float32
     ).astype(jnp.bfloat16)
     width = grouped.shape[1]
-    grouped = grouped.reshape(expert_count, 16, -1)
-    mine = lax.all_to_all(grouped, EP, split_axis=0, concat_axis=0, tiled=True)
-    mine = mine.reshape(slot_count, rep_count, chunk)
-    mine = jnp.transpose(mine, (1, 0, 2))
-    columns = lax.all_to_all(mine, "rep", 0, 0, tiled=True).reshape(-1, chunk)
+    spread = grouped.reshape(expert_count, capacity, rep_count, chunk)
+    spread = jnp.transpose(spread, (2, 0, 1, 3)).reshape(rep_count * expert_count, capacity, chunk)
+    columns = lax.all_to_all(spread, ("rep",) + EP, 0, 0, tiled=True).reshape(-1, chunk)
     gate_part = jnp.einsum("nd,rdk->rnk", columns, gate_rows, preferred_element_type=jnp.float32)
     up_part = jnp.einsum("nd,rdk->rnk", columns, up_rows, preferred_element_type=jnp.float32)
     parts = jnp.concatenate([gate_part, up_part], axis=2).astype(jnp.bfloat16)

time: 372 us -> 363 us (0.976)
  blocking collectives: 119 us -> 112 us
  starting transfers between devices: 42.3 us -> 38.4 us
    all_to_all x2 -> x1, blocking collectives: 52.7 us -> 39.9 us  [local(): lax.all_to_all(spread, ('rep',) + EP, 0, 0, tiled=True).reshape(-1, chunk)]
    all_to_all x1, starting transfers between devices: 13 us -> 9.09 us  [local(): served = lax.all_to_all(back, EP, split_axis=0, concat_axis=0, tiled=True)]
where the time goes in v10:
time: 363 us; the launch traced here: 362 us
  waiting for transfers between devices  140 us (39%)
  blocking collectives  112 us (31%)
  starting transfers between devices  38.4 us (11%)
  matrix products  24.3 us (7%)
  local copies, waits for them, and re-layouts  22.8 us (6%)
  between operations  14.5 us (4%)
  other arithmetic  10.3 us (3%)
    all_to_all x1, blocking collectives, local(): lax.all_to_all(spread, ('rep',) + EP, 0, 0, tiled=True).reshape(-1, chunk)  39.9 us
    all_to_all x1, blocking collectives, local(): parts = lax.all_to_all(parts, 'rep', 0, 0, tiled=True)  31.3 us
    all_to_all x1, waiting for transfers between devices, local(): lax.all_to_all(w_gate[0].reshape(rep_count, chunk, hidden_width), 'rep',...  25.6 us
    all_to_all x1, waiting for transfers between devices, local(): served = lax.all_to_all(back, EP, split_axis=0, concat_axis=0, tiled=True)  25 us
    all_to_all x1, waiting for transfers between devices, local(): down_cols = lax.all_to_all(down_cols, 'rep', 0, 0, tiled=True)  23.2 us
    all_to_all x1, waiting for transfers between devices, local(): lax.all_to_all(w_up[0].reshape(rep_count, chunk, hidden_width), 'rep', 0,...  23 us
    all_to_all x1, waiting for transfers between devices, local(): lax.all_to_all(partial, 'epo', 0, 0, tiled=True).astype(jnp.float32)  22.4 us
    all_to_all x1, blocking collectives, local(): units_all = lax.all_to_all(unit_copies, 'rep', 0, 0, tiled=True)  17.4 us
  transfers between devices with their start and end apart: 7, of which 7 were waited for; matrix products, arithmetic and copies ran while one was open for 4% of the time, Pallas kernels for 0%

profile of v10, /device:TPU:1, one launch (start us, length us, event | category | flops | bytes accessed | tf_op | source)
XLA Modules:
  0.0 361.9 jit_solution(4328097354457535463)
XLA Ops:
  6.6 0.8 constant_dynamic-slice_fusion
  7.7 0.2 fusion.42
  7.9 0.3 fusion
  8.2 0.5 broadcast.180
  8.7 1.1 reduce.6
  9.8 1.2 reshape.261
  11.0 7.5 %all-to-all-start = ((bf16[8,2,18432]{2,1,0:T(2,128)(2,1)}), bf16[8,2,18432]{2,1,0:T(2,128)(2,1)S(1)}, u32[]{:S(2)}, u32[]{:S(2)}) async-start(bf16[8,2,18432]{2,1,0:T(2,128)(2,1)} %reshape.261), calls=%async_computation | async-start | bytes 1179648 | tf_op jit(solution)/shard_map/all_to_all | solution.py:69
  18.6 0.8 dynamic_slice.13
  19.7 0.2 add_reduce_fusion
  19.8 11.1 %all-to-all-done = bf16[8,2,18432]{2,1,0:T(2,128)(2,1)S(1)} async-done(((bf16[8,2,18432]{2,1,0:T(2,128)(2,1)}), bf16[8,2,18432]{2,1,0:T(2,128)(2,1)S(1)}, u32[]{:S(2)}, u32[]{:S(2)}) %all-to-all-start) | async-done | bytes 589856 | tf_op jit(solution)/shard_map/all_to_all | solution.py:69
  30.9 0.6 reshape.262
  31.5 0.8 convolution_convert_fusion.1
  32.3 0.2 reshape.237
  32.5 0.8 maximum_maximum_fusion
  33.2 1.8 copy.121
  35.1 1.6 copy.130
  36.7 4.3 %all-to-all-start.1 = ((bf16[8,128,896]{2,1,0:T(8,128)(2,1)}), bf16[8,128,896]{2,1,0:T(8,128)(2,1)}, u32[]{:S(2)}, u32[]{:S(2)}) async-start(bf16[8,128,896]{2,1,0:T(8,128)(2,1)} %bitcast.92), calls=%async_computation.1 | async-start | bytes 3670016 | tf_op jit(solution)/shard_map/all_to_all | solution.py:100
  41.0 2.7 copy.97
  43.7 23.2 %all-to-all-done.1 = bf16[8,128,896]{2,1,0:T(8,128)(2,1)} async-done(((bf16[8,128,896]{2,1,0:T(8,128)(2,1)}), bf16[8,128,896]{2,1,0:T(8,128)(2,1)}, u32[]{:S(2)}, u32[]{:S(2)}) %all-to-all-start.1) | async-done | bytes 1835040 | tf_op jit(solution)/shard_map/all_to_all | solution.py:100
  66.8 6.8 %all-to-all-start.2 = ((bf16[8,896,128]{1,2,0:T(8,128)(2,1)}), bf16[8,896,128]{1,2,0:T(8,128)(2,1)}, u32[]{:S(2)}, u32[]{:S(2)}) async-start(bf16[8,896,128]{1,2,0:T(8,128)(2,1)} %copy.97), calls=%async_computation.2 | async-start | bytes 3670016 | tf_op jit(solution)/shard_map/all_to_all | solution.py:101
  73.7 2.7 copy.98
  76.4 25.6 %all-to-all-done.2 = bf16[8,896,128]{1,2,0:T(8,128)(2,1)} async-done(((bf16[8,896,128]{1,2,0:T(8,128)(2,1)}), bf16[8,896,128]{1,2,0:T(8,128)(2,1)}, u32[]{:S(2)}, u32[]{:S(2)}) %all-to-all-start.2) | async-done | bytes 1835040 | tf_op jit(solution)/shard_map/all_to_all | solution.py:101
  102.0 4.6 %all-to-all-start.3 = ((bf16[8,896,128]{1,2,0:T(8,128)(2,1)}), bf16[8,896,128]{1,2,0:T(8,128)(2,1)S(1)}, u32[]{:S(2)}, u32[]{:S(2)}) async-start(bf16[8,896,128]{1,2,0:T(8,128)(2,1)} %copy.98), calls=%async_computation.3 | async-start | bytes 3670016 | tf_op jit(solution)/shard_map/all_to_all | solution.py:102
  107.6 0.2 copy.100
  107.9 3.9 %fusion.12 = pred[128,4608]{0,1:T(8,128)(4,1)S(1)} fusion(s32[4608]{0:T(1024)S(1)} %sub.25, pred[4608]{0:T(1024)(128)(4,1)S(1)} %and.68, pred[4608]{0:T(1024)(128)(4,1)S(1)} %and.66), kind=kLoop, calls=%fused_computation.21 | loop fusion | flops 1769472 | bytes 617472 | tf_op jit(solution)/shard_map/or | solution.py:113
  111.7 23.0 %all-to-all-done.3 = bf16[8,896,128]{1,2,0:T(8,128)(2,1)S(1)} async-done(((bf16[8,896,128]{1,2,0:T(8,128)(2,1)}), bf16[8,896,128]{1,2,0:T(8,128)(2,1)S(1)}, u32[]{:S(2)}, u32[]{:S(2)}) %all-to-all-start.3) | async-done | bytes 1835040 | tf_op jit(solution)/shard_map/all_to_all | solution.py:102
  134.8 9.7 %all-gather.3.cloned.1.call-done = bf16[4608,576]{1,0:T(8,128)(2,1)} async-done(((bf16[144,576]{1,0:T(8,128)(2,1)}), bf16[4608,576]{1,0:T(8,128)(2,1)}) %all-gather.3.cloned.1.call-update) | async-done | bytes 5308432 | tf_op jit(solution)/shard_map/all_gather | solution.py:95
  144.4 4.7 %fusion.58 = (f32[2,128]{1,0:T(2,128)S(1)}, f32[2,128,4608]{1,2,0:T(8,128)S(1)}) fusion(bf16[4608,576,1]{1,0,2:T(8,128)(2,1)} %bitcast.108, bf16[128,2,576]{0,2,1:T(8,128)(2,1)S(1)} %bitcast.103, pred[128,4608]{0,1:T(8,128)(4,1)S(1)} %fusion.12), kind=kOutput, calls=%fused_computation.92 | convolution fusion | flops 1362493184 | bytes 10912768 | tf_op jit(solution)/shard_map/thc,kc->htk/dot_general | solution.py:116
  149.2 2.1 copy-done.2
  151.3 0.6 fusion.5
  152.0 5.5 %fusion.18 = bf16[128,2,128]{2,0,1:T(8,128)(2,1)S(1)} fusion(bf16[2,512,128]{2,1,0:T(8,128)(2,1)S(1)} %copy-done.11, f32[2,128,4608]{1,2,0:T(8,128)} %copy-done.2, f32[2,128]{1,0:T(2,128)S(1)} %get-tuple-element.13, bf16[4608,576]{1,0:T(8,128)(2,1)} %all-gather.3.cloned.1.call-done, f32[128,2]{0,1:T(2,128)S(1)} %bitcast.107), kind=kOutput, calls=%fused_computation.31 | convolution fusion | flops 1244168192 | bytes 9766912 | tf_op jit(solution)/shard_map/thc,hcv->thv/dot_general | solution.py:130
  157.7 2.7 fusion.7
  160.4 7.6 %all_to_all.55 = f32[2,64,7168]{2,1,0:T(8,128)} all-to-all(f32[2,64,7168]{2,1,0:T(8,128)S(1)} %fusion.7), channel_id=1, replica_groups=mesh['rep'=8,'epo'=16,'core'=2] {'core'}, dimensions={0} | all-to-all | bytes 7340032 | tf_op jit(solution)/shard_map/all_to_all | solution.py:137
  168.0 2.4 reduce_sum.84
  170.4 1.5 convert_element_type.103
  171.9 6.0 %all-to-all-start.5 = ((bf16[16,16,1792]{2,1,0:T(8,128)(2,1)}), bf16[16,16,1792]{2,1,0:T(8,128)(2,1)S(1)}, u32[]{:S(2)}, u32[]{:S(2)}) async-start(bf16[16,16,1792]{2,1,0:T(8,128)(2,1)} %convert_element_type.103), calls=%async_computation.5 | async-start | bytes 1835008 | tf_op jit(solution)/shard_map/all_to_all | solution.py:140
  178.2 0.2 select_reduce_fusion
  178.4 0.3 convolution_convert_fusion.6
  178.7 22.4 %all-to-all-done.5 = bf16[16,16,1792]{2,1,0:T(8,128)(2,1)S(1)} async-done(((bf16[16,16,1792]{2,1,0:T(8,128)(2,1)}), bf16[16,16,1792]{2,1,0:T(8,128)(2,1)S(1)}, u32[]{:S(2)}, u32[]{:S(2)}) %all-to-all-start.5) | async-done | bytes 917536 | tf_op jit(solution)/shard_map/all_to_all | solution.py:140
  201.1 0.1 convert_reduce_fusion.2
  201.3 0.1 multiply_reduce_fusion
  201.5 0.1 reduce_sum.89
  201.7 0.5 convolution_convert_fusion.2
  202.2 0.1 copy.122
  202.3 0.2 copy.107
  202.5 0.9 copy.108
  203.4 39.9 %all_to_all.56 = bf16[256,2,896]{2,1,0:T(2,128)(2,1)S(1)} all-to-all(bf16[256,2,896]{2,1,0:T(2,128)(2,1)S(1)} %copy.108), channel_id=1, replica_groups=mesh['rep'=8,'epo'=16,'core'=2] {'rep','epo','core'}, dimensions={0} | all-to-all | bytes 1835008 | tf_op jit(solution)/shard_map/all_to_all | solution.py:174
  243.4 1.3 reshape.257
  244.6 3.1 fusion.13
  247.8 1.3 fusion.14
  249.0 0.1 pad_maximum_fusion
  249.2 31.3 %all_to_all.57 = bf16[8,512,256]{1,2,0:T(8,128)(2,1)S(1)} all-to-all(bf16[8,512,256]{1,2,0:T(8,128)(2,1)S(1)} %pad_maximum_fusion), channel_id=1, replica_groups=mesh['rep'=8,'epo'=16,'core'=2] {'rep'}, dimensions={0} | all-to-all | bytes 4194304 | tf_op jit(solution)/shard_map/all_to_all | solution.py:178
  280.4 0.3 convert_reduce_fusion.1
  280.8 0.1 copy.109
  281.0 0.1 broadcast_in_dim.20
  281.1 17.4 %all_to_all.58 = bf16[8,512,128]{2,1,0:T(8,128)(2,1)S(1)} all-to-all(bf16[8,512,128]{2,1,0:T(8,128)(2,1)S(1)} %broadcast_in_dim.20), channel_id=1, replica_groups=mesh['rep'=8,'epo'=16,'core'=2] {'rep'}, dimensions={0} | all-to-all | bytes 2097152 | tf_op jit(solution)/shard_map/all_to_all | solution.py:184
  298.5 3.6 %convert_reduce_fusion = bf16[512,896]{1,0:T(8,128)(2,1)S(1)} fusion(bf16[8,512,128]{2,1,0:T(8,128)(2,1)S(1)} %all_to_all.58, bf16[8,128,896]{2,1,0:T(8,128)(2,1)} %all-to-all-done.1), kind=kOutput, calls=%fused_computation.6 | convolution fusion | flops 946405376 | bytes 3801088 | tf_op jit(solution)/shard_map/rnk,rkc->rnc/dot_general | solution.py:185
  302.1 15.5 %all_to_all.59 = bf16[8,64,896]{2,1,0:T(8,128)(2,1)S(1)} all-to-all(bf16[8,64,896]{2,1,0:T(8,128)(2,1)S(1)} %bitcast.102), channel_id=1, replica_groups=mesh['rep'=8,'epo'=16,'core'=2] {'rep'}, dimensions={0} | all-to-all | bytes 1835008 | tf_op jit(solution)/shard_map/all_to_all | solution.py:189
  317.6 1.4 copy.110
  319.1 9.1 %all-to-all-start.10 = ((bf16[32,16,896]{2,1,0:T(8,128)(2,1)}), bf16[32,16,896]{2,1,0:T(8,128)(2,1)S(1)}, u32[]{:S(2)}, u32[]{:S(2)}) async-start(bf16[32,16,896]{2,1,0:T(8,128)(2,1)} %bitcast.28), calls=%async_computation.10 | async-start | bytes 1835008 | tf_op jit(solution)/shard_map/all_to_all | solution.py:191
  328.3 0.3 fusion.39
  328.5 25.0 %all-to-all-done.10 = bf16[32,16,896]{2,1,0:T(8,128)(2,1)S(1)} async-done(((bf16[32,16,896]{2,1,0:T(8,128)(2,1)}), bf16[32,16,896]{2,1,0:T(8,128)(2,1)S(1)}, u32[]{:S(2)}, u32[]{:S(2)}) %all-to-all-start.10) | async-done | bytes 917536 | tf_op jit(solution)/shard_map/all_to_all | solution.py:191
  353.6 0.4 reshape.247
  354.0 1.1 fusion.1
  (57 shorter events, 1.8 us)
Async XLA Ops:
  6.5 1.4 copy-start
  6.5 12.9 %copy-start.9 = (bf16[1,2304]{1,0:T(2,128)(2,1)S(1)}, bf16[1,2304]{1,0:T(2,128)(2,1)}, u32[]{:S(2)}) copy-start(bf16[1,2304]{1,0:T(2,128)(2,1)} %param.16) | copy-start | bytes 13828
  11.0 19.9 %all-to-all-start = ((bf16[8,2,18432]{2,1,0:T(2,128)(2,1)}), bf16[8,2,18432]{2,1,0:T(2,128)(2,1)S(1)}, u32[]{:S(2)}, u32[]{:S(2)}) async-start(bf16[8,2,18432]{2,1,0:T(2,128)(2,1)} %reshape.261), calls=%async_computation | async-start | bytes 1179648 | tf_op jit(solution)/shard_map/all_to_all | solution.py:69
  18.5 125.9 %all-gather.3.cloned.1.call-start = ((), (), s32[]{:S(2)}) async-start(), calls=%async_computation.11 | async-start | bytes 6082560 | tf_op jit(solution)/shard_map/all_gather | solution.py:95
  35.1 5.9 %copy-start.3 = (bf16[1,7168,128]{2,1,0:T(8,128)(2,1)S(1)}, bf16[1,7168,128]{2,1,0:T(8,128)(2,1)}, u32[]{:S(2)}) copy-start(bf16[1,7168,128]{2,1,0:T(8,128)(2,1)} %param.27) | copy-start | bytes 5505028
  36.7 30.2 %all-to-all-start.1 = ((bf16[8,128,896]{2,1,0:T(8,128)(2,1)}), bf16[8,128,896]{2,1,0:T(8,128)(2,1)}, u32[]{:S(2)}, u32[]{:S(2)}) async-start(bf16[8,128,896]{2,1,0:T(8,128)(2,1)} %bitcast.92), calls=%async_computation.1 | async-start | bytes 3670016 | tf_op jit(solution)/shard_map/all_to_all | solution.py:100
  43.7 30.0 %copy-start.4 = (bf16[1,7168,128]{2,1,0:T(8,128)(2,1)S(1)}, bf16[1,7168,128]{2,1,0:T(8,128)(2,1)}, u32[]{:S(2)}) copy-start(bf16[1,7168,128]{2,1,0:T(8,128)(2,1)} %param.28) | copy-start | bytes 5505028
  66.8 35.2 %all-to-all-start.2 = ((bf16[8,896,128]{1,2,0:T(8,128)(2,1)}), bf16[8,896,128]{1,2,0:T(8,128)(2,1)}, u32[]{:S(2)}, u32[]{:S(2)}) async-start(bf16[8,896,128]{1,2,0:T(8,128)(2,1)} %copy.97), calls=%async_computation.2 | async-start | bytes 3670016 | tf_op jit(solution)/shard_map/all_to_all | solution.py:101
  73.7 34.0 %copy-start.7 = (bf16[1,128,1152]{2,1,0:T(8,128)(2,1)S(1)}, bf16[1,128,1152]{2,1,0:T(8,128)(2,1)}, u32[]{:S(2)}) copy-start(bf16[1,128,1152]{2,1,0:T(8,128)(2,1)} %param.15) | copy-start | bytes 884740
  102.0 32.7 %all-to-all-start.3 = ((bf16[8,896,128]{1,2,0:T(8,128)(2,1)}), bf16[8,896,128]{1,2,0:T(8,128)(2,1)S(1)}, u32[]{:S(2)}, u32[]{:S(2)}) async-start(bf16[8,896,128]{1,2,0:T(8,128)(2,1)} %copy.98), calls=%async_computation.3 | async-start | bytes 3670016 | tf_op jit(solution)/shard_map/all_to_all | solution.py:102
  149.2 2.2 copy-start.2
  149.2 2.8 copy-start.11
  168.0 10.0 %copy-start.6 = (bf16[1,4,7168]{2,1,0:T(4,128)(2,1)S(1)}, bf16[1,4,7168]{2,1,0:T(4,128)(2,1)}, u32[]{:S(2)}) copy-start(bf16[1,4,7168]{2,1,0:T(4,128)(2,1)} %param.21) | copy-start | bytes 172036
  168.0 10.0 %copy-start.10 = (s32[1,4,8]{2,1,0:T(4,128)S(1)}, s32[1,4,8]{2,1,0:T(4,128)}, u32[]{:S(2)}) copy-start(s32[1,4,8]{2,1,0:T(4,128)} %param.25) | copy-start | bytes 388
  168.0 10.2 %copy-start.8 = (bf16[7168]{0:T(1024)(128)(2,1)S(1)}, bf16[7168]{0:T(1024)(128)(2,1)}, u32[]{:S(2)}) copy-start(bf16[7168]{0:T(1024)(128)(2,1)} %param.24) | copy-start | bytes 43012
  171.9 29.2 %all-to-all-start.5 = ((bf16[16,16,1792]{2,1,0:T(8,128)(2,1)}), bf16[16,16,1792]{2,1,0:T(8,128)(2,1)S(1)}, u32[]{:S(2)}, u32[]{:S(2)}) async-start(bf16[16,16,1792]{2,1,0:T(8,128)(2,1)} %convert_element_type.103), calls=%async_computation.5 | async-start | bytes 1835008 | tf_op jit(solution)/shard_map/all_to_all | solution.py:140
  244.6 3.1 copy-start.5
  302.1 26.1 %copy-start.12 = (bf16[1,4,8]{2,1,0:T(4,128)(2,1)S(1)}, bf16[1,4,8]{2,1,0:T(4,128)(2,1)}, u32[]{:S(2)}) copy-start(bf16[1,4,8]{2,1,0:T(4,128)(2,1)} %param.26) | copy-start | bytes 196
  302.1 53.0 %copy-start.1 = (bf16[1,8,36864]{2,1,0:T(8,128)(2,1)S(1)}, bf16[1,8,36864]{2,1,0:T(8,128)(2,1)}, u32[]{:S(2)}) copy-start(bf16[1,8,36864]{2,1,0:T(8,128)(2,1)} %param.17) | copy-start | bytes 1769476
  319.1 34.5 %all-to-all-start.10 = ((bf16[32,16,896]{2,1,0:T(8,128)(2,1)}), bf16[32,16,896]{2,1,0:T(8,128)(2,1)S(1)}, u32[]{:S(2)}, u32[]{:S(2)}) async-start(bf16[32,16,896]{2,1,0:T(8,128)(2,1)} %bitcast.28), calls=%async_computation.10 | async-start | bytes 1835008 | tf_op jit(solution)/shard_map/all_to_all | solution.py:191
Sparse Core Ops, SparseCore 0:
  33.4 111.0 all-gather.2

commit v11 on v10

--- a/solution.py
+++ b/solution.py
@@ -185,10 +185,10 @@
     pieces = jnp.einsum("rnk,rkc->rnc", units_all, down_cols, preferred_element_type=jnp.float32)
     out_cols = jnp.sum(pieces.astype(jnp.bfloat16).astype(jnp.float32), axis=0)
     out_cols = out_cols.astype(jnp.bfloat16)
-    out_cols = out_cols.reshape(rep_count, slot_count, chunk)
-    back = lax.all_to_all(out_cols, "rep", 0, 0, tiled=True)
-    back = jnp.transpose(back, (1, 0, 2)).reshape(expert_count, capacity * rep_count, chunk)
-    served = lax.all_to_all(back, EP, split_axis=0, concat_axis=0, tiled=True)
+    out_cols = out_cols.reshape(rep_count * expert_count, capacity, chunk)
+    back = lax.all_to_all(out_cols, ("rep",) + EP, 0, 0, tiled=True)
+    back = back.reshape(rep_count, expert_count, capacity, chunk)
+    served = jnp.transpose(back, (1, 2, 0, 3))
     mixture = jnp.dot(
         combine, served.reshape(slot_count, width).astype(jnp.float32), precision=lax.Precision.HIGHEST
     )

time: 363 us -> 349 us (0.961)
  blocking collectives: 112 us -> 96.1 us
    all_to_all x1 -> x0, blocking collectives: 15.5 us -> none  [local(): back = lax.all_to_all(out_cols, 'rep', 0, 0, tiled=True)]
where the time goes in v11:
time: 349 us; the launch traced here: 348 us
  waiting for transfers between devices  143 us (41%)
  blocking collectives  96.1 us (28%)
  starting transfers between devices  37.6 us (11%)
  matrix products  24.3 us (7%)
  local copies, waits for them, and re-layouts  22.7 us (7%)
  between operations  14.5 us (4%)
  other arithmetic  10.3 us (3%)
    all_to_all x1, blocking collectives, local(): lax.all_to_all(spread, ('rep',) + EP, 0, 0, tiled=True).reshape(-1, chunk)  39.9 us
    all_to_all x1, blocking collectives, local(): parts = lax.all_to_all(parts, 'rep', 0, 0, tiled=True)  31.3 us
    all_to_all x1, waiting for transfers between devices, local(): back = lax.all_to_all(out_cols, ('rep',) + EP, 0, 0, tiled=True)  27.8 us
    all_to_all x1, waiting for transfers between devices, local(): lax.all_to_all(w_gate[0].reshape(rep_count, chunk, hidden_width), 'rep',...  25.6 us
    all_to_all x1, waiting for transfers between devices, local(): down_cols = lax.all_to_all(down_cols, 'rep', 0, 0, tiled=True)  23.2 us
    all_to_all x1, waiting for transfers between devices, local(): lax.all_to_all(w_up[0].reshape(rep_count, chunk, hidden_width), 'rep', 0,...  23 us
    all_to_all x1, waiting for transfers between devices, local(): lax.all_to_all(partial, 'epo', 0, 0, tiled=True).astype(jnp.float32)  22.4 us
    all_to_all x1, blocking collectives, local(): units_all = lax.all_to_all(unit_copies, 'rep', 0, 0, tiled=True)  17.4 us
  transfers between devices with their start and end apart: 7, of which 7 were waited for; matrix products, arithmetic and copies ran while one was open for 4% of the time, Pallas kernels for 0%

profile of v11, /device:TPU:1, one launch (start us, length us, event | category | flops | bytes accessed | tf_op | source)
XLA Modules:
  0.0 348.4 jit_solution(10237341614748988104)
XLA Ops:
  6.6 0.8 constant_dynamic-slice_fusion
  7.7 0.2 fusion.42
  7.9 0.3 fusion
  8.2 0.5 broadcast.180
  8.7 1.1 reduce.6
  9.8 1.2 reshape.261
  11.0 7.5 %all-to-all-start = ((bf16[8,2,18432]{2,1,0:T(2,128)(2,1)}), bf16[8,2,18432]{2,1,0:T(2,128)(2,1)S(1)}, u32[]{:S(2)}, u32[]{:S(2)}) async-start(bf16[8,2,18432]{2,1,0:T(2,128)(2,1)} %reshape.261), calls=%async_computation | async-start | bytes 1179648 | tf_op jit(solution)/shard_map/all_to_all | solution.py:69
  18.6 0.8 dynamic_slice.13
  19.7 0.2 add_reduce_fusion
  19.8 11.1 %all-to-all-done = bf16[8,2,18432]{2,1,0:T(2,128)(2,1)S(1)} async-done(((bf16[8,2,18432]{2,1,0:T(2,128)(2,1)}), bf16[8,2,18432]{2,1,0:T(2,128)(2,1)S(1)}, u32[]{:S(2)}, u32[]{:S(2)}) %all-to-all-start) | async-done | bytes 589856 | tf_op jit(solution)/shard_map/all_to_all | solution.py:69
  30.9 0.6 reshape.262
  31.5 0.8 convolution_convert_fusion.1
  32.3 0.2 reshape.237
  32.5 0.8 maximum_maximum_fusion
  33.2 1.8 copy.140
  35.1 1.6 copy.150
  36.7 4.3 %all-to-all-start.1 = ((bf16[8,128,896]{2,1,0:T(8,128)(2,1)}), bf16[8,128,896]{2,1,0:T(8,128)(2,1)}, u32[]{:S(2)}, u32[]{:S(2)}) async-start(bf16[8,128,896]{2,1,0:T(8,128)(2,1)} %bitcast.95), calls=%async_computation.1 | async-start | bytes 3670016 | tf_op jit(solution)/shard_map/all_to_all | solution.py:100
  41.0 2.7 copy.115
  43.7 23.2 %all-to-all-done.1 = bf16[8,128,896]{2,1,0:T(8,128)(2,1)} async-done(((bf16[8,128,896]{2,1,0:T(8,128)(2,1)}), bf16[8,128,896]{2,1,0:T(8,128)(2,1)}, u32[]{:S(2)}, u32[]{:S(2)}) %all-to-all-start.1) | async-done | bytes 1835040 | tf_op jit(solution)/shard_map/all_to_all | solution.py:100
  66.8 6.8 %all-to-all-start.2 = ((bf16[8,896,128]{1,2,0:T(8,128)(2,1)}), bf16[8,896,128]{1,2,0:T(8,128)(2,1)}, u32[]{:S(2)}, u32[]{:S(2)}) async-start(bf16[8,896,128]{1,2,0:T(8,128)(2,1)} %copy.115), calls=%async_computation.2 | async-start | bytes 3670016 | tf_op jit(solution)/shard_map/all_to_all | solution.py:101
  73.7 2.7 copy.116
  76.4 25.6 %all-to-all-done.2 = bf16[8,896,128]{1,2,0:T(8,128)(2,1)} async-done(((bf16[8,896,128]{1,2,0:T(8,128)(2,1)}), bf16[8,896,128]{1,2,0:T(8,128)(2,1)}, u32[]{:S(2)}, u32[]{:S(2)}) %all-to-all-start.2) | async-done | bytes 1835040 | tf_op jit(solution)/shard_map/all_to_all | solution.py:101
  102.0 4.6 %all-to-all-start.3 = ((bf16[8,896,128]{1,2,0:T(8,128)(2,1)}), bf16[8,896,128]{1,2,0:T(8,128)(2,1)S(1)}, u32[]{:S(2)}, u32[]{:S(2)}) async-start(bf16[8,896,128]{1,2,0:T(8,128)(2,1)} %copy.116), calls=%async_computation.3 | async-start | bytes 3670016 | tf_op jit(solution)/shard_map/all_to_all | solution.py:102
  107.6 0.2 copy.118
  107.9 3.9 %fusion.12 = pred[128,4608]{0,1:T(8,128)(4,1)S(1)} fusion(s32[4608]{0:T(1024)S(1)} %sub.25, pred[4608]{0:T(1024)(128)(4,1)S(1)} %and.68, pred[4608]{0:T(1024)(128)(4,1)S(1)} %and.66), kind=kLoop, calls=%fused_computation.21 | loop fusion | flops 1769472 | bytes 617472 | tf_op jit(solution)/shard_map/or | solution.py:113
  111.7 23.0 %all-to-all-done.3 = bf16[8,896,128]{1,2,0:T(8,128)(2,1)S(1)} async-done(((bf16[8,896,128]{1,2,0:T(8,128)(2,1)}), bf16[8,896,128]{1,2,0:T(8,128)(2,1)S(1)}, u32[]{:S(2)}, u32[]{:S(2)}) %all-to-all-start.3) | async-done | bytes 1835040 | tf_op jit(solution)/shard_map/all_to_all | solution.py:102
  134.8 9.7 %all-gather.3.cloned.1.call-done = bf16[4608,576]{1,0:T(8,128)(2,1)} async-done(((bf16[144,576]{1,0:T(8,128)(2,1)}), bf16[4608,576]{1,0:T(8,128)(2,1)}) %all-gather.3.cloned.1.call-update) | async-done | bytes 5308432 | tf_op jit(solution)/shard_map/all_gather | solution.py:95
  144.4 4.7 %fusion.58 = (f32[2,128]{1,0:T(2,128)S(1)}, f32[2,128,4608]{1,2,0:T(8,128)S(1)}) fusion(bf16[4608,576,1]{1,0,2:T(8,128)(2,1)} %bitcast.112, bf16[128,2,576]{0,2,1:T(8,128)(2,1)S(1)} %bitcast.107, pred[128,4608]{0,1:T(8,128)(4,1)S(1)} %fusion.12), kind=kOutput, calls=%fused_computation.92 | convolution fusion | flops 1362493184 | bytes 10912768 | tf_op jit(solution)/shard_map/thc,kc->htk/dot_general | solution.py:116
  149.2 2.1 copy-done.2
  151.3 0.6 fusion.5
  152.0 5.5 %fusion.18 = bf16[128,2,128]{2,0,1:T(8,128)(2,1)S(1)} fusion(bf16[2,512,128]{2,1,0:T(8,128)(2,1)S(1)} %copy-done.11, f32[2,128,4608]{1,2,0:T(8,128)} %copy-done.2, f32[2,128]{1,0:T(2,128)S(1)} %get-tuple-element.13, bf16[4608,576]{1,0:T(8,128)(2,1)} %all-gather.3.cloned.1.call-done, f32[128,2]{0,1:T(2,128)S(1)} %bitcast.111), kind=kOutput, calls=%fused_computation.31 | convolution fusion | flops 1244168192 | bytes 9766912 | tf_op jit(solution)/shard_map/thc,hcv->thv/dot_general | solution.py:130
  157.7 2.7 fusion.7
  160.4 7.6 %all_to_all.50 = f32[2,64,7168]{2,1,0:T(8,128)} all-to-all(f32[2,64,7168]{2,1,0:T(8,128)S(1)} %fusion.7), channel_id=1, replica_groups=mesh['rep'=8,'epo'=16,'core'=2] {'core'}, dimensions={0} | all-to-all | bytes 7340032 | tf_op jit(solution)/shard_map/all_to_all | solution.py:137
  168.0 2.4 reduce_sum.84
  170.4 1.5 convert_element_type.103
  171.9 6.0 %all-to-all-start.5 = ((bf16[16,16,1792]{2,1,0:T(8,128)(2,1)}), bf16[16,16,1792]{2,1,0:T(8,128)(2,1)S(1)}, u32[]{:S(2)}, u32[]{:S(2)}) async-start(bf16[16,16,1792]{2,1,0:T(8,128)(2,1)} %convert_element_type.103), calls=%async_computation.5 | async-start | bytes 1835008 | tf_op jit(solution)/shard_map/all_to_all | solution.py:140
  178.2 0.2 select_reduce_fusion
  178.4 0.3 convolution_convert_fusion.6
  178.7 22.4 %all-to-all-done.5 = bf16[16,16,1792]{2,1,0:T(8,128)(2,1)S(1)} async-done(((bf16[16,16,1792]{2,1,0:T(8,128)(2,1)}), bf16[16,16,1792]{2,1,0:T(8,128)(2,1)S(1)}, u32[]{:S(2)}, u32[]{:S(2)}) %all-to-all-start.5) | async-done | bytes 917536 | tf_op jit(solution)/shard_map/all_to_all | solution.py:140
  201.1 0.1 convert_reduce_fusion.2
  201.3 0.1 multiply_reduce_fusion
  201.5 0.1 reduce_sum.89
  201.7 0.5 convolution_convert_fusion.2
  202.2 0.1 copy.141
  202.3 0.2 copy.125
  202.5 0.9 copy.126
  203.4 39.9 %all_to_all.51 = bf16[256,2,896]{2,1,0:T(2,128)(2,1)S(1)} all-to-all(bf16[256,2,896]{2,1,0:T(2,128)(2,1)S(1)} %copy.126), channel_id=1, replica_groups=mesh['rep'=8,'epo'=16,'core'=2] {'rep','epo','core'}, dimensions={0} | all-to-all | bytes 1835008 | tf_op jit(solution)/shard_map/all_to_all | solution.py:174
  243.4 1.3 reshape.257
  244.6 3.1 fusion.13
  247.8 1.3 fusion.14
  249.0 0.1 pad_maximum_fusion
  249.2 31.3 %all_to_all.52 = bf16[8,512,256]{1,2,0:T(8,128)(2,1)S(1)} all-to-all(bf16[8,512,256]{1,2,0:T(8,128)(2,1)S(1)} %pad_maximum_fusion), channel_id=1, replica_groups=mesh['rep'=8,'epo'=16,'core'=2] {'rep'}, dimensions={0} | all-to-all | bytes 4194304 | tf_op jit(solution)/shard_map/all_to_all | solution.py:178
  280.4 0.3 convert_reduce_fusion.1
  280.8 0.1 copy.127
  281.0 0.1 broadcast_in_dim.20
  281.1 17.4 %all_to_all.53 = bf16[8,512,128]{2,1,0:T(8,128)(2,1)S(1)} all-to-all(bf16[8,512,128]{2,1,0:T(8,128)(2,1)S(1)} %broadcast_in_dim.20), channel_id=1, replica_groups=mesh['rep'=8,'epo'=16,'core'=2] {'rep'}, dimensions={0} | all-to-all | bytes 2097152 | tf_op jit(solution)/shard_map/all_to_all | solution.py:184
  298.5 3.6 %convert_reduce_fusion = bf16[512,896]{1,0:T(8,128)(2,1)S(1)} fusion(bf16[8,512,128]{2,1,0:T(8,128)(2,1)S(1)} %all_to_all.53, bf16[8,128,896]{2,1,0:T(8,128)(2,1)} %all-to-all-done.1), kind=kOutput, calls=%fused_computation.6 | convolution fusion | flops 946405376 | bytes 3801088 | tf_op jit(solution)/shard_map/rnk,rkc->rnc/dot_general | solution.py:185
  302.1 1.3 reshape.245
  303.4 8.3 %all-to-all-start.9 = ((bf16[256,2,896]{2,1,0:T(2,128)(2,1)}), bf16[256,2,896]{2,1,0:T(2,128)(2,1)S(1)}, u32[]{:S(2)}, u32[]{:S(2)}) async-start(bf16[256,2,896]{2,1,0:T(2,128)(2,1)} %reshape.245), calls=%async_computation.9 | async-start | bytes 1835008 | tf_op jit(solution)/shard_map/all_to_all | solution.py:189
  311.8 0.3 fusion.39
  312.1 27.8 %all-to-all-done.9 = bf16[256,2,896]{2,1,0:T(2,128)(2,1)S(1)} async-done(((bf16[256,2,896]{2,1,0:T(2,128)(2,1)}), bf16[256,2,896]{2,1,0:T(2,128)(2,1)S(1)}, u32[]{:S(2)}, u32[]{:S(2)}) %all-to-all-start.9) | async-done | bytes 917536 | tf_op jit(solution)/shard_map/all_to_all | solution.py:189
  340.0 0.3 copy.129
  340.3 0.1 copy.142
  340.4 1.1 fusion.1
  (58 shorter events, 1.9 us)
Async XLA Ops:
  6.5 1.4 copy-start
  6.5 12.9 %copy-start.9 = (bf16[1,2304]{1,0:T(2,128)(2,1)S(1)}, bf16[1,2304]{1,0:T(2,128)(2,1)}, u32[]{:S(2)}) copy-start(bf16[1,2304]{1,0:T(2,128)(2,1)} %param.16) | copy-start | bytes 13828
  11.0 19.9 %all-to-all-start = ((bf16[8,2,18432]{2,1,0:T(2,128)(2,1)}), bf16[8,2,18432]{2,1,0:T(2,128)(2,1)S(1)}, u32[]{:S(2)}, u32[]{:S(2)}) async-start(bf16[8,2,18432]{2,1,0:T(2,128)(2,1)} %reshape.261), calls=%async_computation | async-start | bytes 1179648 | tf_op jit(solution)/shard_map/all_to_all | solution.py:69
  18.5 125.9 %all-gather.3.cloned.1.call-start = ((), (), s32[]{:S(2)}) async-start(), calls=%async_computation.10 | async-start | bytes 6082560 | tf_op jit(solution)/shard_map/all_gather | solution.py:95
  35.1 5.9 %copy-start.3 = (bf16[1,7168,128]{2,1,0:T(8,128)(2,1)S(1)}, bf16[1,7168,128]{2,1,0:T(8,128)(2,1)}, u32[]{:S(2)}) copy-start(bf16[1,7168,128]{2,1,0:T(8,128)(2,1)} %param.27) | copy-start | bytes 5505028
  36.7 30.2 %all-to-all-start.1 = ((bf16[8,128,896]{2,1,0:T(8,128)(2,1)}), bf16[8,128,896]{2,1,0:T(8,128)(2,1)}, u32[]{:S(2)}, u32[]{:S(2)}) async-start(bf16[8,128,896]{2,1,0:T(8,128)(2,1)} %bitcast.95), calls=%async_computation.1 | async-start | bytes 3670016 | tf_op jit(solution)/shard_map/all_to_all | solution.py:100
  43.7 30.0 %copy-start.4 = (bf16[1,7168,128]{2,1,0:T(8,128)(2,1)S(1)}, bf16[1,7168,128]{2,1,0:T(8,128)(2,1)}, u32[]{:S(2)}) copy-start(bf16[1,7168,128]{2,1,0:T(8,128)(2,1)} %param.28) | copy-start | bytes 5505028
  66.8 35.2 %all-to-all-start.2 = ((bf16[8,896,128]{1,2,0:T(8,128)(2,1)}), bf16[8,896,128]{1,2,0:T(8,128)(2,1)}, u32[]{:S(2)}, u32[]{:S(2)}) async-start(bf16[8,896,128]{1,2,0:T(8,128)(2,1)} %copy.115), calls=%async_computation.2 | async-start | bytes 3670016 | tf_op jit(solution)/shard_map/all_to_all | solution.py:101
  73.7 34.0 %copy-start.7 = (bf16[1,128,1152]{2,1,0:T(8,128)(2,1)S(1)}, bf16[1,128,1152]{2,1,0:T(8,128)(2,1)}, u32[]{:S(2)}) copy-start(bf16[1,128,1152]{2,1,0:T(8,128)(2,1)} %param.15) | copy-start | bytes 884740
  102.0 32.7 %all-to-all-start.3 = ((bf16[8,896,128]{1,2,0:T(8,128)(2,1)}), bf16[8,896,128]{1,2,0:T(8,128)(2,1)S(1)}, u32[]{:S(2)}, u32[]{:S(2)}) async-start(bf16[8,896,128]{1,2,0:T(8,128)(2,1)} %copy.116), calls=%async_computation.3 | async-start | bytes 3670016 | tf_op jit(solution)/shard_map/all_to_all | solution.py:102
  149.2 2.2 copy-start.2
  149.2 2.8 copy-start.11
  168.0 10.0 %copy-start.6 = (bf16[1,4,7168]{2,1,0:T(4,128)(2,1)S(1)}, bf16[1,4,7168]{2,1,0:T(4,128)(2,1)}, u32[]{:S(2)}) copy-start(bf16[1,4,7168]{2,1,0:T(4,128)(2,1)} %param.21) | copy-start | bytes 172036
  168.0 10.0 %copy-start.10 = (s32[1,4,8]{2,1,0:T(4,128)S(1)}, s32[1,4,8]{2,1,0:T(4,128)}, u32[]{:S(2)}) copy-start(s32[1,4,8]{2,1,0:T(4,128)} %param.25) | copy-start | bytes 388
  168.0 10.2 %copy-start.8 = (bf16[7168]{0:T(1024)(128)(2,1)S(1)}, bf16[7168]{0:T(1024)(128)(2,1)}, u32[]{:S(2)}) copy-start(bf16[7168]{0:T(1024)(128)(2,1)} %param.24) | copy-start | bytes 43012
  171.9 29.2 %all-to-all-start.5 = ((bf16[16,16,1792]{2,1,0:T(8,128)(2,1)}), bf16[16,16,1792]{2,1,0:T(8,128)(2,1)S(1)}, u32[]{:S(2)}, u32[]{:S(2)}) async-start(bf16[16,16,1792]{2,1,0:T(8,128)(2,1)} %convert_element_type.103), calls=%async_computation.5 | async-start | bytes 1835008 | tf_op jit(solution)/shard_map/all_to_all | solution.py:140
  244.6 3.1 copy-start.5
  298.5 13.2 %copy-start.12 = (bf16[1,4,8]{2,1,0:T(4,128)(2,1)S(1)}, bf16[1,4,8]{2,1,0:T(4,128)(2,1)}, u32[]{:S(2)}) copy-start(bf16[1,4,8]{2,1,0:T(4,128)(2,1)} %param.26) | copy-start | bytes 196
  303.4 36.5 %all-to-all-start.9 = ((bf16[256,2,896]{2,1,0:T(2,128)(2,1)}), bf16[256,2,896]{2,1,0:T(2,128)(2,1)S(1)}, u32[]{:S(2)}, u32[]{:S(2)}) async-start(bf16[256,2,896]{2,1,0:T(2,128)(2,1)} %reshape.245), calls=%async_computation.9 | async-start | bytes 1835008 | tf_op jit(solution)/shard_map/all_to_all | solution.py:189
  311.7 29.8 %copy-start.1 = (bf16[1,8,36864]{2,1,0:T(8,128)(2,1)S(1)}, bf16[1,8,36864]{2,1,0:T(8,128)(2,1)}, u32[]{:S(2)}) copy-start(bf16[1,8,36864]{2,1,0:T(8,128)(2,1)} %param.17) | copy-start | bytes 1769476
Sparse Core Ops, SparseCore 0:
  33.4 111.0 all-gather.2

commit v12 on v11

--- a/solution.py
+++ b/solution.py
@@ -97,9 +97,20 @@
     chunk = width // rep_count
     down_cols = w_down[0].reshape(hidden_width, rep_count, chunk)
     down_cols = jnp.transpose(down_cols, (1, 0, 2))
-    down_cols = lax.all_to_all(down_cols, "rep", 0, 0, tiled=True)
-    gate_rows = lax.all_to_all(w_gate[0].reshape(rep_count, chunk, hidden_width), "rep", 0, 0, tiled=True)
-    up_rows = lax.all_to_all(w_up[0].reshape(rep_count, chunk, hidden_width), "rep", 0, 0, tiled=True)
+    piece = chunk * hidden_width
+    bundle = jnp.concatenate(
+        [
+            down_cols.reshape(rep_count, piece // 1024, 1024),
+            w_gate[0].reshape(rep_count, piece // 1024, 1024),
+            w_up[0].reshape(rep_count, piece // 1024, 1024),
+        ],
+        axis=1,
+    )
+    bundle = lax.all_to_all(bundle, "rep", 0, 0, tiled=True)
+    rows_each = piece // 1024
+    down_cols = bundle[:, :rows_each].reshape(rep_count, hidden_width, chunk)
+    gate_rows = bundle[:, rows_each : 2 * rows_each].reshape(rep_count, chunk, hidden_width)
+    up_rows = bundle[:, 2 * rows_each :].reshape(rep_count, chunk, hidden_width)
     chip_keys, down_cols, gate_rows, up_rows = lax.optimization_barrier(
         (chip_keys, down_cols, gate_rows, up_rows)
     )

time: 349 us -> 359 us (1.029)
  local copies, waits for them, and re-layouts: 22.7 us -> 42.5 us
  waiting for transfers between devices: 143 us -> 133 us
  starting transfers between devices: 37.6 us -> 28.4 us
  blocking collectives: 96.1 us -> 102 us
  other arithmetic: 10.3 us -> 15.7 us
    reshape x0 -> x4, local copies, waits for them, and re-layouts: none -> 13 us  [the longest x1 4.48 us: local(): down_cols = bundle[:, :rows_each].reshape(rep_count, hidden_width, chunk)]
    all_to_all x3 -> x1, starting transfers between devices: 15.8 us -> 5.01 us  [local(): bundle = lax.all_to_all(bundle, 'rep', 0, 0, tiled=True)]
    all_gather x1, waiting for transfers between devices: 9.68 us -> 1.53 us  [local(): chip_keys = lax.all_gather(packed[None], EP, axis=0, tiled=True)]
    slice x0 -> x1, local copies, waits for them, and re-layouts: none -> 5.5 us  [local(): up_rows = bundle[:, 2 * rows_each:].reshape(rep_count, chunk, hidden_width)]
    all_to_all x1, blocking collectives: 39.9 us -> 45.4 us  [local(): lax.all_to_all(spread, ('rep',) + EP, 0, 0, tiled=True).reshape(-1, chunk)]
    concatenate x0 -> x1, other arithmetic: none -> 5.35 us  [local(): jnp.concatenate([down_cols.reshape(rep_count, piece // 1024, 1024), w_gat...]
    all_to_all x3 -> x1, waiting for transfers between devices: 71.8 us -> 69.9 us  [local(): bundle = lax.all_to_all(bundle, 'rep', 0, 0, tiled=True)]
  transfers between devices with their start and end apart: 7 -> 5, of which waited for: 7 -> 5; matrix products, arithmetic and copies ran while one was open for 4% -> 11% of each run, Pallas kernels for 0% -> 0%
where the time goes in v12:
time: 359 us; the launch traced here: 358 us
  waiting for transfers between devices  133 us (37%)
  blocking collectives  102 us (28%)
  local copies, waits for them, and re-layouts  42.5 us (12%)
  starting transfers between devices  28.4 us (8%)
  matrix products  22.3 us (6%)
  other arithmetic  15.7 us (4%)
  between operations  14.5 us (4%)
    all_to_all x1, waiting for transfers between devices, local(): bundle = lax.all_to_all(bundle, 'rep', 0, 0, tiled=True)  69.9 us
    all_to_all x1, blocking collectives, local(): lax.all_to_all(spread, ('rep',) + EP, 0, 0, tiled=True).reshape(-1, chunk)  45.4 us
    all_to_all x1, blocking collectives, local(): parts = lax.all_to_all(parts, 'rep', 0, 0, tiled=True)  31.3 us
    all_to_all x1, waiting for transfers between devices, local(): back = lax.all_to_all(out_cols, ('rep',) + EP, 0, 0, tiled=True)  27.8 us
    all_to_all x1, waiting for transfers between devices, local(): lax.all_to_all(partial, 'epo', 0, 0, tiled=True).astype(jnp.float32)  22.5 us
    all_to_all x1, blocking collectives, local(): units_all = lax.all_to_all(unit_copies, 'rep', 0, 0, tiled=True)  17.4 us
    all_to_all x1, waiting for transfers between devices, local(): lax.all_to_all(outgoing, 'rep', split_axis=0, concat_axis=0, tiled=True)  11.1 us
    all_to_all x1, blocking collectives, local(): partial = jnp.sum(lax.all_to_all(partial, 'core', 0, 0, tiled=True), axis=0)  8.36 us
  transfers between devices with their start and end apart: 5, of which 5 were waited for; matrix products, arithmetic and copies ran while one was open for 11% of the time, Pallas kernels for 0%

profile of v12, /device:TPU:1, one launch (start us, length us, event | category | flops | bytes accessed | tf_op | source)
XLA Modules:
  0.0 358.4 jit_solution(12971011153437818731)
XLA Ops:
  6.6 0.8 constant_dynamic-slice_fusion
  7.7 0.2 fusion.42
  7.9 0.3 fusion
  8.2 0.5 broadcast.180
  8.7 1.1 reduce.6
  9.8 1.2 reshape.277
  11.0 7.5 %all-to-all-start = ((bf16[8,2,18432]{2,1,0:T(2,128)(2,1)}), bf16[8,2,18432]{2,1,0:T(2,128)(2,1)S(1)}, u32[]{:S(2)}, u32[]{:S(2)}) async-start(bf16[8,2,18432]{2,1,0:T(2,128)(2,1)} %reshape.277), calls=%async_computation | async-start | bytes 1179648 | tf_op jit(solution)/shard_map/all_to_all | solution.py:69
  18.6 0.8 dynamic_slice.13
  19.7 0.2 add_reduce_fusion
  19.8 11.1 %all-to-all-done = bf16[8,2,18432]{2,1,0:T(2,128)(2,1)S(1)} async-done(((bf16[8,2,18432]{2,1,0:T(2,128)(2,1)}), bf16[8,2,18432]{2,1,0:T(2,128)(2,1)S(1)}, u32[]{:S(2)}, u32[]{:S(2)}) %all-to-all-start) | async-done | bytes 589856 | tf_op jit(solution)/shard_map/all_to_all | solution.py:69
  30.9 0.6 reshape.278
  31.5 0.8 convolution_convert_fusion.1
  32.3 0.2 reshape.249
  32.5 0.8 maximum_maximum_fusion
  33.3 1.8 copy.139
  35.1 0.3 copy.149
  35.4 2.9 reshape.251
  38.3 4.0 %reshape_squeeze.16 = bf16[8,112,1024]{2,1,0:T(8,128)(2,1)} reshape(bf16[1,7168,128]{2,1,0:T(8,128)(2,1)} %param.27) | data formatting | bytes 3670016 | tf_op jit(solution)/shard_map/reshape;squeeze | solution.py:104
  42.3 3.9 %reshape_squeeze.17 = bf16[8,112,1024]{2,1,0:T(8,128)(2,1)} reshape(bf16[1,7168,128]{2,1,0:T(8,128)(2,1)} %param.28) | data formatting | bytes 3670016 | tf_op jit(solution)/shard_map/reshape;squeeze | solution.py:105
  46.2 5.4 %pad_maximum_fusion = bf16[8,336,1024]{2,1,0:T(8,128)(2,1)} fusion(bf16[8,112,1024]{2,1,0:T(8,128)(2,1)} %reshape_squeeze.17, bf16[8,112,1024]{2,1,0:T(8,128)(2,1)} %reshape_squeeze.16, bf16[8,112,1024]{2,1,0:T(8,128)(2,1)S(1)} %copy-done.2), kind=kLoop, calls=%fused_computation.10 | loop fusion | flops 16515072 | bytes 11010048 | tf_op jit(solution)/shard_map/concatenate | solution.py:101
  51.6 5.0 %all-to-all-start.1 = ((bf16[8,336,1024]{2,1,0:T(8,128)(2,1)}), bf16[8,336,1024]{2,1,0:T(8,128)(2,1)}, u32[]{:S(2)}, u32[]{:S(2)}) async-start(bf16[8,336,1024]{2,1,0:T(8,128)(2,1)} %pad_maximum_fusion), calls=%async_computation.1 | async-start | bytes 11010048 | tf_op jit(solution)/shard_map/all_to_all | solution.py:109
  57.6 0.2 copy.113
  57.8 3.9 %fusion.12 = pred[128,4608]{0,1:T(8,128)(4,1)S(1)} fusion(s32[4608]{0:T(1024)S(1)} %sub.25, pred[4608]{0:T(1024)(128)(4,1)S(1)} %and.68, pred[4608]{0:T(1024)(128)(4,1)S(1)} %and.66), kind=kLoop, calls=%fused_computation.22 | loop fusion | flops 1769472 | bytes 617472 | tf_op jit(solution)/shard_map/or | solution.py:124
  61.7 69.9 %all-to-all-done.1 = bf16[8,336,1024]{2,1,0:T(8,128)(2,1)} async-done(((bf16[8,336,1024]{2,1,0:T(8,128)(2,1)}), bf16[8,336,1024]{2,1,0:T(8,128)(2,1)}, u32[]{:S(2)}, u32[]{:S(2)}) %all-to-all-start.1) | async-done | bytes 5505056 | tf_op jit(solution)/shard_map/all_to_all | solution.py:109
  131.5 5.5 %fusion.58 = (bf16[8,112,1024]{2,1,0:T(8,128)(2,1)S(1)}, bf16[8,112,1024]{2,1,0:T(8,128)(2,1)}, bf16[8,112,1024]{2,1,0:T(8,128)(2,1)}) fusion(bf16[8,336,1024]{2,1,0:T(8,128)(2,1)} %all-to-all-done.1), kind=kLoop, calls=%fused_computation.93 | loop fusion | bytes 11010048 | tf_op jit(solution)/shard_map/slice | solution.py:113
  137.0 4.5 %reshape.252 = bf16[8,128,896]{2,1,0:T(8,128)(2,1)} reshape(bf16[8,112,1024]{2,1,0:T(8,128)(2,1)} %get-tuple-element.15) | data formatting | bytes 3670016 | tf_op jit(solution)/shard_map/reshape | solution.py:111
  141.5 3.9 %reshape.253 = bf16[8,896,128]{2,1,0:T(8,128)(2,1)} reshape(bf16[8,112,1024]{2,1,0:T(8,128)(2,1)} %get-tuple-element.14) | data formatting | bytes 3670016 | tf_op jit(solution)/shard_map/reshape | solution.py:112
  145.4 1.7 reshape.254
  147.1 1.5 all-gather.3.cloned.1.call-done
  148.7 4.7 %fusion.59 = (f32[2,128]{1,0:T(2,128)S(1)}, f32[2,128,4608]{1,2,0:T(8,128)S(1)}) fusion(bf16[4608,576,1]{1,0,2:T(8,128)(2,1)} %bitcast.109, bf16[128,2,576]{0,2,1:T(8,128)(2,1)S(1)} %bitcast.104, pred[128,4608]{0,1:T(8,128)(4,1)S(1)} %fusion.12), kind=kOutput, calls=%fused_computation.94 | convolution fusion | flops 1362493184 | bytes 10912768 | tf_op jit(solution)/shard_map/thc,kc->htk/dot_general | solution.py:127
  153.4 2.1 copy-done.3
  155.6 0.6 fusion.5
  156.2 5.5 %fusion.18 = bf16[128,2,128]{2,0,1:T(8,128)(2,1)S(1)} fusion(bf16[2,512,128]{2,1,0:T(8,128)(2,1)S(1)} %copy-done.13, f32[2,128,4608]{1,2,0:T(8,128)} %copy-done.3, f32[2,128]{1,0:T(2,128)S(1)} %get-tuple-element.16, bf16[4608,576]{1,0:T(8,128)(2,1)} %all-gather.3.cloned.1.call-done, f32[128,2]{0,1:T(2,128)S(1)} %bitcast.108), kind=kOutput, calls=%fused_computation.32 | convolution fusion | flops 1244168192 | bytes 9766912 | tf_op jit(solution)/shard_map/thc,hcv->thv/dot_general | solution.py:141
  161.9 2.7 fusion.7
  164.6 8.4 %all_to_all.40 = f32[2,64,7168]{2,1,0:T(8,128)} all-to-all(f32[2,64,7168]{2,1,0:T(8,128)S(1)} %fusion.7), channel_id=1, replica_groups=mesh['rep'=8,'epo'=16,'core'=2] {'core'}, dimensions={0} | all-to-all | bytes 7340032 | tf_op jit(solution)/shard_map/all_to_all | solution.py:148
  173.0 2.4 reduce_sum.84
  175.4 1.5 convert_element_type.103
  176.9 7.6 %all-to-all-start.3 = ((bf16[16,16,1792]{2,1,0:T(8,128)(2,1)}), bf16[16,16,1792]{2,1,0:T(8,128)(2,1)S(1)}, u32[]{:S(2)}, u32[]{:S(2)}) async-start(bf16[16,16,1792]{2,1,0:T(8,128)(2,1)} %convert_element_type.103), calls=%async_computation.3 | async-start | bytes 1835008 | tf_op jit(solution)/shard_map/all_to_all | solution.py:151
  184.8 0.2 select_reduce_fusion
  185.0 0.3 convolution_convert_fusion.6
  185.2 22.5 %all-to-all-done.3 = bf16[16,16,1792]{2,1,0:T(8,128)(2,1)S(1)} async-done(((bf16[16,16,1792]{2,1,0:T(8,128)(2,1)}), bf16[16,16,1792]{2,1,0:T(8,128)(2,1)S(1)}, u32[]{:S(2)}, u32[]{:S(2)}) %all-to-all-start.3) | async-done | bytes 917536 | tf_op jit(solution)/shard_map/all_to_all | solution.py:151
  207.7 0.1 convert_reduce_fusion.2
  207.9 0.1 multiply_reduce_fusion
  208.2 0.5 convolution_convert_fusion.2
  208.7 0.1 copy.140
  208.9 0.2 copy.120
  209.0 0.9 copy.121
  210.0 45.4 %all_to_all.41 = bf16[256,2,896]{2,1,0:T(2,128)(2,1)S(1)} all-to-all(bf16[256,2,896]{2,1,0:T(2,128)(2,1)S(1)} %copy.121), channel_id=1, replica_groups=mesh['rep'=8,'epo'=16,'core'=2] {'rep','epo','core'}, dimensions={0} | all-to-all | bytes 1835008 | tf_op jit(solution)/shard_map/all_to_all | solution.py:185
  255.4 1.3 reshape.273
  256.6 2.6 fusion.13
  259.3 1.3 fusion.14
  260.6 0.1 pad_maximum_fusion.1
  260.7 31.3 %all_to_all.42 = bf16[8,512,256]{1,2,0:T(8,128)(2,1)S(1)} all-to-all(bf16[8,512,256]{1,2,0:T(8,128)(2,1)S(1)} %pad_maximum_fusion.1), channel_id=1, replica_groups=mesh['rep'=8,'epo'=16,'core'=2] {'rep'}, dimensions={0} | all-to-all | bytes 4194304 | tf_op jit(solution)/shard_map/all_to_all | solution.py:189
  292.0 0.3 convert_reduce_fusion.1
  292.5 0.1 broadcast_in_dim.20
  292.7 17.4 %all_to_all.43 = bf16[8,512,128]{2,1,0:T(8,128)(2,1)S(1)} all-to-all(bf16[8,512,128]{2,1,0:T(8,128)(2,1)S(1)} %broadcast_in_dim.20), channel_id=1, replica_groups=mesh['rep'=8,'epo'=16,'core'=2] {'rep'}, dimensions={0} | all-to-all | bytes 2097152 | tf_op jit(solution)/shard_map/all_to_all | solution.py:195
  310.0 2.1 convert_reduce_fusion
  312.1 1.3 reshape.261
  313.4 8.3 %all-to-all-start.7 = ((bf16[256,2,896]{2,1,0:T(2,128)(2,1)}), bf16[256,2,896]{2,1,0:T(2,128)(2,1)S(1)}, u32[]{:S(2)}, u32[]{:S(2)}) async-start(bf16[256,2,896]{2,1,0:T(2,128)(2,1)} %reshape.261), calls=%async_computation.7 | async-start | bytes 1835008 | tf_op jit(solution)/shard_map/all_to_all | solution.py:200
  321.8 0.3 fusion.39
  322.0 27.8 %all-to-all-done.7 = bf16[256,2,896]{2,1,0:T(2,128)(2,1)S(1)} async-done(((bf16[256,2,896]{2,1,0:T(2,128)(2,1)}), bf16[256,2,896]{2,1,0:T(2,128)(2,1)S(1)}, u32[]{:S(2)}, u32[]{:S(2)}) %all-to-all-start.7) | async-done | bytes 917536 | tf_op jit(solution)/shard_map/all_to_all | solution.py:200
  349.9 0.3 copy.126
  350.2 0.1 copy.141
  350.4 1.1 fusion.1
  (64 shorter events, 2.1 us)
Async XLA Ops:
  6.5 1.4 copy-start
  6.5 12.9 %copy-start.11 = (bf16[1,2304]{1,0:T(2,128)(2,1)S(1)}, bf16[1,2304]{1,0:T(2,128)(2,1)}, u32[]{:S(2)}) copy-start(bf16[1,2304]{1,0:T(2,128)(2,1)} %param.16) | copy-start | bytes 13828
  11.0 19.9 %all-to-all-start = ((bf16[8,2,18432]{2,1,0:T(2,128)(2,1)}), bf16[8,2,18432]{2,1,0:T(2,128)(2,1)S(1)}, u32[]{:S(2)}, u32[]{:S(2)}) async-start(bf16[8,2,18432]{2,1,0:T(2,128)(2,1)} %reshape.277), calls=%async_computation | async-start | bytes 1179648 | tf_op jit(solution)/shard_map/all_to_all | solution.py:69
  18.5 130.1 %all-gather.3.cloned.1.call-start = ((), (), s32[]{:S(2)}) async-start(), calls=%async_computation.8 | async-start | bytes 6082560 | tf_op jit(solution)/shard_map/all_gather | solution.py:95
  38.3 7.9 %copy-start.2 = (bf16[8,112,1024]{2,1,0:T(8,128)(2,1)S(1)}, bf16[8,112,1024]{2,1,0:T(8,128)(2,1)}, u32[]{:S(2)}) copy-start(bf16[8,112,1024]{2,1,0:T(8,128)(2,1)} %reshape.251) | copy-start | bytes 5505028
  51.6 6.0 %copy-start.9 = (bf16[1,128,1152]{2,1,0:T(8,128)(2,1)S(1)}, bf16[1,128,1152]{2,1,0:T(8,128)(2,1)}, u32[]{:S(2)}) copy-start(bf16[1,128,1152]{2,1,0:T(8,128)(2,1)} %param.15) | copy-start | bytes 884740
  51.6 80.0 %all-to-all-start.1 = ((bf16[8,336,1024]{2,1,0:T(8,128)(2,1)}), bf16[8,336,1024]{2,1,0:T(8,128)(2,1)}, u32[]{:S(2)}, u32[]{:S(2)}) async-start(bf16[8,336,1024]{2,1,0:T(8,128)(2,1)} %pad_maximum_fusion), calls=%async_computation.1 | async-start | bytes 11010048 | tf_op jit(solution)/shard_map/all_to_all | solution.py:109
  153.4 2.2 copy-start.3
  153.4 2.8 copy-start.13
  173.0 11.5 %copy-start.8 = (bf16[1,4,7168]{2,1,0:T(4,128)(2,1)S(1)}, bf16[1,4,7168]{2,1,0:T(4,128)(2,1)}, u32[]{:S(2)}) copy-start(bf16[1,4,7168]{2,1,0:T(4,128)(2,1)} %param.21) | copy-start | bytes 172036
  173.0 11.6 %copy-start.12 = (s32[1,4,8]{2,1,0:T(4,128)S(1)}, s32[1,4,8]{2,1,0:T(4,128)}, u32[]{:S(2)}) copy-start(s32[1,4,8]{2,1,0:T(4,128)} %param.25) | copy-start | bytes 388
  173.0 11.8 %copy-start.10 = (bf16[7168]{0:T(1024)(128)(2,1)S(1)}, bf16[7168]{0:T(1024)(128)(2,1)}, u32[]{:S(2)}) copy-start(bf16[7168]{0:T(1024)(128)(2,1)} %param.24) | copy-start | bytes 43012
  176.9 30.8 %all-to-all-start.3 = ((bf16[16,16,1792]{2,1,0:T(8,128)(2,1)}), bf16[16,16,1792]{2,1,0:T(8,128)(2,1)S(1)}, u32[]{:S(2)}, u32[]{:S(2)}) async-start(bf16[16,16,1792]{2,1,0:T(8,128)(2,1)} %convert_element_type.103), calls=%async_computation.3 | async-start | bytes 1835008 | tf_op jit(solution)/shard_map/all_to_all | solution.py:151
  208.9 47.8 %copy-start.5 = (bf16[8,896,128]{2,1,0:T(8,128)(2,1)S(1)}, bf16[8,896,128]{2,1,0:T(8,128)(2,1)}, u32[]{:S(2)}) copy-start(bf16[8,896,128]{2,1,0:T(8,128)(2,1)} %reshape.253) | copy-start | bytes 5505028
  256.6 2.6 copy-start.6
  256.6 2.6 copy-start.7
  292.0 18.0 %copy-start.4 = (bf16[8,128,896]{2,1,0:T(8,128)(2,1)S(1)}, bf16[8,128,896]{2,1,0:T(8,128)(2,1)}, u32[]{:S(2)}) copy-start(bf16[8,128,896]{2,1,0:T(8,128)(2,1)} %reshape.252) | copy-start | bytes 5505028
  310.0 11.7 %copy-start.14 = (bf16[1,4,8]{2,1,0:T(4,128)(2,1)S(1)}, bf16[1,4,8]{2,1,0:T(4,128)(2,1)}, u32[]{:S(2)}) copy-start(bf16[1,4,8]{2,1,0:T(4,128)(2,1)} %param.26) | copy-start | bytes 196
  313.4 36.5 %all-to-all-start.7 = ((bf16[256,2,896]{2,1,0:T(2,128)(2,1)}), bf16[256,2,896]{2,1,0:T(2,128)(2,1)S(1)}, u32[]{:S(2)}, u32[]{:S(2)}) async-start(bf16[256,2,896]{2,1,0:T(2,128)(2,1)} %reshape.261), calls=%async_computation.7 | async-start | bytes 1835008 | tf_op jit(solution)/shard_map/all_to_all | solution.py:200
  321.7 29.8 %copy-start.1 = (bf16[1,8,36864]{2,1,0:T(8,128)(2,1)S(1)}, bf16[1,8,36864]{2,1,0:T(8,128)(2,1)}, u32[]{:S(2)}) copy-start(bf16[1,8,36864]{2,1,0:T(8,128)(2,1)} %param.17) | copy-start | bytes 1769476
Sparse Core Ops, SparseCore 0:
  33.4 115.2 all-gather.2

commit v13 on v11

--- a/solution.py
+++ b/solution.py
@@ -97,12 +97,9 @@
     chunk = width // rep_count
     down_cols = w_down[0].reshape(hidden_width, rep_count, chunk)
     down_cols = jnp.transpose(down_cols, (1, 0, 2))
-    down_cols = lax.all_to_all(down_cols, "rep", 0, 0, tiled=True)
     gate_rows = lax.all_to_all(w_gate[0].reshape(rep_count, chunk, hidden_width), "rep", 0, 0, tiled=True)
     up_rows = lax.all_to_all(w_up[0].reshape(rep_count, chunk, hidden_width), "rep", 0, 0, tiled=True)
-    chip_keys, down_cols, gate_rows, up_rows = lax.optimization_barrier(
-        (chip_keys, down_cols, gate_rows, up_rows)
-    )
+    chip_keys, gate_rows, up_rows = lax.optimization_barrier((chip_keys, gate_rows, up_rows))
     keys = chip_keys.reshape(-1, latent_width)
     device_of = lax.broadcasted_iota(jnp.int32, chip_keys.shape[:2], 0).reshape(-1)
     row_of = lax.broadcasted_iota(jnp.int32, chip_keys.shape[:2], 1).reshape(-1)
@@ -136,6 +133,8 @@
     partial = partial.reshape(core_count, SUF // core_count, -1)
     partial = jnp.sum(lax.all_to_all(partial, "core", 0, 0, tiled=True), axis=0)
     partial = partial.reshape(outer_count, 16, -1).astype(jnp.bfloat16)
+    partial, down_cols = lax.optimization_barrier((partial, down_cols))
+    down_cols = lax.all_to_all(down_cols, "rep", 0, 0, tiled=True)
     attention = jnp.sum(
         lax.all_to_all(partial, "epo", 0, 0, tiled=True).astype(jnp.float32), axis=0
     )
@@ -171,6 +170,7 @@
     width = grouped.shape[1]
     spread = grouped.reshape(expert_count, capacity, rep_count, chunk)
     spread = jnp.transpose(spread, (2, 0, 1, 3)).reshape(rep_count * expert_count, capacity, chunk)
+    spread, down_cols = lax.optimization_barrier((spread, down_cols))
     columns = lax.all_to_all(spread, ("rep",) + EP, 0, 0, tiled=True).reshape(-1, chunk)
     gate_part = jnp.einsum("nd,rdk->rnk", columns, gate_rows, preferred_element_type=jnp.float32)
     up_part = jnp.einsum("nd,rdk->rnk", columns, up_rows, preferred_element_type=jnp.float32)

time: 349 us -> 364 us (1.043)
  blocking collectives: 96.1 us -> 122 us
  waiting for transfers between devices: 143 us -> 137 us
  starting transfers between devices: 37.6 us -> 33.6 us
    all_to_all x0 -> x1, blocking collectives: none -> 28.9 us  [local(): lax.all_to_all(partial, 'epo', 0, 0, tiled=True).astype(jnp.float32)]
    all_to_all x1 -> x0, waiting for transfers between devices: 22.4 us -> none  [local(): lax.all_to_all(partial, 'epo', 0, 0, tiled=True).astype(jnp.float32)]
    all_gather x1, waiting for transfers between devices: 9.68 us -> 29.7 us  [local(): chip_keys = lax.all_gather(packed[None], EP, axis=0, tiled=True)]
    all_to_all x1 -> x0, starting transfers between devices: 5.99 us -> none  [local(): lax.all_to_all(partial, 'epo', 0, 0, tiled=True).astype(jnp.float32)]
  transfers between devices with their start and end apart: 7 -> 6, of which waited for: 7 -> 6; matrix products, arithmetic and copies ran while one was open for 4% -> 5% of each run, Pallas kernels for 0% -> 0%
where the time goes in v13:
time: 364 us; the launch traced here: 363 us
  waiting for transfers between devices  137 us (38%)
  blocking collectives  122 us (34%)
  starting transfers between devices  33.6 us (9%)
  matrix products  24.2 us (7%)
  local copies, waits for them, and re-layouts  21.5 us (6%)
  between operations  14.5 us (4%)
  other arithmetic  10.3 us (3%)
    all_to_all x1, blocking collectives, local(): lax.all_to_all(spread, ('rep',) + EP, 0, 0, tiled=True).reshape(-1, chunk)  36.7 us
    all_to_all x1, blocking collectives, local(): parts = lax.all_to_all(parts, 'rep', 0, 0, tiled=True)  31.3 us
    all_gather x1, waiting for transfers between devices, local(): chip_keys = lax.all_gather(packed[None], EP, axis=0, tiled=True)  29.7 us
    all_to_all x1, blocking collectives, local(): lax.all_to_all(partial, 'epo', 0, 0, tiled=True).astype(jnp.float32)  28.9 us
    all_to_all x1, waiting for transfers between devices, local(): back = lax.all_to_all(out_cols, ('rep',) + EP, 0, 0, tiled=True)  27.8 us
    all_to_all x1, waiting for transfers between devices, local(): down_cols = lax.all_to_all(down_cols, 'rep', 0, 0, tiled=True)  23.7 us
    all_to_all x1, waiting for transfers between devices, local(): lax.all_to_all(w_gate[0].reshape(rep_count, chunk, hidden_width), 'rep',...  23.1 us
    all_to_all x1, waiting for transfers between devices, local(): lax.all_to_all(w_up[0].reshape(rep_count, chunk, hidden_width), 'rep', 0,...  21.5 us
  transfers between devices with their start and end apart: 6, of which 6 were waited for; matrix products, arithmetic and copies ran while one was open for 5% of the time, Pallas kernels for 0%

profile of v13, /device:TPU:1, one launch (start us, length us, event | category | flops | bytes accessed | tf_op | source)
XLA Modules:
  0.0 362.8 jit_solution(8723230213256877883)
XLA Ops:
  6.6 0.8 constant_dynamic-slice_fusion
  7.6 0.1 copy.130
  7.7 0.2 fusion.42
  7.9 0.3 fusion
  8.2 0.5 broadcast.180
  8.7 1.1 reduce.6
  9.8 1.2 reshape.261
  11.0 7.5 %all-to-all-start = ((bf16[8,2,18432]{2,1,0:T(2,128)(2,1)}), bf16[8,2,18432]{2,1,0:T(2,128)(2,1)S(1)}, u32[]{:S(2)}, u32[]{:S(2)}) async-start(bf16[8,2,18432]{2,1,0:T(2,128)(2,1)} %reshape.261), calls=%async_computation | async-start | bytes 1179648 | tf_op jit(solution)/shard_map/all_to_all | solution.py:69
  18.6 0.8 dynamic_slice.13
  19.7 0.2 add_reduce_fusion
  19.8 11.1 %all-to-all-done = bf16[8,2,18432]{2,1,0:T(2,128)(2,1)S(1)} async-done(((bf16[8,2,18432]{2,1,0:T(2,128)(2,1)}), bf16[8,2,18432]{2,1,0:T(2,128)(2,1)S(1)}, u32[]{:S(2)}, u32[]{:S(2)}) %all-to-all-start) | async-done | bytes 589856 | tf_op jit(solution)/shard_map/all_to_all | solution.py:69
  30.9 0.6 reshape.262
  31.5 0.8 convolution_convert_fusion.1
  32.3 0.2 reshape.237
  32.5 0.8 maximum_maximum_fusion
  33.3 3.9 %copy.114 = bf16[8,896,128]{1,2,0:T(8,128)(2,1)} copy(bf16[8,896,128]{2,1,0:T(8,128)(2,1)} %bitcast.104) | data formatting | bytes 3670016 | tf_op jit(solution)/shard_map/reshape;squeeze | solution.py:100
  37.2 4.3 %all-to-all-start.1 = ((bf16[8,896,128]{1,2,0:T(8,128)(2,1)}), bf16[8,896,128]{1,2,0:T(8,128)(2,1)}, u32[]{:S(2)}, u32[]{:S(2)}) async-start(bf16[8,896,128]{1,2,0:T(8,128)(2,1)} %copy.114), calls=%async_computation.1 | async-start | bytes 3670016 | tf_op jit(solution)/shard_map/all_to_all | solution.py:100
  41.6 2.7 copy.115
  44.2 23.1 %all-to-all-done.1 = bf16[8,896,128]{1,2,0:T(8,128)(2,1)} async-done(((bf16[8,896,128]{1,2,0:T(8,128)(2,1)}), bf16[8,896,128]{1,2,0:T(8,128)(2,1)}, u32[]{:S(2)}, u32[]{:S(2)}) %all-to-all-start.1) | async-done | bytes 1835040 | tf_op jit(solution)/shard_map/all_to_all | solution.py:100
  67.4 6.8 %all-to-all-start.2 = ((bf16[8,896,128]{1,2,0:T(8,128)(2,1)}), bf16[8,896,128]{1,2,0:T(8,128)(2,1)}, u32[]{:S(2)}, u32[]{:S(2)}) async-start(bf16[8,896,128]{1,2,0:T(8,128)(2,1)} %copy.115), calls=%async_computation.2 | async-start | bytes 3670016 | tf_op jit(solution)/shard_map/all_to_all | solution.py:101
  75.2 0.2 copy.117
  75.4 0.3 copy.140
  75.7 1.5 copy.150
  77.3 3.8 %fusion.12 = pred[128,4608]{0,1:T(8,128)(4,1)S(1)} fusion(s32[4608]{0:T(1024)S(1)} %sub.25, pred[4608]{0:T(1024)(128)(4,1)S(1)} %and.68, pred[4608]{0:T(1024)(128)(4,1)S(1)} %and.66), kind=kLoop, calls=%fused_computation.21 | loop fusion | flops 1769472 | bytes 617472 | tf_op jit(solution)/shard_map/or | solution.py:110
  81.1 21.5 %all-to-all-done.2 = bf16[8,896,128]{1,2,0:T(8,128)(2,1)} async-done(((bf16[8,896,128]{1,2,0:T(8,128)(2,1)}), bf16[8,896,128]{1,2,0:T(8,128)(2,1)}, u32[]{:S(2)}, u32[]{:S(2)}) %all-to-all-start.2) | async-done | bytes 1835040 | tf_op jit(solution)/shard_map/all_to_all | solution.py:101
  102.7 29.7 %all-gather.3.cloned.1.call-done = bf16[4608,576]{1,0:T(8,128)(2,1)} async-done(((bf16[144,576]{1,0:T(8,128)(2,1)}), bf16[4608,576]{1,0:T(8,128)(2,1)}) %all-gather.3.cloned.1.call-update) | async-done | bytes 5308432 | tf_op jit(solution)/shard_map/all_gather | solution.py:95
  132.3 4.7 %fusion.58 = (f32[2,128]{1,0:T(2,128)S(1)}, f32[2,128,4608]{1,2,0:T(8,128)S(1)}) fusion(bf16[4608,576,1]{1,0,2:T(8,128)(2,1)} %bitcast.112, bf16[128,2,576]{0,2,1:T(8,128)(2,1)S(1)} %bitcast.107, pred[128,4608]{0,1:T(8,128)(4,1)S(1)} %fusion.12), kind=kOutput, calls=%fused_computation.92 | convolution fusion | flops 1362493184 | bytes 10912768 | tf_op jit(solution)/shard_map/thc,kc->htk/dot_general | solution.py:113
  137.1 2.1 copy-done.2
  139.3 0.6 fusion.5
  139.9 5.5 %fusion.18 = bf16[128,2,128]{2,0,1:T(8,128)(2,1)S(1)} fusion(bf16[2,512,128]{2,1,0:T(8,128)(2,1)S(1)} %copy-done.11, f32[2,128,4608]{1,2,0:T(8,128)} %copy-done.2, f32[2,128]{1,0:T(2,128)S(1)} %get-tuple-element.19, bf16[4608,576]{1,0:T(8,128)(2,1)} %all-gather.3.cloned.1.call-done, f32[128,2]{0,1:T(2,128)S(1)} %bitcast.111), kind=kOutput, calls=%fused_computation.31 | convolution fusion | flops 1244168192 | bytes 9766912 | tf_op jit(solution)/shard_map/thc,hcv->thv/dot_general | solution.py:127
  145.6 2.7 fusion.7
  148.3 7.6 %all_to_all.50 = f32[2,64,7168]{2,1,0:T(8,128)} all-to-all(f32[2,64,7168]{2,1,0:T(8,128)S(1)} %fusion.7), channel_id=1, replica_groups=mesh['rep'=8,'epo'=16,'core'=2] {'core'}, dimensions={0} | all-to-all | bytes 7340032 | tf_op jit(solution)/shard_map/all_to_all | solution.py:134
  155.9 2.4 reduce_sum.84
  158.3 0.6 convert_element_type.103
  159.0 28.9 %all_to_all.51 = bf16[16,16,1792]{2,1,0:T(8,128)(2,1)S(1)} all-to-all(bf16[16,16,1792]{2,1,0:T(8,128)(2,1)S(1)} %convert_element_type.103), channel_id=1, replica_groups=mesh['rep'=8,'epo'=16,'core'=2] {'epo'}, dimensions={0} | all-to-all | bytes 1835008 | tf_op jit(solution)/shard_map/all_to_all | solution.py:139
  187.9 6.7 %all-to-all-start.5 = ((bf16[8,128,896]{2,1,0:T(8,128)(2,1)}), bf16[8,128,896]{2,1,0:T(8,128)(2,1)S(1)}, u32[]{:S(2)}, u32[]{:S(2)}) async-start(bf16[8,128,896]{2,1,0:T(8,128)(2,1)} %bitcast.95), calls=%async_computation.5 | async-start | bytes 3670016 | tf_op jit(solution)/shard_map/all_to_all | solution.py:137
  194.8 0.2 select_reduce_fusion
  195.0 0.3 convolution_convert_fusion.6
  195.3 0.1 convert_reduce_fusion.2
  195.5 0.1 multiply_reduce_fusion
  195.7 0.1 reduce_sum.89
  195.8 0.5 convolution_convert_fusion.2
  196.3 0.1 copy.141
  196.4 0.2 copy.125
  196.6 23.7 %all-to-all-done.5 = bf16[8,128,896]{2,1,0:T(8,128)(2,1)S(1)} async-done(((bf16[8,128,896]{2,1,0:T(8,128)(2,1)}), bf16[8,128,896]{2,1,0:T(8,128)(2,1)S(1)}, u32[]{:S(2)}, u32[]{:S(2)}) %all-to-all-start.5) | async-done | bytes 1835040 | tf_op jit(solution)/shard_map/all_to_all | solution.py:137
  220.3 0.9 copy.126
  221.2 36.7 %all_to_all.52 = bf16[256,2,896]{2,1,0:T(2,128)(2,1)S(1)} all-to-all(bf16[256,2,896]{2,1,0:T(2,128)(2,1)S(1)} %copy.126), channel_id=1, replica_groups=mesh['rep'=8,'epo'=16,'core'=2] {'rep','epo','core'}, dimensions={0} | all-to-all | bytes 1835008 | tf_op jit(solution)/shard_map/all_to_all | solution.py:174
  257.9 1.3 reshape.257
  259.2 3.1 fusion.13
  262.3 2.8 fusion.14
  265.0 0.1 pad_maximum_fusion
  265.2 31.3 %all_to_all.53 = bf16[8,512,256]{1,2,0:T(8,128)(2,1)S(1)} all-to-all(bf16[8,512,256]{1,2,0:T(8,128)(2,1)S(1)} %pad_maximum_fusion), channel_id=1, replica_groups=mesh['rep'=8,'epo'=16,'core'=2] {'rep'}, dimensions={0} | all-to-all | bytes 4194304 | tf_op jit(solution)/shard_map/all_to_all | solution.py:178
  296.4 0.3 convert_reduce_fusion.1
  296.8 0.1 copy.127
  297.0 0.1 broadcast_in_dim.20
  297.1 17.4 %all_to_all.54 = bf16[8,512,128]{2,1,0:T(8,128)(2,1)S(1)} all-to-all(bf16[8,512,128]{2,1,0:T(8,128)(2,1)S(1)} %broadcast_in_dim.20), channel_id=1, replica_groups=mesh['rep'=8,'epo'=16,'core'=2] {'rep'}, dimensions={0} | all-to-all | bytes 2097152 | tf_op jit(solution)/shard_map/all_to_all | solution.py:184
  314.5 2.1 convert_reduce_fusion
  316.5 1.3 reshape.245
  317.8 8.3 %all-to-all-start.9 = ((bf16[256,2,896]{2,1,0:T(2,128)(2,1)}), bf16[256,2,896]{2,1,0:T(2,128)(2,1)S(1)}, u32[]{:S(2)}, u32[]{:S(2)}) async-start(bf16[256,2,896]{2,1,0:T(2,128)(2,1)} %reshape.245), calls=%async_computation.9 | async-start | bytes 1835008 | tf_op jit(solution)/shard_map/all_to_all | solution.py:189
  326.2 0.3 fusion.39
  326.5 27.8 %all-to-all-done.9 = bf16[256,2,896]{2,1,0:T(2,128)(2,1)S(1)} async-done(((bf16[256,2,896]{2,1,0:T(2,128)(2,1)}), bf16[256,2,896]{2,1,0:T(2,128)(2,1)S(1)}, u32[]{:S(2)}, u32[]{:S(2)}) %all-to-all-start.9) | async-done | bytes 917536 | tf_op jit(solution)/shard_map/all_to_all | solution.py:189
  354.4 0.3 copy.129
  354.7 0.1 copy.142
  354.8 1.1 fusion.1
  (57 shorter events, 1.8 us)
Async XLA Ops:
  6.5 1.4 copy-start
  6.5 12.9 %copy-start.9 = (bf16[1,2304]{1,0:T(2,128)(2,1)S(1)}, bf16[1,2304]{1,0:T(2,128)(2,1)}, u32[]{:S(2)}) copy-start(bf16[1,2304]{1,0:T(2,128)(2,1)} %param.16) | copy-start | bytes 13828
  11.0 19.9 %all-to-all-start = ((bf16[8,2,18432]{2,1,0:T(2,128)(2,1)}), bf16[8,2,18432]{2,1,0:T(2,128)(2,1)S(1)}, u32[]{:S(2)}, u32[]{:S(2)}) async-start(bf16[8,2,18432]{2,1,0:T(2,128)(2,1)} %reshape.261), calls=%async_computation | async-start | bytes 1179648 | tf_op jit(solution)/shard_map/all_to_all | solution.py:69
  18.5 113.8 %all-gather.3.cloned.1.call-start = ((), (), s32[]{:S(2)}) async-start(), calls=%async_computation.10 | async-start | bytes 6082560 | tf_op jit(solution)/shard_map/all_gather | solution.py:95
  33.2 8.3 %copy-start.3 = (bf16[1,7168,128]{2,1,0:T(8,128)(2,1)S(1)}, bf16[1,7168,128]{2,1,0:T(8,128)(2,1)}, u32[]{:S(2)}) copy-start(bf16[1,7168,128]{2,1,0:T(8,128)(2,1)} %param.28) | copy-start | bytes 5505028
  37.2 30.2 %all-to-all-start.1 = ((bf16[8,896,128]{1,2,0:T(8,128)(2,1)}), bf16[8,896,128]{1,2,0:T(8,128)(2,1)}, u32[]{:S(2)}, u32[]{:S(2)}) async-start(bf16[8,896,128]{1,2,0:T(8,128)(2,1)} %copy.114), calls=%async_computation.1 | async-start | bytes 3670016 | tf_op jit(solution)/shard_map/all_to_all | solution.py:100
  41.5 33.6 %copy-start.7 = (bf16[1,128,1152]{2,1,0:T(8,128)(2,1)S(1)}, bf16[1,128,1152]{2,1,0:T(8,128)(2,1)}, u32[]{:S(2)}) copy-start(bf16[1,128,1152]{2,1,0:T(8,128)(2,1)} %param.15) | copy-start | bytes 884740
  44.2 31.2 %copy-start.4 = (bf16[1,128,7168]{2,1,0:T(8,128)(2,1)S(1)}, bf16[1,128,7168]{2,1,0:T(8,128)(2,1)}, u32[]{:S(2)}) copy-start(bf16[1,128,7168]{2,1,0:T(8,128)(2,1)} %param.29) | copy-start | bytes 5505028
  67.4 35.3 %all-to-all-start.2 = ((bf16[8,896,128]{1,2,0:T(8,128)(2,1)}), bf16[8,896,128]{1,2,0:T(8,128)(2,1)}, u32[]{:S(2)}, u32[]{:S(2)}) async-start(bf16[8,896,128]{1,2,0:T(8,128)(2,1)} %copy.115), calls=%async_computation.2 | async-start | bytes 3670016 | tf_op jit(solution)/shard_map/all_to_all | solution.py:101
  137.1 2.2 copy-start.2
  137.1 2.8 copy-start.11
  158.3 36.2 %copy-start.6 = (bf16[1,4,7168]{2,1,0:T(4,128)(2,1)S(1)}, bf16[1,4,7168]{2,1,0:T(4,128)(2,1)}, u32[]{:S(2)}) copy-start(bf16[1,4,7168]{2,1,0:T(4,128)(2,1)} %param.21) | copy-start | bytes 172036
  158.3 36.3 %copy-start.10 = (s32[1,4,8]{2,1,0:T(4,128)S(1)}, s32[1,4,8]{2,1,0:T(4,128)}, u32[]{:S(2)}) copy-start(s32[1,4,8]{2,1,0:T(4,128)} %param.25) | copy-start | bytes 388
  158.3 36.5 %copy-start.8 = (bf16[7168]{0:T(1024)(128)(2,1)S(1)}, bf16[7168]{0:T(1024)(128)(2,1)}, u32[]{:S(2)}) copy-start(bf16[7168]{0:T(1024)(128)(2,1)} %param.24) | copy-start | bytes 43012
  187.9 32.4 %all-to-all-start.5 = ((bf16[8,128,896]{2,1,0:T(8,128)(2,1)}), bf16[8,128,896]{2,1,0:T(8,128)(2,1)S(1)}, u32[]{:S(2)}, u32[]{:S(2)}) async-start(bf16[8,128,896]{2,1,0:T(8,128)(2,1)} %bitcast.95), calls=%async_computation.5 | async-start | bytes 3670016 | tf_op jit(solution)/shard_map/all_to_all | solution.py:137
  259.2 3.1 copy-start.5
  314.5 11.6 %copy-start.12 = (bf16[1,4,8]{2,1,0:T(4,128)(2,1)S(1)}, bf16[1,4,8]{2,1,0:T(4,128)(2,1)}, u32[]{:S(2)}) copy-start(bf16[1,4,8]{2,1,0:T(4,128)(2,1)} %param.26) | copy-start | bytes 196
  317.8 36.5 %all-to-all-start.9 = ((bf16[256,2,896]{2,1,0:T(2,128)(2,1)}), bf16[256,2,896]{2,1,0:T(2,128)(2,1)S(1)}, u32[]{:S(2)}, u32[]{:S(2)}) async-start(bf16[256,2,896]{2,1,0:T(2,128)(2,1)} %reshape.245), calls=%async_computation.9 | async-start | bytes 1835008 | tf_op jit(solution)/shard_map/all_to_all | solution.py:189
  326.1 29.8 %copy-start.1 = (bf16[1,8,36864]{2,1,0:T(8,128)(2,1)S(1)}, bf16[1,8,36864]{2,1,0:T(8,128)(2,1)}, u32[]{:S(2)}) copy-start(bf16[1,8,36864]{2,1,0:T(8,128)(2,1)} %param.17) | copy-start | bytes 1769476
Sparse Core Ops, SparseCore 0:
  33.4 98.9 all-gather.2

commit v14 on v11

--- a/solution.py
+++ b/solution.py
@@ -134,7 +134,8 @@
     head_values = jnp.transpose(head_values, (1, 0, 2, 3)).reshape(SUF, -1)
     partial = jnp.dot(head_values, w_out, preferred_element_type=jnp.float32)
     partial = partial.reshape(core_count, SUF // core_count, -1)
-    partial = jnp.sum(lax.all_to_all(partial, "core", 0, 0, tiled=True), axis=0)
+    partial = lax.all_to_all(partial.astype(jnp.bfloat16), "core", 0, 0, tiled=True)
+    partial = jnp.sum(partial.astype(jnp.float32), axis=0)
     partial = partial.reshape(outer_count, 16, -1).astype(jnp.bfloat16)
     attention = jnp.sum(
         lax.all_to_all(partial, "epo", 0, 0, tiled=True).astype(jnp.float32), axis=0

time: 349 us -> 344 us (0.986)
  transfers between devices with their start and end apart: 7 -> 7, of which waited for: 7 -> 7; matrix products, arithmetic and copies ran while one was open for 4% -> 5% of each run, Pallas kernels for 0% -> 0%
where the time goes in v14:
time: 344 us; the launch traced here: 343 us
  waiting for transfers between devices  143 us (42%)
  blocking collectives  93.1 us (27%)
  starting transfers between devices  38 us (11%)
  matrix products  24.1 us (7%)
  local copies, waits for them, and re-layouts  21.1 us (6%)
  between operations  14.5 us (4%)
  other arithmetic  8.76 us (3%)
    all_to_all x1, blocking collectives, local(): lax.all_to_all(spread, ('rep',) + EP, 0, 0, tiled=True).reshape(-1, chunk)  39.4 us
    all_to_all x1, blocking collectives, local(): parts = lax.all_to_all(parts, 'rep', 0, 0, tiled=True)  31.2 us
    all_to_all x1, waiting for transfers between devices, local(): back = lax.all_to_all(out_cols, ('rep',) + EP, 0, 0, tiled=True)  27.8 us
    all_to_all x1, waiting for transfers between devices, local(): lax.all_to_all(w_gate[0].reshape(rep_count, chunk, hidden_width), 'rep',...  25.9 us
    all_to_all x1, waiting for transfers between devices, local(): down_cols = lax.all_to_all(down_cols, 'rep', 0, 0, tiled=True)  23.2 us
    all_to_all x1, waiting for transfers between devices, local(): lax.all_to_all(w_up[0].reshape(rep_count, chunk, hidden_width), 'rep', 0,...  22.9 us
    all_to_all x1, waiting for transfers between devices, local(): lax.all_to_all(partial, 'epo', 0, 0, tiled=True).astype(jnp.float32)  22.5 us
    all_to_all x1, blocking collectives, local(): units_all = lax.all_to_all(unit_copies, 'rep', 0, 0, tiled=True)  17.4 us
  transfers between devices with their start and end apart: 7, of which 7 were waited for; matrix products, arithmetic and copies ran while one was open for 5% of the time, Pallas kernels for 0%

profile of v14, /device:TPU:1, one launch (start us, length us, event | category | flops | bytes accessed | tf_op | source)
XLA Modules:
  0.0 342.8 jit_solution(10226278535675166483)
XLA Ops:
  6.5 0.8 constant_dynamic-slice_fusion
  7.7 0.2 fusion.41
  7.9 0.3 fusion
  8.2 0.5 broadcast.180
  8.7 1.1 reduce.7
  9.8 1.2 reshape.261
  11.0 7.5 %all-to-all-start = ((bf16[8,2,18432]{2,1,0:T(2,128)(2,1)}), bf16[8,2,18432]{2,1,0:T(2,128)(2,1)S(1)}, u32[]{:S(2)}, u32[]{:S(2)}) async-start(bf16[8,2,18432]{2,1,0:T(2,128)(2,1)} %reshape.261), calls=%async_computation | async-start | bytes 1179648 | tf_op jit(solution)/shard_map/all_to_all | solution.py:69
  18.6 0.8 dynamic_slice.13
  19.6 0.2 add_reduce_fusion
  19.8 11.1 %all-to-all-done = bf16[8,2,18432]{2,1,0:T(2,128)(2,1)S(1)} async-done(((bf16[8,2,18432]{2,1,0:T(2,128)(2,1)}), bf16[8,2,18432]{2,1,0:T(2,128)(2,1)S(1)}, u32[]{:S(2)}, u32[]{:S(2)}) %all-to-all-start) | async-done | bytes 589856 | tf_op jit(solution)/shard_map/all_to_all | solution.py:69
  30.9 0.6 reshape.262
  31.5 0.8 convolution_convert_fusion.1
  32.3 0.2 reshape.237
  32.5 0.8 maximum_maximum_fusion
  33.2 1.8 copy.140
  35.1 1.6 copy.150
  36.7 4.4 %all-to-all-start.1 = ((bf16[8,128,896]{2,1,0:T(8,128)(2,1)}), bf16[8,128,896]{2,1,0:T(8,128)(2,1)}, u32[]{:S(2)}, u32[]{:S(2)}) async-start(bf16[8,128,896]{2,1,0:T(8,128)(2,1)} %bitcast.95), calls=%async_computation.1 | async-start | bytes 3670016 | tf_op jit(solution)/shard_map/all_to_all | solution.py:100
  41.1 2.7 copy.115
  43.8 23.2 %all-to-all-done.1 = bf16[8,128,896]{2,1,0:T(8,128)(2,1)} async-done(((bf16[8,128,896]{2,1,0:T(8,128)(2,1)}), bf16[8,128,896]{2,1,0:T(8,128)(2,1)}, u32[]{:S(2)}, u32[]{:S(2)}) %all-to-all-start.1) | async-done | bytes 1835040 | tf_op jit(solution)/shard_map/all_to_all | solution.py:100
  67.0 6.8 %all-to-all-start.2 = ((bf16[8,896,128]{1,2,0:T(8,128)(2,1)}), bf16[8,896,128]{1,2,0:T(8,128)(2,1)}, u32[]{:S(2)}, u32[]{:S(2)}) async-start(bf16[8,896,128]{1,2,0:T(8,128)(2,1)} %copy.115), calls=%async_computation.2 | async-start | bytes 3670016 | tf_op jit(solution)/shard_map/all_to_all | solution.py:101
  73.8 2.7 copy.116
  76.5 25.9 %all-to-all-done.2 = bf16[8,896,128]{1,2,0:T(8,128)(2,1)} async-done(((bf16[8,896,128]{1,2,0:T(8,128)(2,1)}), bf16[8,896,128]{1,2,0:T(8,128)(2,1)}, u32[]{:S(2)}, u32[]{:S(2)}) %all-to-all-start.2) | async-done | bytes 1835040 | tf_op jit(solution)/shard_map/all_to_all | solution.py:101
  102.3 4.4 %all-to-all-start.3 = ((bf16[8,896,128]{1,2,0:T(8,128)(2,1)}), bf16[8,896,128]{1,2,0:T(8,128)(2,1)S(1)}, u32[]{:S(2)}, u32[]{:S(2)}) async-start(bf16[8,896,128]{1,2,0:T(8,128)(2,1)} %copy.116), calls=%async_computation.3 | async-start | bytes 3670016 | tf_op jit(solution)/shard_map/all_to_all | solution.py:102
  107.8 0.2 copy.118
  108.0 3.9 %fusion.11 = pred[128,4608]{0,1:T(8,128)(4,1)S(1)} fusion(s32[4608]{0:T(1024)S(1)} %sub.25, pred[4608]{0:T(1024)(128)(4,1)S(1)} %and.68, pred[4608]{0:T(1024)(128)(4,1)S(1)} %and.66), kind=kLoop, calls=%fused_computation.21 | loop fusion | flops 1769472 | bytes 617472 | tf_op jit(solution)/shard_map/or | solution.py:113
  111.9 22.9 %all-to-all-done.3 = bf16[8,896,128]{1,2,0:T(8,128)(2,1)S(1)} async-done(((bf16[8,896,128]{1,2,0:T(8,128)(2,1)}), bf16[8,896,128]{1,2,0:T(8,128)(2,1)S(1)}, u32[]{:S(2)}, u32[]{:S(2)}) %all-to-all-start.3) | async-done | bytes 1835040 | tf_op jit(solution)/shard_map/all_to_all | solution.py:102
  134.8 9.8 %all-gather.3.cloned.1.call-done = bf16[4608,576]{1,0:T(8,128)(2,1)} async-done(((bf16[144,576]{1,0:T(8,128)(2,1)}), bf16[4608,576]{1,0:T(8,128)(2,1)}) %all-gather.3.cloned.1.call-update) | async-done | bytes 5308432 | tf_op jit(solution)/shard_map/all_gather | solution.py:95
  144.6 4.7 %fusion.57 = (f32[2,128]{1,0:T(2,128)S(1)}, f32[2,128,4608]{1,2,0:T(8,128)S(1)}) fusion(bf16[4608,576,1]{1,0,2:T(8,128)(2,1)} %bitcast.112, bf16[128,2,576]{0,2,1:T(8,128)(2,1)S(1)} %bitcast.107, pred[128,4608]{0,1:T(8,128)(4,1)S(1)} %fusion.11), kind=kOutput, calls=%fused_computation.92 | convolution fusion | flops 1362493184 | bytes 10912768 | tf_op jit(solution)/shard_map/thc,kc->htk/dot_general | solution.py:116
  149.3 0.6 fusion.5
  150.0 1.5 copy-done.1
  151.5 5.5 %fusion.17 = bf16[128,2,128]{2,0,1:T(8,128)(2,1)S(1)} fusion(bf16[2,512,128]{2,1,0:T(8,128)(2,1)S(1)} %copy-done.11, f32[2,128,4608]{1,2,0:T(8,128)} %copy-done.1, f32[2,128]{1,0:T(2,128)S(1)} %get-tuple-element.13, bf16[4608,576]{1,0:T(8,128)(2,1)} %all-gather.3.cloned.1.call-done, f32[128,2]{0,1:T(2,128)S(1)} %bitcast.111), kind=kOutput, calls=%fused_computation.31 | convolution fusion | flops 1244168192 | bytes 9766912 | tf_op jit(solution)/shard_map/thc,hcv->thv/dot_general | solution.py:130
  157.2 2.7 convolution_convert_fusion.2
  159.9 5.2 %all_to_all.50 = bf16[2,64,7168]{2,1,0:T(8,128)(2,1)S(1)} all-to-all(bf16[2,64,7168]{2,1,0:T(8,128)(2,1)S(1)} %convolution_convert_fusion.2), channel_id=1, replica_groups=mesh['rep'=8,'epo'=16,'core'=2] {'core'}, dimensions={0} | all-to-all | bytes 3670016 | tf_op jit(solution)/shard_map/all_to_all | solution.py:137
  165.0 0.8 reduce_sum.87
  165.9 1.5 convert_element_type.105
  167.4 6.4 %all-to-all-start.5 = ((bf16[16,16,1792]{2,1,0:T(8,128)(2,1)}), bf16[16,16,1792]{2,1,0:T(8,128)(2,1)S(1)}, u32[]{:S(2)}, u32[]{:S(2)}) async-start(bf16[16,16,1792]{2,1,0:T(8,128)(2,1)} %convert_element_type.105), calls=%async_computation.5 | async-start | bytes 1835008 | tf_op jit(solution)/shard_map/all_to_all | solution.py:141
  174.2 0.2 select_reduce_fusion
  174.4 0.3 convolution_convert_fusion.7
  174.6 22.5 %all-to-all-done.5 = bf16[16,16,1792]{2,1,0:T(8,128)(2,1)S(1)} async-done(((bf16[16,16,1792]{2,1,0:T(8,128)(2,1)}), bf16[16,16,1792]{2,1,0:T(8,128)(2,1)S(1)}, u32[]{:S(2)}, u32[]{:S(2)}) %all-to-all-start.5) | async-done | bytes 917536 | tf_op jit(solution)/shard_map/all_to_all | solution.py:141
  197.2 0.1 convert_reduce_fusion.2
  197.4 0.1 multiply_reduce_fusion
  197.6 0.1 reduce_sum.92
  197.7 0.5 convolution_convert_fusion.3
  198.2 0.1 copy.141
  198.4 0.2 copy.125
  198.5 0.9 copy.126
  199.5 39.4 %all_to_all.51 = bf16[256,2,896]{2,1,0:T(2,128)(2,1)S(1)} all-to-all(bf16[256,2,896]{2,1,0:T(2,128)(2,1)S(1)} %copy.126), channel_id=1, replica_groups=mesh['rep'=8,'epo'=16,'core'=2] {'rep','epo','core'}, dimensions={0} | all-to-all | bytes 1835008 | tf_op jit(solution)/shard_map/all_to_all | solution.py:175
  238.8 0.3 reshape.257
  239.2 2.9 fusion.12
  242.1 1.3 fusion.13
  243.4 0.1 pad_maximum_fusion
  243.6 31.2 %all_to_all.52 = bf16[8,512,256]{1,2,0:T(8,128)(2,1)S(1)} all-to-all(bf16[8,512,256]{1,2,0:T(8,128)(2,1)S(1)} %pad_maximum_fusion), channel_id=1, replica_groups=mesh['rep'=8,'epo'=16,'core'=2] {'rep'}, dimensions={0} | all-to-all | bytes 4194304 | tf_op jit(solution)/shard_map/all_to_all | solution.py:179
  274.8 0.3 convert_reduce_fusion.1
  275.2 0.1 copy.127
  275.3 0.1 broadcast_in_dim.20
  275.5 17.4 %all_to_all.53 = bf16[8,512,128]{2,1,0:T(8,128)(2,1)S(1)} all-to-all(bf16[8,512,128]{2,1,0:T(8,128)(2,1)S(1)} %broadcast_in_dim.20), channel_id=1, replica_groups=mesh['rep'=8,'epo'=16,'core'=2] {'rep'}, dimensions={0} | all-to-all | bytes 2097152 | tf_op jit(solution)/shard_map/all_to_all | solution.py:185
  292.8 3.6 %convert_reduce_fusion = bf16[512,896]{1,0:T(8,128)(2,1)S(1)} fusion(bf16[8,512,128]{2,1,0:T(8,128)(2,1)S(1)} %all_to_all.53, bf16[8,128,896]{2,1,0:T(8,128)(2,1)} %all-to-all-done.1), kind=kOutput, calls=%fused_computation.7 | convolution fusion | flops 946405376 | bytes 3801088 | tf_op jit(solution)/shard_map/rnk,rkc->rnc/dot_general | solution.py:186
  296.5 1.3 reshape.245
  297.8 8.3 %all-to-all-start.9 = ((bf16[256,2,896]{2,1,0:T(2,128)(2,1)}), bf16[256,2,896]{2,1,0:T(2,128)(2,1)S(1)}, u32[]{:S(2)}, u32[]{:S(2)}) async-start(bf16[256,2,896]{2,1,0:T(2,128)(2,1)} %reshape.245), calls=%async_computation.9 | async-start | bytes 1835008 | tf_op jit(solution)/shard_map/all_to_all | solution.py:190
  306.2 0.3 fusion.38
  306.4 27.8 %all-to-all-done.9 = bf16[256,2,896]{2,1,0:T(2,128)(2,1)S(1)} async-done(((bf16[256,2,896]{2,1,0:T(2,128)(2,1)}), bf16[256,2,896]{2,1,0:T(2,128)(2,1)S(1)}, u32[]{:S(2)}, u32[]{:S(2)}) %all-to-all-start.9) | async-done | bytes 917536 | tf_op jit(solution)/shard_map/all_to_all | solution.py:190
  334.4 0.3 copy.129
  334.6 0.1 copy.142
  334.8 1.1 fusion.1
  (58 shorter events, 1.9 us)
Async XLA Ops:
  6.5 1.3 copy-start
  7.9 11.6 %copy-start.9 = (bf16[1,2304]{1,0:T(2,128)(2,1)S(1)}, bf16[1,2304]{1,0:T(2,128)(2,1)}, u32[]{:S(2)}) copy-start(bf16[1,2304]{1,0:T(2,128)(2,1)} %param.16) | copy-start | bytes 13828
  11.0 19.9 %all-to-all-start = ((bf16[8,2,18432]{2,1,0:T(2,128)(2,1)}), bf16[8,2,18432]{2,1,0:T(2,128)(2,1)S(1)}, u32[]{:S(2)}, u32[]{:S(2)}) async-start(bf16[8,2,18432]{2,1,0:T(2,128)(2,1)} %reshape.261), calls=%async_computation | async-start | bytes 1179648 | tf_op jit(solution)/shard_map/all_to_all | solution.py:69
  18.5 126.0 %all-gather.3.cloned.1.call-start = ((), (), s32[]{:S(2)}) async-start(), calls=%async_computation.10 | async-start | bytes 6082560 | tf_op jit(solution)/shard_map/all_gather | solution.py:95
  36.7 4.5 %copy-start.2 = (bf16[1,7168,128]{2,1,0:T(8,128)(2,1)S(1)}, bf16[1,7168,128]{2,1,0:T(8,128)(2,1)}, u32[]{:S(2)}) copy-start(bf16[1,7168,128]{2,1,0:T(8,128)(2,1)} %param.27) | copy-start | bytes 5505028
  36.7 30.3 %all-to-all-start.1 = ((bf16[8,128,896]{2,1,0:T(8,128)(2,1)}), bf16[8,128,896]{2,1,0:T(8,128)(2,1)}, u32[]{:S(2)}, u32[]{:S(2)}) async-start(bf16[8,128,896]{2,1,0:T(8,128)(2,1)} %bitcast.95), calls=%async_computation.1 | async-start | bytes 3670016 | tf_op jit(solution)/shard_map/all_to_all | solution.py:100
  43.8 30.0 %copy-start.3 = (bf16[1,7168,128]{2,1,0:T(8,128)(2,1)S(1)}, bf16[1,7168,128]{2,1,0:T(8,128)(2,1)}, u32[]{:S(2)}) copy-start(bf16[1,7168,128]{2,1,0:T(8,128)(2,1)} %param.28) | copy-start | bytes 5505028
  67.0 35.4 %all-to-all-start.2 = ((bf16[8,896,128]{1,2,0:T(8,128)(2,1)}), bf16[8,896,128]{1,2,0:T(8,128)(2,1)}, u32[]{:S(2)}, u32[]{:S(2)}) async-start(bf16[8,896,128]{1,2,0:T(8,128)(2,1)} %copy.115), calls=%async_computation.2 | async-start | bytes 3670016 | tf_op jit(solution)/shard_map/all_to_all | solution.py:101
  76.5 31.3 %copy-start.7 = (bf16[1,128,1152]{2,1,0:T(8,128)(2,1)S(1)}, bf16[1,128,1152]{2,1,0:T(8,128)(2,1)}, u32[]{:S(2)}) copy-start(bf16[1,128,1152]{2,1,0:T(8,128)(2,1)} %param.15) | copy-start | bytes 884740
  102.3 32.4 %all-to-all-start.3 = ((bf16[8,896,128]{1,2,0:T(8,128)(2,1)}), bf16[8,896,128]{1,2,0:T(8,128)(2,1)S(1)}, u32[]{:S(2)}, u32[]{:S(2)}) async-start(bf16[8,896,128]{1,2,0:T(8,128)(2,1)} %copy.116), calls=%async_computation.3 | async-start | bytes 3670016 | tf_op jit(solution)/shard_map/all_to_all | solution.py:102
  134.8 14.5 %copy-start.4 = (bf16[8,896,128]{1,2,0:T(8,128)(2,1)}, bf16[8,896,128]{1,2,0:T(8,128)(2,1)S(1)}, u32[]{:S(2)}) copy-start(bf16[8,896,128]{1,2,0:T(8,128)(2,1)S(1)} %all-to-all-done.3) | copy-start | bytes 5505028
  149.3 2.2 copy-start.1
  149.3 2.2 copy-start.11
  165.9 8.0 %copy-start.6 = (bf16[1,4,7168]{2,1,0:T(4,128)(2,1)S(1)}, bf16[1,4,7168]{2,1,0:T(4,128)(2,1)}, u32[]{:S(2)}) copy-start(bf16[1,4,7168]{2,1,0:T(4,128)(2,1)} %param.21) | copy-start | bytes 172036
  165.9 8.1 %copy-start.10 = (s32[1,4,8]{2,1,0:T(4,128)S(1)}, s32[1,4,8]{2,1,0:T(4,128)}, u32[]{:S(2)}) copy-start(s32[1,4,8]{2,1,0:T(4,128)} %param.25) | copy-start | bytes 388
  165.9 8.3 %copy-start.8 = (bf16[7168]{0:T(1024)(128)(2,1)S(1)}, bf16[7168]{0:T(1024)(128)(2,1)}, u32[]{:S(2)}) copy-start(bf16[7168]{0:T(1024)(128)(2,1)} %param.24) | copy-start | bytes 43012
  167.4 29.7 %all-to-all-start.5 = ((bf16[16,16,1792]{2,1,0:T(8,128)(2,1)}), bf16[16,16,1792]{2,1,0:T(8,128)(2,1)S(1)}, u32[]{:S(2)}, u32[]{:S(2)}) async-start(bf16[16,16,1792]{2,1,0:T(8,128)(2,1)} %convert_element_type.105), calls=%async_computation.5 | async-start | bytes 1835008 | tf_op jit(solution)/shard_map/all_to_all | solution.py:141
  239.2 2.9 copy-start.5
  296.5 9.6 %copy-start.12 = (bf16[1,4,8]{2,1,0:T(4,128)(2,1)S(1)}, bf16[1,4,8]{2,1,0:T(4,128)(2,1)}, u32[]{:S(2)}) copy-start(bf16[1,4,8]{2,1,0:T(4,128)(2,1)} %param.26) | copy-start | bytes 196
  297.8 36.5 %all-to-all-start.9 = ((bf16[256,2,896]{2,1,0:T(2,128)(2,1)}), bf16[256,2,896]{2,1,0:T(2,128)(2,1)S(1)}, u32[]{:S(2)}, u32[]{:S(2)}) async-start(bf16[256,2,896]{2,1,0:T(2,128)(2,1)} %reshape.245), calls=%async_computation.9 | async-start | bytes 1835008 | tf_op jit(solution)/shard_map/all_to_all | solution.py:190
Sparse Core Ops, SparseCore 0:
  33.4 111.1 all-gather.2

commit v15 on v14

--- a/solution.py
+++ b/solution.py
@@ -98,11 +98,15 @@
     down_cols = w_down[0].reshape(hidden_width, rep_count, chunk)
     down_cols = jnp.transpose(down_cols, (1, 0, 2))
     down_cols = lax.all_to_all(down_cols, "rep", 0, 0, tiled=True)
-    gate_rows = lax.all_to_all(w_gate[0].reshape(rep_count, chunk, hidden_width), "rep", 0, 0, tiled=True)
-    up_rows = lax.all_to_all(w_up[0].reshape(rep_count, chunk, hidden_width), "rep", 0, 0, tiled=True)
-    chip_keys, down_cols, gate_rows, up_rows = lax.optimization_barrier(
-        (chip_keys, down_cols, gate_rows, up_rows)
-    )
+    gate_up = jnp.concatenate(
+        [
+            w_gate[0].reshape(rep_count, chunk, hidden_width),
+            w_up[0].reshape(rep_count, chunk, hidden_width),
+        ],
+        axis=2,
+    )
+    gate_up = lax.all_to_all(gate_up, "rep", 0, 0, tiled=True)
+    chip_keys, down_cols, gate_up = lax.optimization_barrier((chip_keys, down_cols, gate_up))
     keys = chip_keys.reshape(-1, latent_width)
     device_of = lax.broadcasted_iota(jnp.int32, chip_keys.shape[:2], 0).reshape(-1)
     row_of = lax.broadcasted_iota(jnp.int32, chip_keys.shape[:2], 1).reshape(-1)
@@ -173,9 +177,8 @@
     spread = grouped.reshape(expert_count, capacity, rep_count, chunk)
     spread = jnp.transpose(spread, (2, 0, 1, 3)).reshape(rep_count * expert_count, capacity, chunk)
     columns = lax.all_to_all(spread, ("rep",) + EP, 0, 0, tiled=True).reshape(-1, chunk)
-    gate_part = jnp.einsum("nd,rdk->rnk", columns, gate_rows, preferred_element_type=jnp.float32)
-    up_part = jnp.einsum("nd,rdk->rnk", columns, up_rows, preferred_element_type=jnp.float32)
-    parts = jnp.concatenate([gate_part, up_part], axis=2).astype(jnp.bfloat16)
+    parts = jnp.einsum("nd,rdk->rnk", columns, gate_up, preferred_element_type=jnp.float32)
+    parts = parts.astype(jnp.bfloat16)
     parts = lax.all_to_all(parts, "rep", 0, 0, tiled=True)
     sums = jnp.sum(parts.astype(jnp.float32), axis=0)
     gate_sum, up_sum = sums[:, :hidden_width], sums[:, hidden_width:]

time: 344 us -> 346 us (level)
  other arithmetic: 8.76 us -> 12.3 us
    all_to_all x1, waiting for transfers between devices: 23.2 us -> 15.2 us  [local(): down_cols = lax.all_to_all(down_cols, 'rep', 0, 0, tiled=True)]
    all_gather x1, waiting for transfers between devices: 9.79 us -> 17.1 us  [local(): chip_keys = lax.all_gather(packed[None], EP, axis=0, tiled=True)]
    all_to_all x2 -> x1, starting transfers between devices: 11.3 us -> 6.83 us  [local(): gate_up = lax.all_to_all(gate_up, 'rep', 0, 0, tiled=True)]
    concatenate x1, other arithmetic: 0.14 us -> 3.7 us  [local(): jnp.concatenate([w_gate[0].reshape(rep_count, chunk, hidden_width), w_up[...]
    all_to_all x2 -> x1, waiting for transfers between devices: 48.8 us -> 47.7 us  [local(): gate_up = lax.all_to_all(gate_up, 'rep', 0, 0, tiled=True)]
  transfers between devices with their start and end apart: 7 -> 6, of which waited for: 7 -> 6; matrix products, arithmetic and copies ran while one was open for 5% -> 6% of each run, Pallas kernels for 0% -> 0%
where the time goes in v15:
time: 346 us; the launch traced here: 345 us
  waiting for transfers between devices  141 us (41%)
  blocking collectives  93.8 us (27%)
  starting transfers between devices  35.5 us (10%)
  matrix products  24.3 us (7%)
  local copies, waits for them, and re-layouts  23.2 us (7%)
  between operations  14.4 us (4%)
  other arithmetic  12.3 us (4%)
    all_to_all x1, waiting for transfers between devices, local(): gate_up = lax.all_to_all(gate_up, 'rep', 0, 0, tiled=True)  47.7 us
    all_to_all x1, blocking collectives, local(): lax.all_to_all(spread, ('rep',) + EP, 0, 0, tiled=True).reshape(-1, chunk)  40 us
    all_to_all x1, blocking collectives, local(): parts = lax.all_to_all(parts, 'rep', 0, 0, tiled=True)  31.3 us
    all_to_all x1, waiting for transfers between devices, local(): back = lax.all_to_all(out_cols, ('rep',) + EP, 0, 0, tiled=True)  27.8 us
    all_to_all x1, waiting for transfers between devices, local(): lax.all_to_all(partial, 'epo', 0, 0, tiled=True).astype(jnp.float32)  22.5 us
    all_to_all x1, blocking collectives, local(): units_all = lax.all_to_all(unit_copies, 'rep', 0, 0, tiled=True)  17.4 us
    all_gather x1, waiting for transfers between devices, local(): chip_keys = lax.all_gather(packed[None], EP, axis=0, tiled=True)  17.1 us
    all_to_all x1, waiting for transfers between devices, local(): down_cols = lax.all_to_all(down_cols, 'rep', 0, 0, tiled=True)  15.2 us
  transfers between devices with their start and end apart: 6, of which 6 were waited for; matrix products, arithmetic and copies ran while one was open for 6% of the time, Pallas kernels for 0%

profile of v15, /device:TPU:1, one launch (start us, length us, event | category | flops | bytes accessed | tf_op | source)
XLA Modules:
  0.0 345.1 jit_solution(4550672787340490507)
XLA Ops:
  6.6 0.8 constant_dynamic-slice_fusion
  7.6 0.1 copy.130
  7.7 0.2 fusion.39
  7.9 0.3 fusion
  8.2 0.5 broadcast.180
  8.7 1.1 reduce.7
  9.8 1.2 reshape.261
  11.0 7.5 %all-to-all-start = ((bf16[8,2,18432]{2,1,0:T(2,128)(2,1)}), bf16[8,2,18432]{2,1,0:T(2,128)(2,1)S(1)}, u32[]{:S(2)}, u32[]{:S(2)}) async-start(bf16[8,2,18432]{2,1,0:T(2,128)(2,1)} %reshape.261), calls=%async_computation | async-start | bytes 1179648 | tf_op jit(solution)/shard_map/all_to_all | solution.py:69
  18.6 0.8 dynamic_slice.13
  19.7 0.2 add_reduce_fusion
  19.8 11.1 %all-to-all-done = bf16[8,2,18432]{2,1,0:T(2,128)(2,1)S(1)} async-done(((bf16[8,2,18432]{2,1,0:T(2,128)(2,1)}), bf16[8,2,18432]{2,1,0:T(2,128)(2,1)S(1)}, u32[]{:S(2)}, u32[]{:S(2)}) %all-to-all-start) | async-done | bytes 589856 | tf_op jit(solution)/shard_map/all_to_all | solution.py:69
  30.9 0.6 reshape.262
  31.5 0.8 convolution_convert_fusion.1
  32.3 0.2 reshape.237
  32.5 0.8 maximum_maximum_fusion
  33.3 1.8 copy.140
  35.1 1.5 copy.150
  36.6 4.3 %all-to-all-start.1 = ((bf16[8,128,896]{2,1,0:T(8,128)(2,1)}), bf16[8,128,896]{2,1,0:T(8,128)(2,1)}, u32[]{:S(2)}, u32[]{:S(2)}) async-start(bf16[8,128,896]{2,1,0:T(8,128)(2,1)} %bitcast.91), calls=%async_computation.1 | async-start | bytes 3670016 | tf_op jit(solution)/shard_map/all_to_all | solution.py:100
  40.9 3.1 copy.115
  44.0 3.8 %copy.116 = bf16[8,896,128]{1,2,0:T(8,128)(2,1)} copy(bf16[8,896,128]{2,1,0:T(8,128)(2,1)} %bitcast.102) | data formatting | bytes 3670016 | tf_op jit(solution)/shard_map/reshape;squeeze | solution.py:104
  47.8 3.7 %pad_maximum_fusion = bf16[8,896,256]{1,2,0:T(8,128)(2,1)} fusion(bf16[8,896,128]{1,2,0:T(8,128)(2,1)} %copy.116, bf16[8,896,128]{1,2,0:T(8,128)(2,1)S(1)} %copy.115), kind=kLoop, calls=%fused_computation.17 | loop fusion | flops 7340032 | bytes 7340032 | tf_op jit(solution)/shard_map/concatenate | solution.py:101
  51.5 15.2 %all-to-all-done.1 = bf16[8,128,896]{2,1,0:T(8,128)(2,1)} async-done(((bf16[8,128,896]{2,1,0:T(8,128)(2,1)}), bf16[8,128,896]{2,1,0:T(8,128)(2,1)}, u32[]{:S(2)}, u32[]{:S(2)}) %all-to-all-start.1) | async-done | bytes 1835040 | tf_op jit(solution)/shard_map/all_to_all | solution.py:100
  66.7 6.8 %all-to-all-start.2 = ((bf16[8,896,256]{1,2,0:T(8,128)(2,1)}), bf16[8,896,256]{1,2,0:T(8,128)(2,1)}, u32[]{:S(2)}, u32[]{:S(2)}) async-start(bf16[8,896,256]{1,2,0:T(8,128)(2,1)} %pad_maximum_fusion), calls=%async_computation.2 | async-start | bytes 7340032 | tf_op jit(solution)/shard_map/all_to_all | solution.py:108
  74.3 0.1 and.66
  74.5 0.1 and.68
  74.6 0.2 copy.118
  74.8 3.9 %fusion.11 = pred[128,4608]{0,1:T(8,128)(4,1)S(1)} fusion(s32[4608]{0:T(1024)S(1)} %sub.25, pred[4608]{0:T(1024)(128)(4,1)S(1)} %and.68, pred[4608]{0:T(1024)(128)(4,1)S(1)} %and.66), kind=kLoop, calls=%fused_computation.22 | loop fusion | flops 1769472 | bytes 617472 | tf_op jit(solution)/shard_map/or | solution.py:117
  78.7 47.7 %all-to-all-done.2 = bf16[8,896,256]{1,2,0:T(8,128)(2,1)} async-done(((bf16[8,896,256]{1,2,0:T(8,128)(2,1)}), bf16[8,896,256]{1,2,0:T(8,128)(2,1)}, u32[]{:S(2)}, u32[]{:S(2)}) %all-to-all-start.2) | async-done | bytes 3670048 | tf_op jit(solution)/shard_map/all_to_all | solution.py:108
  126.3 17.1 %all-gather.3.cloned.1.call-done = bf16[4608,576]{1,0:T(8,128)(2,1)} async-done(((bf16[144,576]{1,0:T(8,128)(2,1)}), bf16[4608,576]{1,0:T(8,128)(2,1)}) %all-gather.3.cloned.1.call-update) | async-done | bytes 5308432 | tf_op jit(solution)/shard_map/all_gather | solution.py:95
  143.5 4.7 %fusion.55 = (f32[2,128]{1,0:T(2,128)S(1)}, f32[2,128,4608]{1,2,0:T(8,128)S(1)}) fusion(bf16[4608,576,1]{1,0,2:T(8,128)(2,1)} %bitcast.108, bf16[128,2,576]{0,2,1:T(8,128)(2,1)S(1)} %bitcast.103, pred[128,4608]{0,1:T(8,128)(4,1)S(1)} %fusion.11), kind=kOutput, calls=%fused_computation.89 | convolution fusion | flops 1362493184 | bytes 10912768 | tf_op jit(solution)/shard_map/thc,kc->htk/dot_general | solution.py:120
  148.2 2.1 copy-done.2
  150.4 0.6 fusion.5
  151.0 5.5 %fusion.15 = bf16[128,2,128]{2,0,1:T(8,128)(2,1)S(1)} fusion(bf16[2,512,128]{2,1,0:T(8,128)(2,1)S(1)} %copy-done.8, f32[2,128,4608]{1,2,0:T(8,128)} %copy-done.2, f32[2,128]{1,0:T(2,128)S(1)} %get-tuple-element.11, bf16[4608,576]{1,0:T(8,128)(2,1)} %all-gather.3.cloned.1.call-done, f32[128,2]{0,1:T(2,128)S(1)} %bitcast.107), kind=kOutput, calls=%fused_computation.28 | convolution fusion | flops 1244168192 | bytes 9766912 | tf_op jit(solution)/shard_map/thc,hcv->thv/dot_general | solution.py:134
  156.7 2.7 convolution_convert_fusion.2
  159.4 5.2 %all_to_all.45 = bf16[2,64,7168]{2,1,0:T(8,128)(2,1)S(1)} all-to-all(bf16[2,64,7168]{2,1,0:T(8,128)(2,1)S(1)} %convolution_convert_fusion.2), channel_id=1, replica_groups=mesh['rep'=8,'epo'=16,'core'=2] {'core'}, dimensions={0} | all-to-all | bytes 3670016 | tf_op jit(solution)/shard_map/all_to_all | solution.py:141
  164.6 0.8 reduce_sum.87
  165.4 1.5 convert_element_type.110
  167.0 8.6 %all-to-all-start.4 = ((bf16[16,16,1792]{2,1,0:T(8,128)(2,1)}), bf16[16,16,1792]{2,1,0:T(8,128)(2,1)S(1)}, u32[]{:S(2)}, u32[]{:S(2)}) async-start(bf16[16,16,1792]{2,1,0:T(8,128)(2,1)} %convert_element_type.110), calls=%async_computation.4 | async-start | bytes 1835008 | tf_op jit(solution)/shard_map/all_to_all | solution.py:145
  175.8 0.2 select_reduce_fusion
  176.0 0.3 convolution_convert_fusion.5
  176.3 22.5 %all-to-all-done.4 = bf16[16,16,1792]{2,1,0:T(8,128)(2,1)S(1)} async-done(((bf16[16,16,1792]{2,1,0:T(8,128)(2,1)}), bf16[16,16,1792]{2,1,0:T(8,128)(2,1)S(1)}, u32[]{:S(2)}, u32[]{:S(2)}) %all-to-all-start.4) | async-done | bytes 917536 | tf_op jit(solution)/shard_map/all_to_all | solution.py:145
  198.8 0.1 convert_reduce_fusion.2
  199.0 0.1 multiply_reduce_fusion
  199.2 0.1 reduce_sum.92
  199.4 0.5 convolution_convert_fusion.3
  199.8 0.1 copy.141
  200.0 0.2 copy.125
  200.2 0.9 copy.126
  201.1 40.0 %all_to_all.46 = bf16[256,2,896]{2,1,0:T(2,128)(2,1)S(1)} all-to-all(bf16[256,2,896]{2,1,0:T(2,128)(2,1)S(1)} %copy.126), channel_id=1, replica_groups=mesh['rep'=8,'epo'=16,'core'=2] {'rep','epo','core'}, dimensions={0} | all-to-all | bytes 1835008 | tf_op jit(solution)/shard_map/all_to_all | solution.py:179
  241.1 0.3 reshape.257
  241.4 4.4 %convert_bitcast_fusion = bf16[8,512,256]{1,2,0:T(8,128)(2,1)S(1)} fusion(bf16[8,896,256]{1,2,0:T(8,128)(2,1)} %all-to-all-done.2, bf16[512,896,1]{1,0,2:T(8,128)(2,1)S(1)} %reshape.257), kind=kOutput, calls=%fused_computation.23 | convolution fusion | flops 1880096768 | bytes 6684672 | tf_op jit(solution)/shard_map/nd,rdk->rnk/dot_general | solution.py:180
  245.8 31.3 %all_to_all.47 = bf16[8,512,256]{1,2,0:T(8,128)(2,1)S(1)} all-to-all(bf16[8,512,256]{1,2,0:T(8,128)(2,1)S(1)} %convert_bitcast_fusion), channel_id=1, replica_groups=mesh['rep'=8,'epo'=16,'core'=2] {'rep'}, dimensions={0} | all-to-all | bytes 4194304 | tf_op jit(solution)/shard_map/all_to_all | solution.py:182
  277.1 0.3 convert_reduce_fusion.1
  277.5 0.1 copy.127
  277.6 0.1 broadcast_in_dim.20
  277.8 17.4 %all_to_all.48 = bf16[8,512,128]{2,1,0:T(8,128)(2,1)S(1)} all-to-all(bf16[8,512,128]{2,1,0:T(8,128)(2,1)S(1)} %broadcast_in_dim.20), channel_id=1, replica_groups=mesh['rep'=8,'epo'=16,'core'=2] {'rep'}, dimensions={0} | all-to-all | bytes 2097152 | tf_op jit(solution)/shard_map/all_to_all | solution.py:188
  295.1 3.6 %convert_reduce_fusion = bf16[512,896]{1,0:T(8,128)(2,1)S(1)} fusion(bf16[8,512,128]{2,1,0:T(8,128)(2,1)S(1)} %all_to_all.48, bf16[8,128,896]{2,1,0:T(8,128)(2,1)} %all-to-all-done.1), kind=kOutput, calls=%fused_computation.7 | convolution fusion | flops 946405376 | bytes 3801088 | tf_op jit(solution)/shard_map/rnk,rkc->rnc/dot_general | solution.py:189
  298.8 1.3 reshape.245
  300.1 8.3 %all-to-all-start.8 = ((bf16[256,2,896]{2,1,0:T(2,128)(2,1)}), bf16[256,2,896]{2,1,0:T(2,128)(2,1)S(1)}, u32[]{:S(2)}, u32[]{:S(2)}) async-start(bf16[256,2,896]{2,1,0:T(2,128)(2,1)} %reshape.245), calls=%async_computation.8 | async-start | bytes 1835008 | tf_op jit(solution)/shard_map/all_to_all | solution.py:193
  308.5 0.3 fusion.36
  308.7 27.8 %all-to-all-done.8 = bf16[256,2,896]{2,1,0:T(2,128)(2,1)S(1)} async-done(((bf16[256,2,896]{2,1,0:T(2,128)(2,1)}), bf16[256,2,896]{2,1,0:T(2,128)(2,1)S(1)}, u32[]{:S(2)}, u32[]{:S(2)}) %all-to-all-start.8) | async-done | bytes 917536 | tf_op jit(solution)/shard_map/all_to_all | solution.py:193
  336.6 0.3 copy.129
  336.9 0.1 copy.142
  337.1 1.1 fusion.1
  (49 shorter events, 1.5 us)
Async XLA Ops:
  6.5 1.4 copy-start
  6.5 12.9 %copy-start.6 = (bf16[1,2304]{1,0:T(2,128)(2,1)S(1)}, bf16[1,2304]{1,0:T(2,128)(2,1)}, u32[]{:S(2)}) copy-start(bf16[1,2304]{1,0:T(2,128)(2,1)} %param.16) | copy-start | bytes 13828
  11.0 19.9 %all-to-all-start = ((bf16[8,2,18432]{2,1,0:T(2,128)(2,1)}), bf16[8,2,18432]{2,1,0:T(2,128)(2,1)S(1)}, u32[]{:S(2)}, u32[]{:S(2)}) async-start(bf16[8,2,18432]{2,1,0:T(2,128)(2,1)} %reshape.261), calls=%async_computation | async-start | bytes 1179648 | tf_op jit(solution)/shard_map/all_to_all | solution.py:69
  18.5 125.0 %all-gather.3.cloned.1.call-start = ((), (), s32[]{:S(2)}) async-start(), calls=%async_computation.9 | async-start | bytes 6082560 | tf_op jit(solution)/shard_map/all_gather | solution.py:95
  36.6 30.1 %all-to-all-start.1 = ((bf16[8,128,896]{2,1,0:T(8,128)(2,1)}), bf16[8,128,896]{2,1,0:T(8,128)(2,1)}, u32[]{:S(2)}, u32[]{:S(2)}) async-start(bf16[8,128,896]{2,1,0:T(8,128)(2,1)} %bitcast.91), calls=%async_computation.1 | async-start | bytes 3670016 | tf_op jit(solution)/shard_map/all_to_all | solution.py:100
  51.5 23.1 %copy-start.4 = (bf16[1,128,1152]{2,1,0:T(8,128)(2,1)S(1)}, bf16[1,128,1152]{2,1,0:T(8,128)(2,1)}, u32[]{:S(2)}) copy-start(bf16[1,128,1152]{2,1,0:T(8,128)(2,1)} %param.15) | copy-start | bytes 884740
  66.7 59.6 %all-to-all-start.2 = ((bf16[8,896,256]{1,2,0:T(8,128)(2,1)}), bf16[8,896,256]{1,2,0:T(8,128)(2,1)}, u32[]{:S(2)}, u32[]{:S(2)}) async-start(bf16[8,896,256]{1,2,0:T(8,128)(2,1)} %pad_maximum_fusion), calls=%async_computation.2 | async-start | bytes 7340032 | tf_op jit(solution)/shard_map/all_to_all | solution.py:108
  148.2 2.2 copy-start.2
  148.2 2.8 copy-start.8
  164.6 11.0 %copy-start.3 = (bf16[1,4,7168]{2,1,0:T(4,128)(2,1)S(1)}, bf16[1,4,7168]{2,1,0:T(4,128)(2,1)}, u32[]{:S(2)}) copy-start(bf16[1,4,7168]{2,1,0:T(4,128)(2,1)} %param.21) | copy-start | bytes 172036
  164.6 11.0 %copy-start.7 = (s32[1,4,8]{2,1,0:T(4,128)S(1)}, s32[1,4,8]{2,1,0:T(4,128)}, u32[]{:S(2)}) copy-start(s32[1,4,8]{2,1,0:T(4,128)} %param.25) | copy-start | bytes 388
  164.6 11.2 %copy-start.5 = (bf16[7168]{0:T(1024)(128)(2,1)S(1)}, bf16[7168]{0:T(1024)(128)(2,1)}, u32[]{:S(2)}) copy-start(bf16[7168]{0:T(1024)(128)(2,1)} %param.24) | copy-start | bytes 43012
  167.0 31.8 %all-to-all-start.4 = ((bf16[16,16,1792]{2,1,0:T(8,128)(2,1)}), bf16[16,16,1792]{2,1,0:T(8,128)(2,1)S(1)}, u32[]{:S(2)}, u32[]{:S(2)}) async-start(bf16[16,16,1792]{2,1,0:T(8,128)(2,1)} %convert_element_type.110), calls=%async_computation.4 | async-start | bytes 1835008 | tf_op jit(solution)/shard_map/all_to_all | solution.py:145
  295.1 13.2 %copy-start.9 = (bf16[1,4,8]{2,1,0:T(4,128)(2,1)S(1)}, bf16[1,4,8]{2,1,0:T(4,128)(2,1)}, u32[]{:S(2)}) copy-start(bf16[1,4,8]{2,1,0:T(4,128)(2,1)} %param.26) | copy-start | bytes 196
  300.1 36.5 %all-to-all-start.8 = ((bf16[256,2,896]{2,1,0:T(2,128)(2,1)}), bf16[256,2,896]{2,1,0:T(2,128)(2,1)S(1)}, u32[]{:S(2)}, u32[]{:S(2)}) async-start(bf16[256,2,896]{2,1,0:T(2,128)(2,1)} %reshape.245), calls=%async_computation.8 | async-start | bytes 1835008 | tf_op jit(solution)/shard_map/all_to_all | solution.py:193
  308.4 29.8 %copy-start.1 = (bf16[1,8,36864]{2,1,0:T(8,128)(2,1)S(1)}, bf16[1,8,36864]{2,1,0:T(8,128)(2,1)}, u32[]{:S(2)}) copy-start(bf16[1,8,36864]{2,1,0:T(8,128)(2,1)} %param.17) | copy-start | bytes 1769476
Sparse Core Ops, SparseCore 0:
  33.4 110.0 all-gather.2

commit v16 on v14

--- a/solution.py
+++ b/solution.py
@@ -66,6 +66,12 @@
         preferred_element_type=jnp.float32,
     )
     outgoing = outgoing.astype(jnp.bfloat16).reshape(rep_count, per_holder, block_width)
+    hidden_width, width = w_down.shape[1], w_down.shape[2]
+    chunk = width // rep_count
+    down_cols = w_down[0].reshape(hidden_width, rep_count, chunk)
+    down_cols = jnp.transpose(down_cols, (1, 0, 2))
+    down_cols = lax.all_to_all(down_cols, "rep", 0, 0, tiled=True)
+    outgoing, down_cols = lax.optimization_barrier((outgoing, down_cols))
     incoming = lax.all_to_all(outgoing, "rep", split_axis=0, concat_axis=0, tiled=True)
     own_holders = lax.dynamic_index_in_dim(mine_holders, rep_index, 0, keepdims=False)
     own_order = lax.dynamic_index_in_dim(occurrence, rep_index, 0, keepdims=False)
@@ -93,16 +99,9 @@
     )
     row_count = packed.shape[0]
     chip_keys = lax.all_gather(packed[None], EP, axis=0, tiled=True)
-    hidden_width, width = w_down.shape[1], w_down.shape[2]
-    chunk = width // rep_count
-    down_cols = w_down[0].reshape(hidden_width, rep_count, chunk)
-    down_cols = jnp.transpose(down_cols, (1, 0, 2))
-    down_cols = lax.all_to_all(down_cols, "rep", 0, 0, tiled=True)
     gate_rows = lax.all_to_all(w_gate[0].reshape(rep_count, chunk, hidden_width), "rep", 0, 0, tiled=True)
     up_rows = lax.all_to_all(w_up[0].reshape(rep_count, chunk, hidden_width), "rep", 0, 0, tiled=True)
-    chip_keys, down_cols, gate_rows, up_rows = lax.optimization_barrier(
-        (chip_keys, down_cols, gate_rows, up_rows)
-    )
+    chip_keys, gate_rows, up_rows = lax.optimization_barrier((chip_keys, gate_rows, up_rows))
     keys = chip_keys.reshape(-1, latent_width)
     device_of = lax.broadcasted_iota(jnp.int32, chip_keys.shape[:2], 0).reshape(-1)
     row_of = lax.broadcasted_iota(jnp.int32, chip_keys.shape[:2], 1).reshape(-1)

time: 344 us -> 361 us (1.049)
  waiting for transfers between devices: 143 us -> 163 us
    all_gather x1, waiting for transfers between devices: 9.79 us -> 30 us  [local(): chip_keys = lax.all_gather(packed[None], EP, axis=0, tiled=True)]
    all_to_all x1, starting transfers between devices: 7.48 us -> 3.54 us  [local(): lax.all_to_all(outgoing, 'rep', split_axis=0, concat_axis=0, tiled=True)]
  transfers between devices with their start and end apart: 7 -> 7, of which waited for: 7 -> 7; matrix products, arithmetic and copies ran while one was open for 5% -> 4% of each run, Pallas kernels for 0% -> 0%
where the time goes in v16:
time: 361 us; the launch traced here: 360 us
  waiting for transfers between devices  163 us (45%)
  blocking collectives  93.3 us (26%)
  starting transfers between devices  35.6 us (10%)
  matrix products  22.5 us (6%)
  local copies, waits for them, and re-layouts  22 us (6%)
  between operations  14.5 us (4%)
  other arithmetic  8.76 us (2%)
    all_to_all x1, blocking collectives, local(): lax.all_to_all(spread, ('rep',) + EP, 0, 0, tiled=True).reshape(-1, chunk)  39.5 us
    all_to_all x1, blocking collectives, local(): parts = lax.all_to_all(parts, 'rep', 0, 0, tiled=True)  31.3 us
    all_gather x1, waiting for transfers between devices, local(): chip_keys = lax.all_gather(packed[None], EP, axis=0, tiled=True)  30 us
    all_to_all x1, waiting for transfers between devices, local(): back = lax.all_to_all(out_cols, ('rep',) + EP, 0, 0, tiled=True)  27.8 us
    all_to_all x1, waiting for transfers between devices, local(): down_cols = lax.all_to_all(down_cols, 'rep', 0, 0, tiled=True)  24.8 us
    all_to_all x1, waiting for transfers between devices, local(): lax.all_to_all(w_up[0].reshape(rep_count, chunk, hidden_width), 'rep', 0,...  23.3 us
    all_to_all x1, waiting for transfers between devices, local(): lax.all_to_all(w_gate[0].reshape(rep_count, chunk, hidden_width), 'rep',...  23.1 us
    all_to_all x1, waiting for transfers between devices, local(): lax.all_to_all(partial, 'epo', 0, 0, tiled=True).astype(jnp.float32)  22.5 us
  transfers between devices with their start and end apart: 7, of which 7 were waited for; matrix products, arithmetic and copies ran while one was open for 4% of the time, Pallas kernels for 0%

profile of v16, /device:TPU:1, one launch (start us, length us, event | category | flops | bytes accessed | tf_op | source)
XLA Modules:
  0.0 360.1 jit_solution(7537036922747173821)
XLA Ops:
  6.5 1.9 copy.140
  8.4 1.5 copy.150
  10.0 7.6 %all-to-all-start = ((bf16[8,128,896]{2,1,0:T(8,128)(2,1)}), bf16[8,128,896]{2,1,0:T(8,128)(2,1)S(1)}, u32[]{:S(2)}, u32[]{:S(2)}) async-start(bf16[8,128,896]{2,1,0:T(8,128)(2,1)} %bitcast.95), calls=%async_computation | async-start | bytes 3670016 | tf_op jit(solution)/shard_map/all_to_all | solution.py:73
  17.9 0.1 copy.130
  18.0 0.2 fusion.41
  18.2 0.3 fusion
  18.5 24.8 %all-to-all-done = bf16[8,128,896]{2,1,0:T(8,128)(2,1)S(1)} async-done(((bf16[8,128,896]{2,1,0:T(8,128)(2,1)}), bf16[8,128,896]{2,1,0:T(8,128)(2,1)S(1)}, u32[]{:S(2)}, u32[]{:S(2)}) %all-to-all-start) | async-done | bytes 1835040 | tf_op jit(solution)/shard_map/all_to_all | solution.py:73
  43.3 1.2 copy-done.3
  44.6 0.5 broadcast.180
  45.1 1.1 reduce.7
  46.1 1.2 reshape.261
  47.4 3.5 all-to-all-start.1
  51.4 0.2 add_reduce_fusion
  51.6 11.7 %all-to-all-done.1 = bf16[8,2,18432]{2,1,0:T(2,128)(2,1)S(1)} async-done(((bf16[8,2,18432]{2,1,0:T(2,128)(2,1)}), bf16[8,2,18432]{2,1,0:T(2,128)(2,1)S(1)}, u32[]{:S(2)}, u32[]{:S(2)}) %all-to-all-start.1) | async-done | bytes 589856 | tf_op jit(solution)/shard_map/all_to_all | solution.py:75
  63.3 0.6 reshape.262
  63.9 0.8 convolution_convert_fusion.1
  64.6 0.2 reshape.237
  64.8 0.8 maximum_maximum_fusion
  65.6 3.8 %copy.115 = bf16[8,896,128]{1,2,0:T(8,128)(2,1)} copy(bf16[8,896,128]{2,1,0:T(8,128)(2,1)} %bitcast.105) | data formatting | bytes 3670016 | tf_op jit(solution)/shard_map/reshape;squeeze | solution.py:102
  69.4 4.4 %all-to-all-start.2 = ((bf16[8,896,128]{1,2,0:T(8,128)(2,1)}), bf16[8,896,128]{1,2,0:T(8,128)(2,1)}, u32[]{:S(2)}, u32[]{:S(2)}) async-start(bf16[8,896,128]{1,2,0:T(8,128)(2,1)} %copy.115), calls=%async_computation.2 | async-start | bytes 3670016 | tf_op jit(solution)/shard_map/all_to_all | solution.py:102
  73.9 2.7 copy.116
  76.6 23.1 %all-to-all-done.2 = bf16[8,896,128]{1,2,0:T(8,128)(2,1)} async-done(((bf16[8,896,128]{1,2,0:T(8,128)(2,1)}), bf16[8,896,128]{1,2,0:T(8,128)(2,1)}, u32[]{:S(2)}, u32[]{:S(2)}) %all-to-all-start.2) | async-done | bytes 1835040 | tf_op jit(solution)/shard_map/all_to_all | solution.py:102
  99.7 6.8 %all-to-all-start.3 = ((bf16[8,896,128]{1,2,0:T(8,128)(2,1)}), bf16[8,896,128]{1,2,0:T(8,128)(2,1)S(1)}, u32[]{:S(2)}, u32[]{:S(2)}) async-start(bf16[8,896,128]{1,2,0:T(8,128)(2,1)} %copy.116), calls=%async_computation.3 | async-start | bytes 3670016 | tf_op jit(solution)/shard_map/all_to_all | solution.py:103
  107.5 0.2 copy.118
  107.7 3.9 %fusion.11 = pred[128,4608]{0,1:T(8,128)(4,1)S(1)} fusion(s32[4608]{0:T(1024)S(1)} %sub.25, pred[4608]{0:T(1024)(128)(4,1)S(1)} %and.68, pred[4608]{0:T(1024)(128)(4,1)S(1)} %and.66), kind=kLoop, calls=%fused_computation.21 | loop fusion | flops 1769472 | bytes 617472 | tf_op jit(solution)/shard_map/or | solution.py:112
  111.6 23.3 %all-to-all-done.3 = bf16[8,896,128]{1,2,0:T(8,128)(2,1)S(1)} async-done(((bf16[8,896,128]{1,2,0:T(8,128)(2,1)}), bf16[8,896,128]{1,2,0:T(8,128)(2,1)S(1)}, u32[]{:S(2)}, u32[]{:S(2)}) %all-to-all-start.3) | async-done | bytes 1835040 | tf_op jit(solution)/shard_map/all_to_all | solution.py:103
  134.9 30.0 %all-gather.3.cloned.1.call-done = bf16[4608,576]{1,0:T(8,128)(2,1)} async-done(((bf16[144,576]{1,0:T(8,128)(2,1)}), bf16[4608,576]{1,0:T(8,128)(2,1)}) %all-gather.3.cloned.1.call-update) | async-done | bytes 5308432 | tf_op jit(solution)/shard_map/all_gather | solution.py:101
  164.9 4.7 %fusion.57 = (f32[2,128]{1,0:T(2,128)S(1)}, f32[2,128,4608]{1,2,0:T(8,128)S(1)}) fusion(bf16[4608,576,1]{1,0,2:T(8,128)(2,1)} %bitcast.112, bf16[128,2,576]{0,2,1:T(8,128)(2,1)S(1)} %bitcast.107, pred[128,4608]{0,1:T(8,128)(4,1)S(1)} %fusion.11), kind=kOutput, calls=%fused_computation.92 | convolution fusion | flops 1362493184 | bytes 10912768 | tf_op jit(solution)/shard_map/thc,kc->htk/dot_general | solution.py:115
  169.7 0.6 fusion.5
  170.3 1.5 copy-done.1
  171.9 5.5 %fusion.17 = bf16[128,2,128]{2,0,1:T(8,128)(2,1)S(1)} fusion(bf16[2,512,128]{2,1,0:T(8,128)(2,1)S(1)} %copy-done.14, f32[2,128,4608]{1,2,0:T(8,128)} %copy-done.1, f32[2,128]{1,0:T(2,128)S(1)} %get-tuple-element.15, bf16[4608,576]{1,0:T(8,128)(2,1)} %all-gather.3.cloned.1.call-done, f32[128,2]{0,1:T(2,128)S(1)} %bitcast.111), kind=kOutput, calls=%fused_computation.31 | convolution fusion | flops 1244168192 | bytes 9766912 | tf_op jit(solution)/shard_map/thc,hcv->thv/dot_general | solution.py:129
  177.5 2.7 convolution_convert_fusion.2
  180.2 5.1 %all_to_all.50 = bf16[2,64,7168]{2,1,0:T(8,128)(2,1)S(1)} all-to-all(bf16[2,64,7168]{2,1,0:T(8,128)(2,1)S(1)} %convolution_convert_fusion.2), channel_id=1, replica_groups=mesh['rep'=8,'epo'=16,'core'=2] {'core'}, dimensions={0} | all-to-all | bytes 3670016 | tf_op jit(solution)/shard_map/all_to_all | solution.py:136
  185.4 0.8 reduce_sum.87
  186.2 1.5 convert_element_type.105
  187.8 4.9 %all-to-all-start.5 = ((bf16[16,16,1792]{2,1,0:T(8,128)(2,1)}), bf16[16,16,1792]{2,1,0:T(8,128)(2,1)S(1)}, u32[]{:S(2)}, u32[]{:S(2)}) async-start(bf16[16,16,1792]{2,1,0:T(8,128)(2,1)} %convert_element_type.105), calls=%async_computation.5 | async-start | bytes 1835008 | tf_op jit(solution)/shard_map/all_to_all | solution.py:140
  192.9 0.2 select_reduce_fusion
  193.1 0.3 convolution_convert_fusion.7
  193.4 22.5 %all-to-all-done.5 = bf16[16,16,1792]{2,1,0:T(8,128)(2,1)S(1)} async-done(((bf16[16,16,1792]{2,1,0:T(8,128)(2,1)}), bf16[16,16,1792]{2,1,0:T(8,128)(2,1)S(1)}, u32[]{:S(2)}, u32[]{:S(2)}) %all-to-all-start.5) | async-done | bytes 917536 | tf_op jit(solution)/shard_map/all_to_all | solution.py:140
  215.8 0.1 convert_reduce_fusion.2
  216.0 0.1 multiply_reduce_fusion
  216.2 0.1 reduce_sum.92
  216.4 0.5 convolution_convert_fusion.3
  216.9 0.1 copy.141
  217.0 0.2 copy.125
  217.2 0.9 copy.126
  218.1 39.5 %all_to_all.51 = bf16[256,2,896]{2,1,0:T(2,128)(2,1)S(1)} all-to-all(bf16[256,2,896]{2,1,0:T(2,128)(2,1)S(1)} %copy.126), channel_id=1, replica_groups=mesh['rep'=8,'epo'=16,'core'=2] {'rep','epo','core'}, dimensions={0} | all-to-all | bytes 1835008 | tf_op jit(solution)/shard_map/all_to_all | solution.py:174
  257.6 0.3 reshape.257
  258.0 2.9 fusion.12
  260.9 1.3 fusion.13
  262.2 0.1 pad_maximum_fusion
  262.3 31.3 %all_to_all.52 = bf16[8,512,256]{1,2,0:T(8,128)(2,1)S(1)} all-to-all(bf16[8,512,256]{1,2,0:T(8,128)(2,1)S(1)} %pad_maximum_fusion), channel_id=1, replica_groups=mesh['rep'=8,'epo'=16,'core'=2] {'rep'}, dimensions={0} | all-to-all | bytes 4194304 | tf_op jit(solution)/shard_map/all_to_all | solution.py:178
  293.6 0.3 convert_reduce_fusion.1
  294.0 0.1 copy.127
  294.1 0.1 broadcast_in_dim.20
  294.3 17.5 %all_to_all.53 = bf16[8,512,128]{2,1,0:T(8,128)(2,1)S(1)} all-to-all(bf16[8,512,128]{2,1,0:T(8,128)(2,1)S(1)} %broadcast_in_dim.20), channel_id=1, replica_groups=mesh['rep'=8,'epo'=16,'core'=2] {'rep'}, dimensions={0} | all-to-all | bytes 2097152 | tf_op jit(solution)/shard_map/all_to_all | solution.py:184
  311.8 2.1 convert_reduce_fusion
  313.8 1.3 reshape.245
  315.1 8.3 %all-to-all-start.9 = ((bf16[256,2,896]{2,1,0:T(2,128)(2,1)}), bf16[256,2,896]{2,1,0:T(2,128)(2,1)S(1)}, u32[]{:S(2)}, u32[]{:S(2)}) async-start(bf16[256,2,896]{2,1,0:T(2,128)(2,1)} %reshape.245), calls=%async_computation.9 | async-start | bytes 1835008 | tf_op jit(solution)/shard_map/all_to_all | solution.py:189
  323.5 0.3 fusion.38
  323.8 27.8 %all-to-all-done.9 = bf16[256,2,896]{2,1,0:T(2,128)(2,1)S(1)} async-done(((bf16[256,2,896]{2,1,0:T(2,128)(2,1)}), bf16[256,2,896]{2,1,0:T(2,128)(2,1)S(1)}, u32[]{:S(2)}, u32[]{:S(2)}) %all-to-all-start.9) | async-done | bytes 917536 | tf_op jit(solution)/shard_map/all_to_all | solution.py:189
  351.7 0.3 copy.129
  352.0 0.1 copy.142
  352.1 1.1 fusion.1
  (64 shorter events, 1.9 us)
Async XLA Ops:
  6.5 11.6 %copy-start = (bf16[1,8,36864]{2,1,0:T(8,128)(2,1)S(1)}, bf16[1,8,36864]{2,1,0:T(8,128)(2,1)}, u32[]{:S(2)}) copy-start(bf16[1,8,36864]{2,1,0:T(8,128)(2,1)} %param.17) | copy-start | bytes 1769476
  10.0 7.6 %copy-start.11 = (s32[8,64]{1,0:T(8,128)S(1)}, s32[8,64]{1,0:T(8,128)}, u32[]{:S(2)}) copy-start(s32[8,64]{1,0:T(8,128)} %param.18) | copy-start | bytes 6148
  10.0 7.6 %copy-start.12 = (s32[8,64]{1,0:T(8,128)S(1)}, s32[8,64]{1,0:T(8,128)}, u32[]{:S(2)}) copy-start(s32[8,64]{1,0:T(8,128)} %param.19) | copy-start | bytes 6148
  10.0 33.4 %all-to-all-start = ((bf16[8,128,896]{2,1,0:T(8,128)(2,1)}), bf16[8,128,896]{2,1,0:T(8,128)(2,1)S(1)}, u32[]{:S(2)}, u32[]{:S(2)}) async-start(bf16[8,128,896]{2,1,0:T(8,128)(2,1)} %bitcast.95), calls=%async_computation | async-start | bytes 3670016 | tf_op jit(solution)/shard_map/all_to_all | solution.py:73
  18.2 33.0 %copy-start.10 = (bf16[1,2304]{1,0:T(2,128)(2,1)S(1)}, bf16[1,2304]{1,0:T(2,128)(2,1)}, u32[]{:S(2)}) copy-start(bf16[1,2304]{1,0:T(2,128)(2,1)} %param.16) | copy-start | bytes 13828
  43.3 1.2 copy-start.3
  47.4 15.9 %all-to-all-start.1 = ((bf16[8,2,18432]{2,1,0:T(2,128)(2,1)}), bf16[8,2,18432]{2,1,0:T(2,128)(2,1)S(1)}, u32[]{:S(2)}, u32[]{:S(2)}) async-start(bf16[8,2,18432]{2,1,0:T(2,128)(2,1)} %reshape.261), calls=%async_computation.1 | async-start | bytes 1179648 | tf_op jit(solution)/shard_map/all_to_all | solution.py:75
  50.9 114.0 %all-gather.3.cloned.1.call-start = ((), (), s32[]{:S(2)}) async-start(), calls=%async_computation.10 | async-start | bytes 6082560 | tf_op jit(solution)/shard_map/all_gather | solution.py:101
  69.4 4.5 %copy-start.2 = (bf16[1,7168,128]{2,1,0:T(8,128)(2,1)S(1)}, bf16[1,7168,128]{2,1,0:T(8,128)(2,1)}, u32[]{:S(2)}) copy-start(bf16[1,7168,128]{2,1,0:T(8,128)(2,1)} %param.28) | copy-start | bytes 5505028
  69.4 30.3 %all-to-all-start.2 = ((bf16[8,896,128]{1,2,0:T(8,128)(2,1)}), bf16[8,896,128]{1,2,0:T(8,128)(2,1)}, u32[]{:S(2)}, u32[]{:S(2)}) async-start(bf16[8,896,128]{1,2,0:T(8,128)(2,1)} %copy.115), calls=%async_computation.2 | async-start | bytes 3670016 | tf_op jit(solution)/shard_map/all_to_all | solution.py:102
  76.5 30.9 %copy-start.8 = (bf16[1,128,1152]{2,1,0:T(8,128)(2,1)S(1)}, bf16[1,128,1152]{2,1,0:T(8,128)(2,1)}, u32[]{:S(2)}) copy-start(bf16[1,128,1152]{2,1,0:T(8,128)(2,1)} %param.15) | copy-start | bytes 884740
  99.7 35.2 %all-to-all-start.3 = ((bf16[8,896,128]{1,2,0:T(8,128)(2,1)}), bf16[8,896,128]{1,2,0:T(8,128)(2,1)S(1)}, u32[]{:S(2)}, u32[]{:S(2)}) async-start(bf16[8,896,128]{1,2,0:T(8,128)(2,1)} %copy.116), calls=%async_computation.3 | async-start | bytes 3670016 | tf_op jit(solution)/shard_map/all_to_all | solution.py:103
  134.9 34.8 %copy-start.5 = (bf16[8,896,128]{1,2,0:T(8,128)(2,1)}, bf16[8,896,128]{1,2,0:T(8,128)(2,1)S(1)}, u32[]{:S(2)}) copy-start(bf16[8,896,128]{1,2,0:T(8,128)(2,1)S(1)} %all-to-all-done.3) | copy-start | bytes 5505028
  169.7 2.2 copy-start.1
  169.7 2.2 copy-start.14
  186.2 6.5 %copy-start.7 = (bf16[1,4,7168]{2,1,0:T(4,128)(2,1)S(1)}, bf16[1,4,7168]{2,1,0:T(4,128)(2,1)}, u32[]{:S(2)}) copy-start(bf16[1,4,7168]{2,1,0:T(4,128)(2,1)} %param.21) | copy-start | bytes 172036
  186.2 6.5 %copy-start.13 = (s32[1,4,8]{2,1,0:T(4,128)S(1)}, s32[1,4,8]{2,1,0:T(4,128)}, u32[]{:S(2)}) copy-start(s32[1,4,8]{2,1,0:T(4,128)} %param.25) | copy-start | bytes 388
  186.2 6.7 %copy-start.9 = (bf16[7168]{0:T(1024)(128)(2,1)S(1)}, bf16[7168]{0:T(1024)(128)(2,1)}, u32[]{:S(2)}) copy-start(bf16[7168]{0:T(1024)(128)(2,1)} %param.24) | copy-start | bytes 43012
  187.8 28.1 %all-to-all-start.5 = ((bf16[16,16,1792]{2,1,0:T(8,128)(2,1)}), bf16[16,16,1792]{2,1,0:T(8,128)(2,1)S(1)}, u32[]{:S(2)}, u32[]{:S(2)}) async-start(bf16[16,16,1792]{2,1,0:T(8,128)(2,1)} %convert_element_type.105), calls=%async_computation.5 | async-start | bytes 1835008 | tf_op jit(solution)/shard_map/all_to_all | solution.py:140
  258.0 2.9 copy-start.6
  293.9 17.9 %copy-start.4 = (bf16[8,128,896]{2,1,0:T(8,128)(2,1)S(1)}, bf16[8,128,896]{2,1,0:T(8,128)(2,1)}, u32[]{:S(2)}) copy-start(bf16[8,128,896]{2,1,0:T(8,128)(2,1)} %copy-done.3) | copy-start | bytes 5505028
  313.8 9.6 %copy-start.15 = (bf16[1,4,8]{2,1,0:T(4,128)(2,1)S(1)}, bf16[1,4,8]{2,1,0:T(4,128)(2,1)}, u32[]{:S(2)}) copy-start(bf16[1,4,8]{2,1,0:T(4,128)(2,1)} %param.26) | copy-start | bytes 196
  315.1 36.5 %all-to-all-start.9 = ((bf16[256,2,896]{2,1,0:T(2,128)(2,1)}), bf16[256,2,896]{2,1,0:T(2,128)(2,1)S(1)}, u32[]{:S(2)}, u32[]{:S(2)}) async-start(bf16[256,2,896]{2,1,0:T(2,128)(2,1)} %reshape.245), calls=%async_computation.9 | async-start | bytes 1835008 | tf_op jit(solution)/shard_map/all_to_all | solution.py:189
Sparse Core Ops, SparseCore 0:
  65.7 99.1 all-gather.2
